TPU v7x, 256 devices: a whole 4x4x8 slice. The times are simulated.
256 devices in a mesh: lat: 16 (over z, core), elev: 16 (over y, x).
Axes of the slice: x: 4, y: 4, z: 8, core: 2. Of those that a mesh axis runs over, the one named last changes fastest.
Arguments:
- volume: bfloat16 [128, 128, 128, 256], P('lat', 'elev'), may hold values from -64 to 64
- lat_taps: float32 [7], replicated, may hold values from 0.05 to 0.3
- elev_taps: float32 [7], replicated, may hold values from 0.05 to 0.3
- time_taps: bfloat16 [32], replicated, may hold values from -3 to 3
- clutter_rank: int32 [], replicated, may hold values from 4 to 32
- noise_rank: int32 [], replicated, may hold values from 128 to 256
Outputs:
- cleaned: bfloat16 [128, 128, 128, 256], P('lat', 'elev')
- power: float32 [128, 128, 128], P('lat', 'elev')
- band_weights: float32 [256, 256], replicated
All inputs are finite; a program needn't handle non-finite values.
Results may differ from a plain program's by a relative error of at most 0.0034.
The roundings to bfloat16 on the way count: a program that leaves them out, or rounds other values in their place, can miss the bound.
Values may be sent and summed in bfloat16 or wider, within the bound.
No kernel may reach another device: no remote copies, remote signals or barrier semaphores. Data moves between devices by JAX's collectives and lax.ppermute only.
A program may use at most 64 MiB of HBM per device.

v0:
```python
import jax
import jax.numpy as jnp
from jax import lax
from jax.sharding import PartitionSpec as P


def padded(block, sides, width):
    for axis, dim in sides:
        count = lax.axis_size(axis)
        forward = [(i, i + 1) for i in range(count - 1)]
        backward = [(target, source) for source, target in forward]
        low = lax.ppermute(
            lax.slice_in_dim(block, block.shape[dim] - width, None, axis=dim), axis, forward
        )
        high = lax.ppermute(lax.slice_in_dim(block, 0, width, axis=dim), axis, backward)
        block = jnp.concatenate([low, block, high], axis=dim)
    return block


def time_matrix(time_taps, frames):
    count_taps = time_taps.shape[0]
    source = jnp.arange(frames, dtype=jnp.int32)[:, None]
    target = jnp.arange(frames, dtype=jnp.int32)[None, :]
    lagged = target - source
    matched = lagged[:, :, None] == jnp.arange(count_taps, dtype=jnp.int32)[None, None, :]
    single = jnp.sum(
        jnp.where(matched, time_taps.astype(jnp.float32)[None, None, :], jnp.float32(0.0)), axis=2
    )
    paired = jnp.kron(jnp.eye(2, dtype=jnp.float32), single)
    return paired.astype(jnp.bfloat16)


def smooth(extended, lat_taps, elev_taps, lat_count, elev_count):
    lat_sum = lat_taps[0] * extended[0:lat_count].astype(jnp.float32)
    for index_tap in range(1, 7):
        lat_sum = lat_sum + lat_taps[index_tap] * extended[
            index_tap : index_tap + lat_count
        ].astype(jnp.float32)
    result = elev_taps[0] * lat_sum[:, 0:elev_count]
    for index_tap in range(1, 7):
        result = result + elev_taps[index_tap] * lat_sum[:, index_tap : index_tap + elev_count]
    return result


def filtered_rows(extended, lat_taps, elev_taps, matrix, lat_count, elev_count):
    smoothed = smooth(extended, lat_taps, elev_taps, lat_count, elev_count).astype(jnp.bfloat16)
    flat_rows = smoothed.reshape(-1, matrix.shape[0])
    return jnp.dot(flat_rows, matrix, preferred_element_type=jnp.float32).astype(jnp.bfloat16)


def band_filter(gram_sum, clutter_rank, noise_rank):
    width = gram_sum.shape[0]
    identity = jnp.eye(width, dtype=jnp.float32)
    total_trace = jnp.sum(gram_sum * identity)

    def resolvent(rank_value):
        level = total_trace / rank_value.astype(jnp.float32)
        factor = jnp.linalg.cholesky(gram_sum + level * identity)
        solved = lax.linalg.triangular_solve(
            factor, jnp.sqrt(level) * identity, left_side=True, lower=True
        )
        return jnp.dot(solved.T, solved, precision=lax.Precision.HIGHEST)

    return resolvent(clutter_rank) - resolvent(noise_rank)


def body(volume, lat_taps, elev_taps, time_taps, clutter_rank, noise_rank):
    lat_count, elev_count, depth, columns = volume.shape
    matrix = time_matrix(time_taps, columns // 2)
    extended = padded(volume, (("lat", 0), ("elev", 1)), 3)
    row_block = filtered_rows(extended, lat_taps, elev_taps, matrix, lat_count, elev_count)
    local_gram = lax.dot_general(
        row_block, row_block, (((0,), (0,)), ((), ())), preferred_element_type=jnp.float32
    )
    gram_sum = lax.psum(local_gram, ("lat", "elev"))
    weights = band_filter(gram_sum, clutter_rank, noise_rank)
    cleaned_rows = jnp.dot(
        row_block, weights.astype(jnp.bfloat16), preferred_element_type=jnp.float32
    ).astype(jnp.bfloat16)
    cleaned = cleaned_rows.reshape(lat_count, elev_count, depth, columns)
    power = jnp.sum(jnp.square(cleaned.astype(jnp.float32)), axis=3)
    return (cleaned, power, weights)


def solution(mesh):
    placed = (P("lat", "elev", None, None), P(), P(), P(), P(), P())
    return jax.shard_map(
        body,
        mesh=mesh,
        in_specs=placed,
        out_specs=(P("lat", "elev", None, None), P("lat", "elev", None), P()),
        check_vma=False,
    )
```

profile of v0, /device:TPU:2, one launch (start us, length us, event | category | flops | bytes accessed | tf_op | source)
XLA Modules:
  0.0 562.0 jit_solution(13308468101731325432)
XLA Ops:
  7.2 2.2 fusion.40
  9.5 1.8 collective-permute-start
  11.3 1.3 collective-permute-start.1
  12.6 1.6 collective-permute-done
  14.9 3.3 collective-permute-done.1
  19.1 3.4 collective-permute-start.2
  22.5 2.6 collective-permute-start.3
  27.4 39.9 %collective-permute-done.2 = bf16[14,3,128,256]{3,2,1,0:T(8,128)(2,1)S(1)} collective-permute-done((bf16[14,3,128,256]{3,2,1,0:T(8,128)(2,1)S(1)}, bf16[14,3,128,256]{3,2,1,0:T(8,128)(2,1)S(1)}, u32[]{:S(2)}, u32[]{:S(2)}) %collective-permute-start.2) | collective-permute-done | bytes 2752544 | tf_op jit(solution)/shard_map/ppermute | solution.py:12
  67.2 3.7 collective-permute-done.3
  70.9 5.9 %pad_maximum_fusion = bf16[14,14,128,256]{3,2,1,0:T(8,128)(2,1)} fusion(bf16[14,3,128,256]{3,2,1,0:T(8,128)(2,1)S(1)} %collective-permute-done.3, bf16[14,8,128,256]{3,2,1,0:T(8,128)(2,1)S(1)} %constant_dynamic-update-slice_fusion, bf16[14,3,128,256]{3,2,1,0:T(8,128)(2,1)S(1)} %collective-permute-done.2), kind=kLoop, calls=%fused_computation.5 | loop fusion | flops 12845056 | bytes 25690112 | tf_op jit(solution)/shard_map/concatenate | solution.py:16
  76.8 26.1 %multiply_add_fusion = f32[8,14,128,256]{3,2,1,0:T(8,128)S(1)} fusion(bf16[14,14,128,256]{3,2,1,0:T(8,128)(2,1)} %pad_maximum_fusion, f32[]{:T(128)} %bitcast.7, f32[]{:T(128)} %bitcast.6, f32[]{:T(128)} %bitcast.5, f32[]{:T(128)} %bitcast.4, f32[]{:T(128)} %bitcast.3, f32[]{:T(128)} %bitcast.2, f32[]{:T(128)} %bitcast.1), kind=kLoop, calls=%fused_computation.4 | loop fusion | flops 73400320 | bytes 66060316 | tf_op jit(solution)/shard_map/add | solution.py:36
  102.9 11.7 %fusion.1 = bf16[8,8,128,256]{3,2,1,0:T(8,128)(2,1)S(1)} fusion(f32[8,14,128,256]{3,2,1,0:T(8,128)S(1)} %multiply_add_fusion, f32[]{:T(128)} %bitcast.13, f32[]{:T(128)} %bitcast.12, f32[]{:T(128)} %bitcast.11, f32[]{:T(128)} %bitcast.10, f32[]{:T(128)} %bitcast.9, f32[]{:T(128)} %bitcast.8, f32[]{:T(128)} %bitcast), kind=kLoop, calls=%fused_computation.10 | loop fusion | flops 29360128 | bytes 62914588 | tf_op jit(solution)/shard_map/convert_element_type | solution.py:46
  114.6 1.3 convolution_convert_fusion.1
  115.9 1.9 copy-done.1
  117.8 2.4 fusion.43
  121.6 288.6 %all-reduce.3.cloned.1.call-done = f32[256,256]{0,1:T(8,128)} async-done(((f32[256,256]{0,1:T(8,128)}), f32[256,256]{0,1:T(8,128)}) %all-reduce.3.cloned.1.call-update) | async-done | bytes 262160 | tf_op jit(solution)/shard_map/psum | solution.py:75
  410.2 1.6 select_reduce_fusion.1
  414.5 11.7 %cholesky.164 = f32[128,128]{1,0:T(8,128)S(1)} custom-call(f32[128,128]{1,0:T(8,128)S(1)} %cholesky.197), custom_call_target="Cholesky" | custom-call | tf_op jit(solution)/shard_map/jit(cholesky)/cholesky | solution.py:58
  426.3 9.8 %custom-call.15 = f32[1,128,128]{1,2,0:T(8,128)S(1)} custom-call(f32[1,128,128]{2,1,0:T(8,128)S(1)} %get-tuple-element.50), custom_call_target="InvertDiagBlocksLowerTriangular" | custom-call | tf_op jit(solution)/shard_map/jit(cholesky)/cholesky | solution.py:58
  436.6 22.1 %cholesky.181 = f32[128,128]{1,0:T(8,128)S(1)} custom-call(f32[128,128]{1,0:T(8,128)S(1)} %convolution_subtract_fusion.3), custom_call_target="Cholesky" | custom-call | tf_op jit(solution)/shard_map/jit(cholesky)/cholesky | solution.py:58
  461.4 4.0 while.5
  462.0 1.4 bitcast_dynamic-update-slice_fusion.5
  464.0 1.4 bitcast_dynamic-update-slice_fusion.5
  465.4 19.7 %custom-call.16 = f32[2,128,128]{1,2,0:T(8,128)S(1)} custom-call(f32[2,128,128]{2,1,0:T(8,128)S(1)} %get-tuple-element.20), custom_call_target="InvertDiagBlocksLowerTriangular" | custom-call | tf_op jit(solution)/shard_map/triangular_solve/custom-call.0 | solution.py:59
  486.2 11.7 %cholesky.130 = f32[128,128]{1,0:T(8,128)S(1)} custom-call(f32[128,128]{1,0:T(8,128)S(1)} %cholesky.194), custom_call_target="Cholesky" | custom-call | tf_op jit(solution)/shard_map/jit(cholesky)/cholesky | solution.py:58
  497.9 9.8 %custom-call.13 = f32[1,128,128]{1,2,0:T(8,128)S(1)} custom-call(f32[1,128,128]{2,1,0:T(8,128)S(1)} %get-tuple-element.54), custom_call_target="InvertDiagBlocksLowerTriangular" | custom-call | tf_op jit(solution)/shard_map/jit(cholesky)/cholesky | solution.py:58
  508.2 11.7 %cholesky.147 = f32[128,128]{1,0:T(8,128)S(1)} custom-call(f32[128,128]{1,0:T(8,128)S(1)} %convolution_subtract_fusion.4), custom_call_target="Cholesky" | custom-call | tf_op jit(solution)/shard_map/jit(cholesky)/cholesky | solution.py:58
  522.6 4.0 while.4
  523.2 1.4 bitcast_dynamic-update-slice_fusion.4
  525.2 1.4 bitcast_dynamic-update-slice_fusion.4
  526.6 19.9 %custom-call.14 = f32[2,128,128]{1,2,0:T(8,128)S(1)} custom-call(f32[2,128,128]{2,1,0:T(8,128)S(1)} %get-tuple-element.19), custom_call_target="InvertDiagBlocksLowerTriangular" | custom-call | tf_op jit(solution)/shard_map/triangular_solve/custom-call.0 | solution.py:59
  548.8 6.2 %multiply_reduce_fusion = (f32[8192]{0:T(1024)}, bf16[8192,256]{1,0:T(8,128)(2,1)}) fusion(bf16[8192,256]{1,0:T(8,128)(2,1)} %copy-done.1, f32[256,256]{1,0:T(8,128)S(1)} %convolution_subtract_fusion), kind=kOutput, calls=%fused_computation.22 | convolution fusion | flops 1082187776 | bytes 8683520 | tf_op jit(solution)/shard_map/dot_general | solution.py:77
  (68 shorter events, 14.5 us)
Async XLA Ops:
  7.2 403.0 %all-reduce.3.cloned.1.call-start = ((), (), s32[]{:S(2)}) async-start(), calls=%async_computation | async-start | bytes 524288 | tf_op jit(solution)/shard_map/psum | solution.py:75
  7.2 7.1 %copy-start = (bf16[8,8,128,256]{3,2,1,0:T(8,128)(2,1)S(1)}, bf16[8,8,128,256]{3,2,1,0:T(8,128)(2,1)}, u32[]{:S(2)}) copy-start(bf16[8,8,128,256]{3,2,1,0:T(8,128)(2,1)} %param.9) | copy-start | bytes 12582916
  9.5 4.8 collective-permute-start
  11.3 6.9 %collective-permute-start.1 = (bf16[3,8,128,256]{3,2,1,0:T(8,128)(2,1)S(1)}, bf16[3,8,128,256]{3,2,1,0:T(8,128)(2,1)S(1)}, u32[]{:S(2)}, u32[]{:S(2)}) collective-permute-start(bf16[3,8,128,256]{3,2,1,0:T(8,128)(2,1)S(1)} %get-tuple-element.43), channel_id=1, source_target_pairs={{16,0},{32,16},{48,32},{64,48},{80,64},{96,80},{112,96},{128,112},... | collective-permute-start | bytes 4718600 | tf_op jit(solution)/shard_map/ppermute | solution.py:15
  14.8 10.2 %copy-start.5 = (bf16[32]{0:T(256)(128)(2,1)S(1)}, bf16[32]{0:T(256)(128)(2,1)}, u32[]{:S(2)}) copy-start(bf16[32]{0:T(256)(128)(2,1)} %param.12) | copy-start | bytes 196
  14.9 10.3 %copy-start.3 = (f32[7]{0:T(128)S(1)}, f32[7]{0:T(128)}, u32[]{:S(2)}) copy-start(f32[7]{0:T(128)} %param.10) | copy-start | bytes 88
  14.9 10.9 %copy-start.4 = (f32[7]{0:T(128)S(1)}, f32[7]{0:T(128)}, u32[]{:S(2)}) copy-start(f32[7]{0:T(128)} %param.11) | copy-start | bytes 88
  19.1 48.2 %collective-permute-start.2 = (bf16[14,3,128,256]{3,2,1,0:T(8,128)(2,1)S(1)}, bf16[14,3,128,256]{3,2,1,0:T(8,128)(2,1)S(1)}, u32[]{:S(2)}, u32[]{:S(2)}) collective-permute-start(bf16[14,3,128,256]{3,2,1,0:T(8,128)(2,1)S(1)} %get-tuple-element.41), channel_id=1, source_target_pairs={{0,1},{1,2},{2,3},{3,4},{4,5},{5,6},{6,7},{7,8},{8,9},{9,10},{10,1... | collective-permute-start | bytes 8257544 | tf_op jit(solution)/shard_map/ppermute | solution.py:12
  22.5 48.5 %collective-permute-start.3 = (bf16[14,3,128,256]{3,2,1,0:T(8,128)(2,1)S(1)}, bf16[14,3,128,256]{3,2,1,0:T(8,128)(2,1)S(1)}, u32[]{:S(2)}, u32[]{:S(2)}) collective-permute-start(bf16[14,3,128,256]{3,2,1,0:T(8,128)(2,1)S(1)} %get-tuple-element.42), channel_id=1, source_target_pairs={{1,0},{2,1},{3,2},{4,3},{5,4},{6,5},{7,6},{8,7},{9,8},{10,9},{11,1... | collective-permute-start | bytes 8257544 | tf_op jit(solution)/shard_map/ppermute | solution.py:15
  115.9 1.9 copy-start.1
  548.8 6.2 %copy-start.2 = (f32[256,256]{1,0:T(8,128)}, f32[256,256]{1,0:T(8,128)S(1)}, u32[]{:S(2)}) copy-start(f32[256,256]{1,0:T(8,128)S(1)} %convolution_subtract_fusion) | copy-start | bytes 786436
Sparse Core Ops, SparseCore 0:
  120.4 289.7 all-reduce.2
where the time goes:
time: 569 us; the launch traced here: 562 us
  waiting for transfers between devices  337 us (59%)
  other arithmetic  166 us (29%)
  between operations  20 us (4%)
  local copies, waits for them, and re-layouts  15.2 us (3%)
  matrix products  14 us (2%)
  starting transfers between devices  9.18 us (2%)
    psum x1, waiting for transfers between devices, body(): gram_sum = lax.psum(local_gram, ('lat', 'elev'))  289 us
    another operation x14, other arithmetic, resolvent(): factor = jnp.linalg.cholesky(gram_sum + level * identity)  79.5 us
    ppermute x2, waiting for transfers between devices, padded(): lax.ppermute(lax.slice_in_dim(block, block.shape[dim] - width, None, axis...  41.5 us
    another operation x5, other arithmetic, resolvent(): lax.linalg.triangular_solve(factor, jnp.sqrt(level) * identity, left_side...  39.6 us
    add x1, other arithmetic, smooth(): lat_sum + lat_taps[index_tap] * extended[index_tap:index_tap + lat_count]...  26.1 us
    convert_element_type x1, other arithmetic, filtered_rows(): smooth(extended, lat_taps, elev_taps, lat_count, elev_count)  11.7 us
  transfers between devices with their start and end apart: 5, of which 5 were waited for; matrix products, arithmetic and copies ran while one was open for 1% of the time, Pallas kernels for 0%

commit v1 on v0

--- a/solution.py
+++ b/solution.py
@@ -48,20 +48,54 @@
     return jnp.dot(flat_rows, matrix, preferred_element_type=jnp.float32).astype(jnp.bfloat16)
 
 
-def band_filter(gram_sum, clutter_rank, noise_rank):
+def butterfly_sum(block):
+    for axis in ("lat", "elev"):
+        count = lax.axis_size(axis)
+        stride = 1
+        while stride < count:
+            pairs = [(i, i ^ stride) for i in range(count)]
+            block = block + lax.ppermute(block, axis, pairs)
+            stride *= 2
+    return block
+
+
+def packed_gram_sum(gram):
+    half = gram.shape[0] // 2
+    upper = gram[:half, :half]
+    side = gram[:half, half:]
+    lower = gram[half:, half:]
+    row = jnp.arange(half, dtype=jnp.int32)[:, None]
+    col = jnp.arange(half, dtype=jnp.int32)[None, :]
+    keep_upper = row <= col
+    merged = jnp.where(keep_upper, upper, lower)
+    diagonal = jnp.diagonal(lower)[None, :]
+    packed = butterfly_sum(jnp.concatenate([side, merged, diagonal], axis=0))
+    side = packed[:half]
+    merged = packed[half : 2 * half]
+    diagonal = packed[2 * half]
+    upper = jnp.where(keep_upper, merged, merged.T)
+    lower = jnp.where(row > col, merged, merged.T)
+    lower = jnp.where(row == col, diagonal[None, :], lower)
+    return jnp.concatenate(
+        [jnp.concatenate([upper, side], axis=1), jnp.concatenate([side.T, lower], axis=1)], axis=0
+    )
+
+
+def band_filter(gram_sum, clutter_rank, noise_rank, steps=13):
     width = gram_sum.shape[0]
     identity = jnp.eye(width, dtype=jnp.float32)
     total_trace = jnp.sum(gram_sum * identity)
-
-    def resolvent(rank_value):
-        level = total_trace / rank_value.astype(jnp.float32)
-        factor = jnp.linalg.cholesky(gram_sum + level * identity)
-        solved = lax.linalg.triangular_solve(
-            factor, jnp.sqrt(level) * identity, left_side=True, lower=True
+    levels = total_trace / jnp.stack([clutter_rank, noise_rank]).astype(jnp.float32)
+    shifted = gram_sum[None] + levels[:, None, None] * identity[None]
+    scale = 2.0 / (2.0 * levels + total_trace)
+    inverse = scale[:, None, None] * identity[None]
+    for _ in range(steps):
+        product = jnp.einsum("bij,bjk->bik", shifted, inverse, precision=lax.Precision.HIGHEST)
+        inverse = 2.0 * inverse - jnp.einsum(
+            "bij,bjk->bik", inverse, product, precision=lax.Precision.HIGHEST
         )
-        return jnp.dot(solved.T, solved, precision=lax.Precision.HIGHEST)
-
-    return resolvent(clutter_rank) - resolvent(noise_rank)
+    resolvents = levels[:, None, None] * inverse
+    return resolvents[0] - resolvents[1]
 
 
 def body(volume, lat_taps, elev_taps, time_taps, clutter_rank, noise_rank):
@@ -72,7 +106,7 @@
     local_gram = lax.dot_general(
         row_block, row_block, (((0,), (0,)), ((), ())), preferred_element_type=jnp.float32
     )
-    gram_sum = lax.psum(local_gram, ("lat", "elev"))
+    gram_sum = packed_gram_sum(local_gram)
     weights = band_filter(gram_sum, clutter_rank, noise_rank)
     cleaned_rows = jnp.dot(
         row_block, weights.astype(jnp.bfloat16), preferred_element_type=jnp.float32

time: 569 us -> 235 us (0.41); the launches traced: 562 us -> 234 us
  waiting for transfers between devices: 337 us -> 80.5 us
  other arithmetic: 166 us -> 50.8 us
  starting transfers between devices: 9.18 us -> 61.6 us
  between operations: 20 us -> 2.47 us
  matrix products: 14 us -> 24.6 us
    psum x1 -> x0, waiting for transfers between devices: 289 us -> none  [body(): gram_sum = lax.psum(local_gram, ('lat', 'elev'))]
    another operation x19 -> x0, other arithmetic: 119 us -> none  [the longest x14 79.5 us: resolvent(): factor = jnp.linalg.cholesky(gram_sum + level * identity)]
    ppermute x0 -> x8, starting transfers between devices: none -> 52.4 us  [butterfly_sum(): block = block + lax.ppermute(block, axis, pairs)]
    ppermute x0 -> x8, waiting for transfers between devices: none -> 32 us  [butterfly_sum(): block = block + lax.ppermute(block, axis, pairs)]
    dot_general x2 -> x26, matrix products: 1.19 us -> 18.2 us  [the longest x13 9.42 us: band_filter(): jnp.einsum('bij,bjk->bik', shifted, inverse, precision=lax.Precision.HIGH...]
    another operation x19 -> x0, local copies, waits for them, and re-layouts: 8.04 us -> none  [the longest x15 7.99 us: resolvent(): lax.linalg.triangular_solve(factor, jnp.sqrt(level) * identity, left_side...]
  transfers between devices with their start and end apart: 5 -> 12, of which waited for: 5 -> 12; matrix products, arithmetic and copies ran while one was open for 1% -> 1% of each run, Pallas kernels for 0% -> 0%
where the time goes in v1:
time: 235 us; the launch traced here: 234 us
  waiting for transfers between devices  80.5 us (34%)
  starting transfers between devices  61.6 us (26%)
  other arithmetic  50.8 us (22%)
  matrix products  24.6 us (10%)
  local copies, waits for them, and re-layouts  13.9 us (6%)
  between operations  2.47 us (1%)
    ppermute x8, starting transfers between devices, butterfly_sum(): block = block + lax.ppermute(block, axis, pairs)  52.4 us
    ppermute x2, waiting for transfers between devices, padded(): lax.ppermute(lax.slice_in_dim(block, block.shape[dim] - width, None, axis...  41.5 us
    ppermute x8, waiting for transfers between devices, butterfly_sum(): block = block + lax.ppermute(block, axis, pairs)  32 us
    add x1, other arithmetic, smooth(): lat_sum + lat_taps[index_tap] * extended[index_tap:index_tap + lat_count]...  26.1 us
    convert_element_type x1, other arithmetic, filtered_rows(): smooth(extended, lat_taps, elev_taps, lat_count, elev_count)  11.1 us
    concatenate x1, other arithmetic, padded(): block = jnp.concatenate([low, block, high], axis=dim)  11 us
    dot_general x13, matrix products, band_filter(): jnp.einsum('bij,bjk->bik', shifted, inverse, precision=lax.Precision.HIGH...  9.42 us
    dot_general x13, matrix products, band_filter(): jnp.einsum('bij,bjk->bik', inverse, product, precision=lax.Precision.HIGH...  8.75 us
  transfers between devices with their start and end apart: 12, of which 12 were waited for; matrix products, arithmetic and copies ran while one was open for 1% of the time, Pallas kernels for 0%

profile of v1, /device:TPU:2, one launch (start us, length us, event | category | flops | bytes accessed | tf_op | source)
XLA Modules:
  0.0 233.8 jit_solution(15782317533450651435)
XLA Ops:
  0.6 2.2 fusion.75
  2.9 1.8 collective-permute-start
  4.7 1.3 collective-permute-start.1
  6.0 1.6 collective-permute-done
  8.3 3.3 %collective-permute-done.1 = bf16[3,8,128,256]{3,2,1,0:T(8,128)(2,1)S(1)} collective-permute-done((bf16[3,8,128,256]{3,2,1,0:T(8,128)(2,1)S(1)}, bf16[3,8,128,256]{3,2,1,0:T(8,128)(2,1)S(1)}, u32[]{:S(2)}, u32[]{:S(2)}) %collective-permute-start.1) | collective-permute-done | bytes 1572896 | tf_op jit(solution)/shard_map/ppermute | solution.py:15
  11.8 2.9 %copy-done.2 = bf16[14,8,128,256]{3,2,1,0:T(8,128)(2,1)} copy-done((bf16[14,8,128,256]{3,2,1,0:T(8,128)(2,1)}, bf16[14,8,128,256]{3,2,1,0:T(8,128)(2,1)S(1)}, u32[]{:S(2)}) %copy-start.2) | copy-done | bytes 7340056
  14.7 2.8 %fusion.74 = (bf16[14,3,128,256]{3,2,1,0:T(8,128)(2,1)}, bf16[14,3,128,256]{3,2,1,0:T(8,128)(2,1)}) fusion(bf16[14,8,128,256]{3,2,1,0:T(8,128)(2,1)S(1)} %constant_dynamic-update-slice_fusion), kind=kLoop, calls=%fused_computation.125 | loop fusion | bytes 11010048 | tf_op jit(solution)/shard_map/slice | solution.py:13
  17.5 3.4 %collective-permute-start.2 = (bf16[14,3,128,256]{3,2,1,0:T(8,128)(2,1)}, bf16[14,3,128,256]{3,2,1,0:T(8,128)(2,1)S(1)}, u32[]{:S(2)}, u32[]{:S(2)}) collective-permute-start(bf16[14,3,128,256]{3,2,1,0:T(8,128)(2,1)} %get-tuple-element.5), channel_id=1, source_target_pairs={{0,1},{1,2},{2,3},{3,4},{4,5},{5,6},{6,7},{7,8},{8,9},{9,10},{10,1... | collective-permute-start | bytes 8257544 | tf_op jit(solution)/shard_map/ppermute | solution.py:12
  20.9 2.6 %collective-permute-start.3 = (bf16[14,3,128,256]{3,2,1,0:T(8,128)(2,1)}, bf16[14,3,128,256]{3,2,1,0:T(8,128)(2,1)}, u32[]{:S(2)}, u32[]{:S(2)}) collective-permute-start(bf16[14,3,128,256]{3,2,1,0:T(8,128)(2,1)} %get-tuple-element.6), channel_id=1, source_target_pairs={{1,0},{2,1},{3,2},{4,3},{5,4},{6,5},{7,6},{8,7},{9,8},{10,9},{11,1... | collective-permute-start | bytes 8257544 | tf_op jit(solution)/shard_map/ppermute | solution.py:15
  26.0 39.8 %collective-permute-done.2 = bf16[14,3,128,256]{3,2,1,0:T(8,128)(2,1)S(1)} collective-permute-done((bf16[14,3,128,256]{3,2,1,0:T(8,128)(2,1)}, bf16[14,3,128,256]{3,2,1,0:T(8,128)(2,1)S(1)}, u32[]{:S(2)}, u32[]{:S(2)}) %collective-permute-start.2) | collective-permute-done | bytes 2752544 | tf_op jit(solution)/shard_map/ppermute | solution.py:12
  65.8 3.8 %collective-permute-done.3 = bf16[14,3,128,256]{3,2,1,0:T(8,128)(2,1)} collective-permute-done((bf16[14,3,128,256]{3,2,1,0:T(8,128)(2,1)}, bf16[14,3,128,256]{3,2,1,0:T(8,128)(2,1)}, u32[]{:S(2)}, u32[]{:S(2)}) %collective-permute-start.3) | collective-permute-done | bytes 2752544 | tf_op jit(solution)/shard_map/ppermute | solution.py:15
  69.6 11.0 %pad_maximum_fusion = bf16[14,14,128,256]{3,2,1,0:T(8,128)(2,1)} fusion(bf16[14,3,128,256]{3,2,1,0:T(8,128)(2,1)} %collective-permute-done.3, bf16[14,8,128,256]{3,2,1,0:T(8,128)(2,1)} %copy-done.2, bf16[14,3,128,256]{3,2,1,0:T(8,128)(2,1)S(1)} %collective-permute-done.2), kind=kLoop, calls=%fused_computation.2 | loop fusion | flops 12845056 | bytes 25690112 | tf_op jit(solution)/shard_map/concatenate | solution.py:16
  80.6 26.1 %multiply_add_fusion = f32[8,14,128,256]{3,2,1,0:T(8,128)S(1)} fusion(bf16[14,14,128,256]{3,2,1,0:T(8,128)(2,1)} %pad_maximum_fusion, f32[]{:T(128)} %bitcast.7, f32[]{:T(128)} %bitcast.6, f32[]{:T(128)} %bitcast.5, f32[]{:T(128)} %bitcast.4, f32[]{:T(128)} %bitcast.3, f32[]{:T(128)} %bitcast.2, f32[]{:T(128)} %bitcast.1), kind=kLoop, calls=%fused_computation.1 | loop fusion | flops 73400320 | bytes 66060316 | tf_op jit(solution)/shard_map/add | solution.py:36
  106.6 11.1 %fusion.1 = bf16[8,8,128,256]{3,2,1,0:T(8,128)(2,1)S(1)} fusion(f32[8,14,128,256]{3,2,1,0:T(8,128)S(1)} %multiply_add_fusion, f32[]{:T(128)} %bitcast.13, f32[]{:T(128)} %bitcast.12, f32[]{:T(128)} %bitcast.11, f32[]{:T(128)} %bitcast.10, f32[]{:T(128)} %bitcast.9, f32[]{:T(128)} %bitcast.8, f32[]{:T(128)} %bitcast), kind=kLoop, calls=%fused_computation.7 | loop fusion | flops 29360128 | bytes 62914588 | tf_op jit(solution)/shard_map/convert_element_type | solution.py:46
  117.8 1.3 convolution_convert_fusion.1
  119.1 2.0 copy-done
  121.1 1.3 fusion.80
  123.6 16.0 %collective-permute-start.4 = (f32[257,128]{1,0:T(8,128)S(1)}, f32[257,128]{1,0:T(8,128)S(1)}, u32[]{:S(2)}, u32[]{:S(2)}) collective-permute-start(f32[257,128]{1,0:T(8,128)S(1)} %pad_maximum_fusion.1), channel_id=1, source_target_pairs={{0,16},{16,0},{32,48},{48,32},{64,80},{80,64},{96,112},{112,96},{1... | collective-permute-start | bytes 394760 | tf_op jit(solution)/shard_map/ppermute | solution.py:57
  140.6 16.9 %collective-permute-start.5 = (f32[257,128]{1,0:T(8,128)S(1)}, f32[257,128]{1,0:T(8,128)S(1)}, u32[]{:S(2)}, u32[]{:S(2)}) collective-permute-start(f32[257,128]{1,0:T(8,128)S(1)} %fusion.72), channel_id=1, source_target_pairs={{0,32},{16,48},{32,0},{48,16},{64,96},{80,112},{96,64},{112,80},{1... | collective-permute-start | bytes 394760 | tf_op jit(solution)/shard_map/ppermute | solution.py:57
  157.6 4.1 %collective-permute-done.5 = f32[257,128]{1,0:T(8,128)S(1)} collective-permute-done((f32[257,128]{1,0:T(8,128)S(1)}, f32[257,128]{1,0:T(8,128)S(1)}, u32[]{:S(2)}, u32[]{:S(2)}) %collective-permute-start.5) | collective-permute-done | bytes 131616 | tf_op jit(solution)/shard_map/ppermute | solution.py:57
  161.7 3.4 %collective-permute-start.6 = (f32[257,128]{1,0:T(8,128)S(1)}, f32[257,128]{1,0:T(8,128)S(1)}, u32[]{:S(2)}, u32[]{:S(2)}) collective-permute-start(f32[257,128]{1,0:T(8,128)S(1)} %add.93), channel_id=1, source_target_pairs={{0,64},{16,80},{32,96},{48,112},{64,0},{80,16},{96,32},{112,48},{1... | collective-permute-start | bytes 394760 | tf_op jit(solution)/shard_map/ppermute | solution.py:57
  165.0 6.3 %collective-permute-done.6 = f32[257,128]{1,0:T(8,128)S(1)} collective-permute-done((f32[257,128]{1,0:T(8,128)S(1)}, f32[257,128]{1,0:T(8,128)S(1)}, u32[]{:S(2)}, u32[]{:S(2)}) %collective-permute-start.6) | collective-permute-done | bytes 131616 | tf_op jit(solution)/shard_map/ppermute | solution.py:57
  171.4 6.5 %collective-permute-start.7 = (f32[257,128]{1,0:T(8,128)S(1)}, f32[257,128]{1,0:T(8,128)S(1)}, u32[]{:S(2)}, u32[]{:S(2)}) collective-permute-start(f32[257,128]{1,0:T(8,128)S(1)} %add.94), channel_id=1, source_target_pairs={{0,128},{16,144},{32,160},{48,176},{64,192},{80,208},{96,224},{112... | collective-permute-start | bytes 394760 | tf_op jit(solution)/shard_map/ppermute | solution.py:57
  177.9 6.3 %collective-permute-done.7 = f32[257,128]{1,0:T(8,128)S(1)} collective-permute-done((f32[257,128]{1,0:T(8,128)S(1)}, f32[257,128]{1,0:T(8,128)S(1)}, u32[]{:S(2)}, u32[]{:S(2)}) %collective-permute-start.7) | collective-permute-done | bytes 131616 | tf_op jit(solution)/shard_map/ppermute | solution.py:57
  185.0 4.3 %collective-permute-done.8 = f32[257,128]{1,0:T(8,128)S(1)} collective-permute-done((f32[257,128]{1,0:T(8,128)S(1)}, f32[257,128]{1,0:T(8,128)S(1)}, u32[]{:S(2)}, u32[]{:S(2)}) %collective-permute-start.8) | collective-permute-done | bytes 131616 | tf_op jit(solution)/shard_map/ppermute | solution.py:57
  189.3 4.3 %collective-permute-start.9 = (f32[257,128]{1,0:T(8,128)S(1)}, f32[257,128]{1,0:T(8,128)S(1)}, u32[]{:S(2)}, u32[]{:S(2)}) collective-permute-start(f32[257,128]{1,0:T(8,128)S(1)} %add.96), channel_id=1, source_target_pairs={{0,2},{1,3},{2,0},{3,1},{4,6},{5,7},{6,4},{7,5},{8,10},{9,11},{10,... | collective-permute-start | bytes 394760 | tf_op jit(solution)/shard_map/ppermute | solution.py:57
  193.6 3.0 %collective-permute-done.9 = f32[257,128]{1,0:T(8,128)S(1)} collective-permute-done((f32[257,128]{1,0:T(8,128)S(1)}, f32[257,128]{1,0:T(8,128)S(1)}, u32[]{:S(2)}, u32[]{:S(2)}) %collective-permute-start.9) | collective-permute-done | bytes 131616 | tf_op jit(solution)/shard_map/ppermute | solution.py:57
  196.7 1.7 collective-permute-start.10
  198.3 4.5 %collective-permute-done.10 = f32[257,128]{1,0:T(8,128)S(1)} collective-permute-done((f32[257,128]{1,0:T(8,128)S(1)}, f32[257,128]{1,0:T(8,128)S(1)}, u32[]{:S(2)}, u32[]{:S(2)}) %collective-permute-start.10) | collective-permute-done | bytes 131616 | tf_op jit(solution)/shard_map/ppermute | solution.py:57
  202.8 2.9 %collective-permute-start.11 = (f32[257,128]{1,0:T(8,128)S(1)}, f32[257,128]{1,0:T(8,128)S(1)}, u32[]{:S(2)}, u32[]{:S(2)}) collective-permute-start(f32[257,128]{1,0:T(8,128)S(1)} %add.98), channel_id=1, source_target_pairs={{0,8},{1,9},{2,10},{3,11},{4,12},{5,13},{6,14},{7,15},{8,0},{9,1},... | collective-permute-start | bytes 394760 | tf_op jit(solution)/shard_map/ppermute | solution.py:57
  207.2 2.4 %collective-permute-done.11 = f32[257,128]{1,0:T(8,128)S(1)} collective-permute-done((f32[257,128]{1,0:T(8,128)S(1)}, f32[257,128]{1,0:T(8,128)S(1)}, u32[]{:S(2)}, u32[]{:S(2)}) %collective-permute-start.11) | collective-permute-done | bytes 131616 | tf_op jit(solution)/shard_map/ppermute | solution.py:57
  230.0 3.9 %multiply_reduce_fusion = (f32[8192]{0:T(1024)}, bf16[8192,256]{1,0:T(8,128)(2,1)}) fusion(bf16[8192,256]{1,0:T(8,128)(2,1)S(1)} %copy-done.1, f32[256,256]{1,0:T(8,128)S(1)} %fusion.23), kind=kOutput, calls=%fused_computation.19 | convolution fusion | flops 1082187776 | bytes 8683520 | tf_op jit(solution)/shard_map/dot_general | solution.py:111
  (77 shorter events, 26.5 us)
Async XLA Ops:
  0.6 7.2 %copy-start.3 = (bf16[8,8,128,256]{3,2,1,0:T(8,128)(2,1)S(1)}, bf16[8,8,128,256]{3,2,1,0:T(8,128)(2,1)}, u32[]{:S(2)}) copy-start(bf16[8,8,128,256]{3,2,1,0:T(8,128)(2,1)} %param.6) | copy-start | bytes 12582916
  2.9 4.8 %collective-permute-start = (bf16[3,8,128,256]{3,2,1,0:T(8,128)(2,1)S(1)}, bf16[3,8,128,256]{3,2,1,0:T(8,128)(2,1)S(1)}, u32[]{:S(2)}, u32[]{:S(2)}) collective-permute-start(bf16[3,8,128,256]{3,2,1,0:T(8,128)(2,1)S(1)} %get-tuple-element.8), channel_id=1, source_target_pairs={{0,16},{16,32},{32,48},{48,64},{64,80},{80,96},{96,112},{112,128},... | collective-permute-start | bytes 4718600 | tf_op jit(solution)/shard_map/ppermute | solution.py:12
  4.7 6.9 %collective-permute-start.1 = (bf16[3,8,128,256]{3,2,1,0:T(8,128)(2,1)S(1)}, bf16[3,8,128,256]{3,2,1,0:T(8,128)(2,1)S(1)}, u32[]{:S(2)}, u32[]{:S(2)}) collective-permute-start(bf16[3,8,128,256]{3,2,1,0:T(8,128)(2,1)S(1)} %get-tuple-element.7), channel_id=1, source_target_pairs={{16,0},{32,16},{48,32},{64,48},{80,64},{96,80},{112,96},{128,112},... | collective-permute-start | bytes 4718600 | tf_op jit(solution)/shard_map/ppermute | solution.py:15
  8.3 15.2 %copy-start.7 = (bf16[32]{0:T(256)(128)(2,1)S(1)}, bf16[32]{0:T(256)(128)(2,1)}, u32[]{:S(2)}) copy-start(bf16[32]{0:T(256)(128)(2,1)} %param.9) | copy-start | bytes 196
  8.3 15.4 %copy-start.5 = (f32[7]{0:T(128)S(1)}, f32[7]{0:T(128)}, u32[]{:S(2)}) copy-start(f32[7]{0:T(128)} %param.7) | copy-start | bytes 88
  8.3 16.1 %copy-start.6 = (f32[7]{0:T(128)S(1)}, f32[7]{0:T(128)}, u32[]{:S(2)}) copy-start(f32[7]{0:T(128)} %param.8) | copy-start | bytes 88
  11.8 2.9 %copy-start.2 = (bf16[14,8,128,256]{3,2,1,0:T(8,128)(2,1)}, bf16[14,8,128,256]{3,2,1,0:T(8,128)(2,1)S(1)}, u32[]{:S(2)}) copy-start(bf16[14,8,128,256]{3,2,1,0:T(8,128)(2,1)S(1)} %constant_dynamic-update-slice_fusion) | copy-start | bytes 22020100
  17.5 48.3 %collective-permute-start.2 = (bf16[14,3,128,256]{3,2,1,0:T(8,128)(2,1)}, bf16[14,3,128,256]{3,2,1,0:T(8,128)(2,1)S(1)}, u32[]{:S(2)}, u32[]{:S(2)}) collective-permute-start(bf16[14,3,128,256]{3,2,1,0:T(8,128)(2,1)} %get-tuple-element.5), channel_id=1, source_target_pairs={{0,1},{1,2},{2,3},{3,4},{4,5},{5,6},{6,7},{7,8},{8,9},{9,10},{10,1... | collective-permute-start | bytes 8257544 | tf_op jit(solution)/shard_map/ppermute | solution.py:12
  20.9 48.7 %collective-permute-start.3 = (bf16[14,3,128,256]{3,2,1,0:T(8,128)(2,1)}, bf16[14,3,128,256]{3,2,1,0:T(8,128)(2,1)}, u32[]{:S(2)}, u32[]{:S(2)}) collective-permute-start(bf16[14,3,128,256]{3,2,1,0:T(8,128)(2,1)} %get-tuple-element.6), channel_id=1, source_target_pairs={{1,0},{2,1},{3,2},{4,3},{5,4},{6,5},{7,6},{8,7},{9,8},{10,9},{11,1... | collective-permute-start | bytes 8257544 | tf_op jit(solution)/shard_map/ppermute | solution.py:15
  119.0 2.0 copy-start
  123.6 17.0 %collective-permute-start.4 = (f32[257,128]{1,0:T(8,128)S(1)}, f32[257,128]{1,0:T(8,128)S(1)}, u32[]{:S(2)}, u32[]{:S(2)}) collective-permute-start(f32[257,128]{1,0:T(8,128)S(1)} %pad_maximum_fusion.1), channel_id=1, source_target_pairs={{0,16},{16,0},{32,48},{48,32},{64,80},{80,64},{96,112},{112,96},{1... | collective-permute-start | bytes 394760 | tf_op jit(solution)/shard_map/ppermute | solution.py:57
  140.6 21.0 %collective-permute-start.5 = (f32[257,128]{1,0:T(8,128)S(1)}, f32[257,128]{1,0:T(8,128)S(1)}, u32[]{:S(2)}, u32[]{:S(2)}) collective-permute-start(f32[257,128]{1,0:T(8,128)S(1)} %fusion.72), channel_id=1, source_target_pairs={{0,32},{16,48},{32,0},{48,16},{64,96},{80,112},{96,64},{112,80},{1... | collective-permute-start | bytes 394760 | tf_op jit(solution)/shard_map/ppermute | solution.py:57
  161.7 9.7 %collective-permute-start.6 = (f32[257,128]{1,0:T(8,128)S(1)}, f32[257,128]{1,0:T(8,128)S(1)}, u32[]{:S(2)}, u32[]{:S(2)}) collective-permute-start(f32[257,128]{1,0:T(8,128)S(1)} %add.93), channel_id=1, source_target_pairs={{0,64},{16,80},{32,96},{48,112},{64,0},{80,16},{96,32},{112,48},{1... | collective-permute-start | bytes 394760 | tf_op jit(solution)/shard_map/ppermute | solution.py:57
  171.4 12.8 %collective-permute-start.7 = (f32[257,128]{1,0:T(8,128)S(1)}, f32[257,128]{1,0:T(8,128)S(1)}, u32[]{:S(2)}, u32[]{:S(2)}) collective-permute-start(f32[257,128]{1,0:T(8,128)S(1)} %add.94), channel_id=1, source_target_pairs={{0,128},{16,144},{32,160},{48,176},{64,192},{80,208},{96,224},{112... | collective-permute-start | bytes 394760 | tf_op jit(solution)/shard_map/ppermute | solution.py:57
  184.2 5.1 %collective-permute-start.8 = (f32[257,128]{1,0:T(8,128)S(1)}, f32[257,128]{1,0:T(8,128)S(1)}, u32[]{:S(2)}, u32[]{:S(2)}) collective-permute-start(f32[257,128]{1,0:T(8,128)S(1)} %add.95), channel_id=1, source_target_pairs={{0,1},{1,0},{2,3},{3,2},{4,5},{5,4},{6,7},{7,6},{8,9},{9,8},{10,11... | collective-permute-start | bytes 394760 | tf_op jit(solution)/shard_map/ppermute | solution.py:57
  189.3 7.3 %collective-permute-start.9 = (f32[257,128]{1,0:T(8,128)S(1)}, f32[257,128]{1,0:T(8,128)S(1)}, u32[]{:S(2)}, u32[]{:S(2)}) collective-permute-start(f32[257,128]{1,0:T(8,128)S(1)} %add.96), channel_id=1, source_target_pairs={{0,2},{1,3},{2,0},{3,1},{4,6},{5,7},{6,4},{7,5},{8,10},{9,11},{10,... | collective-permute-start | bytes 394760 | tf_op jit(solution)/shard_map/ppermute | solution.py:57
  196.7 6.2 %collective-permute-start.10 = (f32[257,128]{1,0:T(8,128)S(1)}, f32[257,128]{1,0:T(8,128)S(1)}, u32[]{:S(2)}, u32[]{:S(2)}) collective-permute-start(f32[257,128]{1,0:T(8,128)S(1)} %add.97), channel_id=1, source_target_pairs={{0,4},{1,5},{2,6},{3,7},{4,0},{5,1},{6,2},{7,3},{8,12},{9,13},{10,... | collective-permute-start | bytes 394760 | tf_op jit(solution)/shard_map/ppermute | solution.py:57
  202.8 6.8 %collective-permute-start.11 = (f32[257,128]{1,0:T(8,128)S(1)}, f32[257,128]{1,0:T(8,128)S(1)}, u32[]{:S(2)}, u32[]{:S(2)}) collective-permute-start(f32[257,128]{1,0:T(8,128)S(1)} %add.98), channel_id=1, source_target_pairs={{0,8},{1,9},{2,10},{3,11},{4,12},{5,13},{6,14},{7,15},{8,0},{9,1},... | collective-permute-start | bytes 394760 | tf_op jit(solution)/shard_map/ppermute | solution.py:57
  222.7 7.3 %copy-start.1 = (bf16[8192,256]{1,0:T(8,128)(2,1)S(1)}, bf16[8192,256]{1,0:T(8,128)(2,1)}, u32[]{:S(2)}) copy-start(bf16[8192,256]{1,0:T(8,128)(2,1)} %copy-done) | copy-start | bytes 12582916
  230.0 3.9 %copy-start.4 = (f32[256,256]{1,0:T(8,128)}, f32[256,256]{1,0:T(8,128)S(1)}, u32[]{:S(2)}) copy-start(f32[256,256]{1,0:T(8,128)S(1)} %fusion.23) | copy-start | bytes 786436

commit v2 on v1

--- a/solution.py
+++ b/solution.py
@@ -4,17 +4,49 @@
 from jax.sharding import PartitionSpec as P
 
 
-def padded(block, sides, width):
-    for axis, dim in sides:
+def halo_pieces(block, width):
+    lat_count = lax.axis_size("lat")
+    elev_count = lax.axis_size("elev")
+    lat_size, elev_size = block.shape[0], block.shape[1]
+    low_lat = slice(lat_size - width, lat_size)
+    high_lat = slice(0, width)
+    low_elev = slice(elev_size - width, elev_size)
+    high_elev = slice(0, width)
+
+    def shift(piece, axis, step):
         count = lax.axis_size(axis)
-        forward = [(i, i + 1) for i in range(count - 1)]
-        backward = [(target, source) for source, target in forward]
-        low = lax.ppermute(
-            lax.slice_in_dim(block, block.shape[dim] - width, None, axis=dim), axis, forward
-        )
-        high = lax.ppermute(lax.slice_in_dim(block, 0, width, axis=dim), axis, backward)
-        block = jnp.concatenate([low, block, high], axis=dim)
-    return block
+        pairs = [(i, i + step) for i in range(count) if 0 <= i + step < count]
+        return lax.ppermute(piece, axis, pairs)
+
+    def shift_both(piece, lat_step, elev_step):
+        pairs = []
+        for i in range(lat_count):
+            for j in range(elev_count):
+                ti, tj = i + lat_step, j + elev_step
+                if 0 <= ti < lat_count and 0 <= tj < elev_count:
+                    pairs.append((i * elev_count + j, ti * elev_count + tj))
+        return lax.ppermute(piece, ("lat", "elev"), pairs)
+
+    north = shift(block[low_lat], "lat", 1)
+    south = shift(block[high_lat], "lat", -1)
+    west = shift(block[:, low_elev], "elev", 1)
+    east = shift(block[:, high_elev], "elev", -1)
+    north_west = shift_both(block[low_lat, low_elev], 1, 1)
+    north_east = shift_both(block[low_lat, high_elev], 1, -1)
+    south_west = shift_both(block[high_lat, low_elev], -1, 1)
+    south_east = shift_both(block[high_lat, high_elev], -1, -1)
+    top = jnp.concatenate([north_west, north, north_east], axis=1)
+    middle = jnp.concatenate([west, block, east], axis=1)
+    bottom = jnp.concatenate([south_west, south, south_east], axis=1)
+    return jnp.concatenate([top, middle, bottom], axis=0)
+
+
+def band_taps(taps, count, width):
+    out_index = jnp.arange(count, dtype=jnp.int32)[:, None]
+    in_index = jnp.arange(count + 2 * width, dtype=jnp.int32)[None, :]
+    lag = in_index - out_index
+    matched = lag[:, :, None] == jnp.arange(taps.shape[0], dtype=jnp.int32)[None, None, :]
+    return jnp.sum(jnp.where(matched, taps[None, None, :], jnp.float32(0.0)), axis=2)
 
 
 def time_matrix(time_taps, frames):
@@ -30,20 +62,12 @@
     return paired.astype(jnp.bfloat16)
 
 
-def smooth(extended, lat_taps, elev_taps, lat_count, elev_count):
-    lat_sum = lat_taps[0] * extended[0:lat_count].astype(jnp.float32)
-    for index_tap in range(1, 7):
-        lat_sum = lat_sum + lat_taps[index_tap] * extended[
-            index_tap : index_tap + lat_count
-        ].astype(jnp.float32)
-    result = elev_taps[0] * lat_sum[:, 0:elev_count]
-    for index_tap in range(1, 7):
-        result = result + elev_taps[index_tap] * lat_sum[:, index_tap : index_tap + elev_count]
-    return result
-
-
 def filtered_rows(extended, lat_taps, elev_taps, matrix, lat_count, elev_count):
-    smoothed = smooth(extended, lat_taps, elev_taps, lat_count, elev_count).astype(jnp.bfloat16)
+    weights = jnp.kron(band_taps(lat_taps, lat_count, 3), band_taps(elev_taps, elev_count, 3))
+    sources = extended.reshape(weights.shape[1], -1).astype(jnp.float32)
+    smoothed = jnp.dot(
+        weights, sources, precision=lax.Precision.HIGH, preferred_element_type=jnp.float32
+    ).astype(jnp.bfloat16)
     flat_rows = smoothed.reshape(-1, matrix.shape[0])
     return jnp.dot(flat_rows, matrix, preferred_element_type=jnp.float32).astype(jnp.bfloat16)
 
@@ -101,7 +125,7 @@
 def body(volume, lat_taps, elev_taps, time_taps, clutter_rank, noise_rank):
     lat_count, elev_count, depth, columns = volume.shape
     matrix = time_matrix(time_taps, columns // 2)
-    extended = padded(volume, (("lat", 0), ("elev", 1)), 3)
+    extended = halo_pieces(volume, 3)
     row_block = filtered_rows(extended, lat_taps, elev_taps, matrix, lat_count, elev_count)
     local_gram = lax.dot_general(
         row_block, row_block, (((0,), (0,)), ((), ())), preferred_element_type=jnp.float32

time: 235 us -> 230 us (0.979)
  other arithmetic: 50.8 us -> 9.34 us
  local copies, waits for them, and re-layouts: 13.9 us -> 51.2 us
  starting transfers between devices: 61.6 us -> 39.7 us
  waiting for transfers between devices: 80.5 us -> 91.6 us
  matrix products: 24.6 us -> 33.5 us
    ppermute x8, starting transfers between devices: 52.4 us -> 19.9 us  [butterfly_sum(): block = block + lax.ppermute(block, axis, pairs)]
    unnamed x19 -> x17, local copies, waits for them, and re-layouts: 5.65 us -> 34.7 us
    add x1 -> x0, other arithmetic: 26.1 us -> none  [smooth(): lat_sum + lat_taps[index_tap] * extended[index_tap:index_tap + lat_count]...]
    convert_element_type x1 -> x0, other arithmetic: 11.1 us -> none  [filtered_rows(): smooth(extended, lat_taps, elev_taps, lat_count, elev_count)]
    ppermute x4 -> x8, starting transfers between devices: 9.13 us -> 19.8 us  [the longest x4 10.2 us: shift(): return lax.ppermute(piece, axis, pairs)]
    ppermute x4 -> x8, waiting for transfers between devices: 48.5 us -> 57.3 us  [the longest x4 57.3 us: shift_both(): return lax.ppermute(piece, ('lat', 'elev'), pairs)]
    reshape x0 -> x1, local copies, waits for them, and re-layouts: none -> 7.4 us  [filtered_rows(): flat_rows = smoothed.reshape(-1, matrix.shape[0])]
    dot_general x0 -> x1, matrix products: none -> 6.78 us  [filtered_rows(): jnp.dot(weights, sources, precision=lax.Precision.HIGH, preferred_element...]
  transfers between devices with their start and end apart: 12 -> 16, of which waited for: 12 -> 10; matrix products, arithmetic and copies ran while one was open for 1% -> 2% of each run, Pallas kernels for 0% -> 0%
where the time goes in v2:
time: 230 us; the launch traced here: 228 us
  waiting for transfers between devices  91.6 us (40%)
  local copies, waits for them, and re-layouts  51.2 us (22%)
  starting transfers between devices  39.7 us (17%)
  matrix products  33.5 us (15%)
  other arithmetic  9.34 us (4%)
  between operations  2.52 us (1%)
    ppermute x4, waiting for transfers between devices, shift_both(): return lax.ppermute(piece, ('lat', 'elev'), pairs)  57.3 us
    unnamed x17, local copies, waits for them, and re-layouts  34.7 us
    ppermute x8, waiting for transfers between devices, butterfly_sum(): block = block + lax.ppermute(block, axis, pairs)  34.2 us
    ppermute x8, starting transfers between devices, butterfly_sum(): block = block + lax.ppermute(block, axis, pairs)  19.9 us
    ppermute x4, starting transfers between devices, shift(): return lax.ppermute(piece, axis, pairs)  10.2 us
    ppermute x4, starting transfers between devices, shift_both(): return lax.ppermute(piece, ('lat', 'elev'), pairs)  9.54 us
    dot_general x13, matrix products, band_filter(): jnp.einsum('bij,bjk->bik', shifted, inverse, precision=lax.Precision.HIGH...  9.38 us
    dot_general x13, matrix products, band_filter(): jnp.einsum('bij,bjk->bik', inverse, product, precision=lax.Precision.HIGH...  8.75 us
  transfers between devices with their start and end apart: 16, of which 10 were waited for; matrix products, arithmetic and copies ran while one was open for 2% of the time, Pallas kernels for 0%

profile of v2, /device:TPU:2, one launch (start us, length us, event | category | flops | bytes accessed | tf_op | source)
XLA Modules:
  0.0 227.9 jit_solution(4880888459022175918)
XLA Ops:
  0.6 3.1 %fusion.67 = (bf16[3,3,128,256]{3,2,1,0:T(8,128)(2,1)S(1)}, bf16[3,3,128,256]{3,2,1,0:T(8,128)(2,1)}, bf16[3,3,128,256]{3,2,1,0:T(8,128)(2,1)S(1)}, bf16[3,3,128,256]{3,2,1,0:T(8,128)(2,1)}) fusion(bf16[8,8,128,256]{3,2,1,0:T(8,128)(2,1)} %param.6), kind=kLoop, calls=%fused_computation.113 | loop fusion | bytes 4718592 | tf_op jit(solution)/shard_map/slice | solution.py:34
  3.7 2.9 %collective-permute-start = (bf16[3,3,128,256]{3,2,1,0:T(8,128)(2,1)S(1)}, bf16[3,3,128,256]{3,2,1,0:T(8,128)(2,1)S(1)}, u32[]{:S(2)}, u32[]{:S(2)}) collective-permute-start(bf16[3,3,128,256]{3,2,1,0:T(8,128)(2,1)S(1)} %get-tuple-element.7), channel_id=1, source_target_pairs={{0,17},{1,18},{2,19},{3,20},{4,21},{5,22},{6,23},{7,24},{8,25},{9,... | collective-permute-start | bytes 1769480 | tf_op jit(solution)/shard_map/ppermute | solution.py:28
  6.6 4.1 %collective-permute-start.2 = (bf16[3,3,128,256]{3,2,1,0:T(8,128)(2,1)S(1)}, bf16[3,3,128,256]{3,2,1,0:T(8,128)(2,1)S(1)}, u32[]{:S(2)}, u32[]{:S(2)}) collective-permute-start(bf16[3,3,128,256]{3,2,1,0:T(8,128)(2,1)S(1)} %get-tuple-element.9), channel_id=1, source_target_pairs={{1,16},{2,17},{3,18},{4,19},{5,20},{6,21},{7,22},{8,23},{9,24},{10... | collective-permute-start | bytes 1769480 | tf_op jit(solution)/shard_map/ppermute | solution.py:28
  10.7 2.0 fusion.68
  12.7 1.9 collective-permute-start.1
  14.7 2.1 fusion.69
  16.7 3.4 %collective-permute-start.3 = (bf16[8,3,128,256]{3,2,1,0:T(8,128)(2,1)}, bf16[8,3,128,256]{3,2,1,0:T(8,128)(2,1)}, u32[]{:S(2)}, u32[]{:S(2)}) collective-permute-start(bf16[8,3,128,256]{3,2,1,0:T(8,128)(2,1)} %get-tuple-element.13), channel_id=1, source_target_pairs={{0,1},{1,2},{2,3},{3,4},{4,5},{5,6},{6,7},{7,8},{8,9},{9,10},{10,1... | collective-permute-start | bytes 4718600 | tf_op jit(solution)/shard_map/ppermute | solution.py:19
  20.1 3.7 %collective-permute-start.4 = (bf16[8,3,128,256]{3,2,1,0:T(8,128)(2,1)}, bf16[8,3,128,256]{3,2,1,0:T(8,128)(2,1)}, u32[]{:S(2)}, u32[]{:S(2)}) collective-permute-start(bf16[8,3,128,256]{3,2,1,0:T(8,128)(2,1)} %get-tuple-element.14), channel_id=1, source_target_pairs={{1,0},{2,1},{3,2},{4,3},{5,4},{6,5},{7,6},{8,7},{9,8},{10,9},{11,1... | collective-permute-start | bytes 4718600 | tf_op jit(solution)/shard_map/ppermute | solution.py:19
  23.8 1.3 collective-permute-start.6
  25.1 1.3 collective-permute-start.5
  27.0 41.8 %collective-permute-done.5 = bf16[3,3,128,256]{3,2,1,0:T(8,128)(2,1)} collective-permute-done((bf16[3,3,128,256]{3,2,1,0:T(8,128)(2,1)}, bf16[3,3,128,256]{3,2,1,0:T(8,128)(2,1)}, u32[]{:S(2)}, u32[]{:S(2)}) %collective-permute-start.5) | collective-permute-done | bytes 589856 | tf_op jit(solution)/shard_map/ppermute | solution.py:28
  71.0 15.5 %collective-permute-done.7 = bf16[3,3,128,256]{3,2,1,0:T(8,128)(2,1)S(1)} collective-permute-done((bf16[3,3,128,256]{3,2,1,0:T(8,128)(2,1)}, bf16[3,3,128,256]{3,2,1,0:T(8,128)(2,1)S(1)}, u32[]{:S(2)}, u32[]{:S(2)}) %collective-permute-start.7) | collective-permute-done | bytes 589856 | tf_op jit(solution)/shard_map/ppermute | solution.py:28
  86.6 6.5 %maximum_maximum_fusion = bf16[14,14,128,256]{3,2,1,0:T(8,128)(2,1)S(1)} fusion(bf16[3,3,128,256]{3,2,1,0:T(8,128)(2,1)S(1)} %collective-permute-done.7, bf16[3,8,128,256]{3,2,1,0:T(8,128)(2,1)} %collective-permute-done.6, bf16[3,3,128,256]{3,2,1,0:T(8,128)(2,1)} %collective-permute-done.5, bf16[8,3,128,256]{3,2,1,0:T(8,128)(2,1)} %collective-permute-done.4, ...), kind=kLoop, calls=%fused_computation.2 | loop fusion | flops 51380224 | bytes 25690112 | tf_op jit(solution)/shard_map/concatenate | solution.py:41
  94.4 32.6 %copy.28 = bf16[25,8,128,256]{3,1,2,0:T(8,128)(2,1)S(1)} copy(bf16[25,8,128,256]{3,2,1,0:T(8,128)(2,1)S(1)} %bitcast.73) | data formatting | bytes 26214400
  127.0 6.8 %convolution_convert_fusion = bf16[64,32768]{1,0:T(8,128)(2,1)} fusion(f32[64,196]{1,0:T(8,128)S(1)} %mul.142, bf16[196,32768]{1,0:T(8,128)(2,1)S(1)} %bitcast.72), kind=kOutput, calls=%fused_computation.1 | convolution fusion | flops 2468347904 | bytes 17089536 | tf_op jit(solution)/shard_map/dot_general | solution.py:68
  133.8 7.4 %reshape.126 = bf16[8192,256]{1,0:T(8,128)(2,1)} reshape(bf16[64,32768]{1,0:T(8,128)(2,1)} %convolution_convert_fusion) | data formatting | bytes 8388608 | tf_op jit(solution)/shard_map/reshape | solution.py:71
  141.2 3.4 %convolution_convert_fusion.2 = bf16[8192,256]{1,0:T(8,128)(2,1)S(1)} fusion(bf16[8192,256]{1,0:T(8,128)(2,1)} %reshape.126, bf16[32,8,2,128]{3,2,1,0:T(2,128)(2,1)S(1)} %bitcast.75), kind=kOutput, calls=%fused_computation.4 | convolution fusion | flops 1075838976 | bytes 8519680 | tf_op jit(solution)/shard_map/dot_general | solution.py:72
  144.7 1.3 fusion.72
  148.1 1.3 collective-permute-done.8
  149.4 2.1 collective-permute-start.9
  151.5 3.9 %collective-permute-done.9 = f32[257,128]{1,0:T(8,128)S(1)} collective-permute-done((f32[257,128]{1,0:T(8,128)S(1)}, f32[257,128]{1,0:T(8,128)S(1)}, u32[]{:S(2)}, u32[]{:S(2)}) %collective-permute-start.9) | collective-permute-done | bytes 131616 | tf_op jit(solution)/shard_map/ppermute | solution.py:81
  155.4 4.6 %collective-permute-start.10 = (f32[257,128]{1,0:T(8,128)S(1)}, f32[257,128]{1,0:T(8,128)S(1)}, u32[]{:S(2)}, u32[]{:S(2)}) collective-permute-start(f32[257,128]{1,0:T(8,128)S(1)} %add.45), channel_id=1, source_target_pairs={{0,64},{16,80},{32,96},{48,112},{64,0},{80,16},{96,32},{112,48},{1... | collective-permute-start | bytes 394760 | tf_op jit(solution)/shard_map/ppermute | solution.py:81
  160.0 6.2 %collective-permute-done.10 = f32[257,128]{1,0:T(8,128)S(1)} collective-permute-done((f32[257,128]{1,0:T(8,128)S(1)}, f32[257,128]{1,0:T(8,128)S(1)}, u32[]{:S(2)}, u32[]{:S(2)}) %collective-permute-start.10) | collective-permute-done | bytes 131616 | tf_op jit(solution)/shard_map/ppermute | solution.py:81
  166.2 4.1 %collective-permute-start.11 = (f32[257,128]{1,0:T(8,128)S(1)}, f32[257,128]{1,0:T(8,128)S(1)}, u32[]{:S(2)}, u32[]{:S(2)}) collective-permute-start(f32[257,128]{1,0:T(8,128)S(1)} %add.46), channel_id=1, source_target_pairs={{0,128},{16,144},{32,160},{48,176},{64,192},{80,208},{96,224},{112... | collective-permute-start | bytes 394760 | tf_op jit(solution)/shard_map/ppermute | solution.py:81
  170.3 7.5 %collective-permute-done.11 = f32[257,128]{1,0:T(8,128)S(1)} collective-permute-done((f32[257,128]{1,0:T(8,128)S(1)}, f32[257,128]{1,0:T(8,128)S(1)}, u32[]{:S(2)}, u32[]{:S(2)}) %collective-permute-start.11) | collective-permute-done | bytes 131616 | tf_op jit(solution)/shard_map/ppermute | solution.py:81
  178.1 5.0 %collective-permute-done.12 = f32[257,128]{1,0:T(8,128)S(1)} collective-permute-done((f32[257,128]{1,0:T(8,128)S(1)}, f32[257,128]{1,0:T(8,128)S(1)}, u32[]{:S(2)}, u32[]{:S(2)}) %collective-permute-start.12) | collective-permute-done | bytes 131616 | tf_op jit(solution)/shard_map/ppermute | solution.py:81
  183.1 5.3 %collective-permute-start.13 = (f32[257,128]{1,0:T(8,128)S(1)}, f32[257,128]{1,0:T(8,128)S(1)}, u32[]{:S(2)}, u32[]{:S(2)}) collective-permute-start(f32[257,128]{1,0:T(8,128)S(1)} %add.48), channel_id=1, source_target_pairs={{0,2},{1,3},{2,0},{3,1},{4,6},{5,7},{6,4},{7,5},{8,10},{9,11},{10,... | collective-permute-start | bytes 394760 | tf_op jit(solution)/shard_map/ppermute | solution.py:81
  188.4 3.0 %collective-permute-done.13 = f32[257,128]{1,0:T(8,128)S(1)} collective-permute-done((f32[257,128]{1,0:T(8,128)S(1)}, f32[257,128]{1,0:T(8,128)S(1)}, u32[]{:S(2)}, u32[]{:S(2)}) %collective-permute-start.13) | collective-permute-done | bytes 131616 | tf_op jit(solution)/shard_map/ppermute | solution.py:81
  192.2 5.0 %collective-permute-done.14 = f32[257,128]{1,0:T(8,128)S(1)} collective-permute-done((f32[257,128]{1,0:T(8,128)S(1)}, f32[257,128]{1,0:T(8,128)S(1)}, u32[]{:S(2)}, u32[]{:S(2)}) %collective-permute-start.14) | collective-permute-done | bytes 131616 | tf_op jit(solution)/shard_map/ppermute | solution.py:81
  197.2 2.8 %collective-permute-start.15 = (f32[257,128]{1,0:T(8,128)S(1)}, f32[257,128]{1,0:T(8,128)S(1)}, u32[]{:S(2)}, u32[]{:S(2)}) collective-permute-start(f32[257,128]{1,0:T(8,128)S(1)} %add.50), channel_id=1, source_target_pairs={{0,8},{1,9},{2,10},{3,11},{4,12},{5,13},{6,14},{7,15},{8,0},{9,1},... | collective-permute-start | bytes 394760 | tf_op jit(solution)/shard_map/ppermute | solution.py:81
  201.5 2.3 %collective-permute-done.15 = f32[257,128]{1,0:T(8,128)S(1)} collective-permute-done((f32[257,128]{1,0:T(8,128)S(1)}, f32[257,128]{1,0:T(8,128)S(1)}, u32[]{:S(2)}, u32[]{:S(2)}) %collective-permute-start.15) | collective-permute-done | bytes 131616 | tf_op jit(solution)/shard_map/ppermute | solution.py:81
  224.0 3.9 %multiply_reduce_fusion = (f32[8192]{0:T(1024)}, bf16[8192,256]{1,0:T(8,128)(2,1)}) fusion(bf16[8192,256]{1,0:T(8,128)(2,1)S(1)} %copy-done.1, f32[256,256]{1,0:T(8,128)S(1)} %fusion.16), kind=kOutput, calls=%fused_computation.5 | convolution fusion | flops 1082187776 | bytes 8683520 | tf_op jit(solution)/shard_map/dot_general | solution.py:135
  (85 shorter events, 27.4 us)
Async XLA Ops:
  0.6 10.1 %copy-start.2 = (bf16[8,8,128,256]{3,2,1,0:T(8,128)(2,1)S(1)}, bf16[8,8,128,256]{3,2,1,0:T(8,128)(2,1)}, u32[]{:S(2)}) copy-start(bf16[8,8,128,256]{3,2,1,0:T(8,128)(2,1)} %param.6) | copy-start | bytes 12582916
  3.7 20.1 %collective-permute-start = (bf16[3,3,128,256]{3,2,1,0:T(8,128)(2,1)S(1)}, bf16[3,3,128,256]{3,2,1,0:T(8,128)(2,1)S(1)}, u32[]{:S(2)}, u32[]{:S(2)}) collective-permute-start(bf16[3,3,128,256]{3,2,1,0:T(8,128)(2,1)S(1)} %get-tuple-element.7), channel_id=1, source_target_pairs={{0,17},{1,18},{2,19},{3,20},{4,21},{5,22},{6,23},{7,24},{8,25},{9,... | collective-permute-start | bytes 1769480 | tf_op jit(solution)/shard_map/ppermute | solution.py:28
  6.6 18.5 %collective-permute-start.2 = (bf16[3,3,128,256]{3,2,1,0:T(8,128)(2,1)S(1)}, bf16[3,3,128,256]{3,2,1,0:T(8,128)(2,1)S(1)}, u32[]{:S(2)}, u32[]{:S(2)}) collective-permute-start(bf16[3,3,128,256]{3,2,1,0:T(8,128)(2,1)S(1)} %get-tuple-element.9), channel_id=1, source_target_pairs={{1,16},{2,17},{3,18},{4,19},{5,20},{6,21},{7,22},{8,23},{9,24},{10... | collective-permute-start | bytes 1769480 | tf_op jit(solution)/shard_map/ppermute | solution.py:28
  12.7 13.7 %copy-start.4 = (f32[7]{0:T(128)S(1)}, f32[7]{0:T(128)}, u32[]{:S(2)}) copy-start(f32[7]{0:T(128)} %param.7) | copy-start | bytes 88
  12.7 13.7 %copy-start.5 = (f32[7]{0:T(128)S(1)}, f32[7]{0:T(128)}, u32[]{:S(2)}) copy-start(f32[7]{0:T(128)} %param.8) | copy-start | bytes 88
  12.7 14.1 %copy-start.6 = (bf16[32]{0:T(256)(128)(2,1)S(1)}, bf16[32]{0:T(256)(128)(2,1)}, u32[]{:S(2)}) copy-start(bf16[32]{0:T(256)(128)(2,1)} %param.9) | copy-start | bytes 196
  12.7 73.8 %collective-permute-start.1 = (bf16[3,8,128,256]{3,2,1,0:T(8,128)(2,1)}, bf16[3,8,128,256]{3,2,1,0:T(8,128)(2,1)S(1)}, u32[]{:S(2)}, u32[]{:S(2)}) collective-permute-start(bf16[3,8,128,256]{3,2,1,0:T(8,128)(2,1)} %get-tuple-element.11), channel_id=1, source_target_pairs={{0,16},{16,32},{32,48},{48,64},{64,80},{80,96},{96,112},{112,128},... | collective-permute-start | bytes 4718600 | tf_op jit(solution)/shard_map/ppermute | solution.py:19
  16.7 69.8 %collective-permute-start.3 = (bf16[8,3,128,256]{3,2,1,0:T(8,128)(2,1)}, bf16[8,3,128,256]{3,2,1,0:T(8,128)(2,1)}, u32[]{:S(2)}, u32[]{:S(2)}) collective-permute-start(bf16[8,3,128,256]{3,2,1,0:T(8,128)(2,1)} %get-tuple-element.13), channel_id=1, source_target_pairs={{0,1},{1,2},{2,3},{3,4},{4,5},{5,6},{6,7},{7,8},{8,9},{9,10},{10,1... | collective-permute-start | bytes 4718600 | tf_op jit(solution)/shard_map/ppermute | solution.py:19
  20.1 66.5 %collective-permute-start.4 = (bf16[8,3,128,256]{3,2,1,0:T(8,128)(2,1)}, bf16[8,3,128,256]{3,2,1,0:T(8,128)(2,1)}, u32[]{:S(2)}, u32[]{:S(2)}) collective-permute-start(bf16[8,3,128,256]{3,2,1,0:T(8,128)(2,1)} %get-tuple-element.14), channel_id=1, source_target_pairs={{1,0},{2,1},{3,2},{4,3},{5,4},{6,5},{7,6},{8,7},{9,8},{10,9},{11,1... | collective-permute-start | bytes 4718600 | tf_op jit(solution)/shard_map/ppermute | solution.py:19
  23.8 62.8 %collective-permute-start.6 = (bf16[3,8,128,256]{3,2,1,0:T(8,128)(2,1)}, bf16[3,8,128,256]{3,2,1,0:T(8,128)(2,1)}, u32[]{:S(2)}, u32[]{:S(2)}) collective-permute-start(bf16[3,8,128,256]{3,2,1,0:T(8,128)(2,1)} %get-tuple-element.12), channel_id=1, source_target_pairs={{16,0},{32,16},{48,32},{64,48},{80,64},{96,80},{112,96},{128,112},... | collective-permute-start | bytes 4718600 | tf_op jit(solution)/shard_map/ppermute | solution.py:19
  25.1 43.7 %collective-permute-start.5 = (bf16[3,3,128,256]{3,2,1,0:T(8,128)(2,1)}, bf16[3,3,128,256]{3,2,1,0:T(8,128)(2,1)}, u32[]{:S(2)}, u32[]{:S(2)}) collective-permute-start(bf16[3,3,128,256]{3,2,1,0:T(8,128)(2,1)} %get-tuple-element.8), channel_id=1, source_target_pairs={{16,1},{17,2},{18,3},{19,4},{20,5},{21,6},{22,7},{23,8},{24,9},{25... | collective-permute-start | bytes 1769480 | tf_op jit(solution)/shard_map/ppermute | solution.py:28
  68.8 17.7 %collective-permute-start.7 = (bf16[3,3,128,256]{3,2,1,0:T(8,128)(2,1)}, bf16[3,3,128,256]{3,2,1,0:T(8,128)(2,1)S(1)}, u32[]{:S(2)}, u32[]{:S(2)}) collective-permute-start(bf16[3,3,128,256]{3,2,1,0:T(8,128)(2,1)} %get-tuple-element.10), channel_id=1, source_target_pairs={{17,0},{18,1},{19,2},{20,3},{21,4},{22,5},{23,6},{24,7},{25,8},{26... | collective-permute-start | bytes 1769480 | tf_op jit(solution)/shard_map/ppermute | solution.py:28
  144.7 2.0 copy-start
  148.0 1.4 collective-permute-start.8
  149.4 6.0 %collective-permute-start.9 = (f32[257,128]{1,0:T(8,128)S(1)}, f32[257,128]{1,0:T(8,128)S(1)}, u32[]{:S(2)}, u32[]{:S(2)}) collective-permute-start(f32[257,128]{1,0:T(8,128)S(1)} %fusion.65), channel_id=1, source_target_pairs={{0,32},{16,48},{32,0},{48,16},{64,96},{80,112},{96,64},{112,80},{1... | collective-permute-start | bytes 394760 | tf_op jit(solution)/shard_map/ppermute | solution.py:81
  155.4 10.8 %collective-permute-start.10 = (f32[257,128]{1,0:T(8,128)S(1)}, f32[257,128]{1,0:T(8,128)S(1)}, u32[]{:S(2)}, u32[]{:S(2)}) collective-permute-start(f32[257,128]{1,0:T(8,128)S(1)} %add.45), channel_id=1, source_target_pairs={{0,64},{16,80},{32,96},{48,112},{64,0},{80,16},{96,32},{112,48},{1... | collective-permute-start | bytes 394760 | tf_op jit(solution)/shard_map/ppermute | solution.py:81
  166.2 11.5 %collective-permute-start.11 = (f32[257,128]{1,0:T(8,128)S(1)}, f32[257,128]{1,0:T(8,128)S(1)}, u32[]{:S(2)}, u32[]{:S(2)}) collective-permute-start(f32[257,128]{1,0:T(8,128)S(1)} %add.46), channel_id=1, source_target_pairs={{0,128},{16,144},{32,160},{48,176},{64,192},{80,208},{96,224},{112... | collective-permute-start | bytes 394760 | tf_op jit(solution)/shard_map/ppermute | solution.py:81
  177.8 5.3 %collective-permute-start.12 = (f32[257,128]{1,0:T(8,128)S(1)}, f32[257,128]{1,0:T(8,128)S(1)}, u32[]{:S(2)}, u32[]{:S(2)}) collective-permute-start(f32[257,128]{1,0:T(8,128)S(1)} %add.47), channel_id=1, source_target_pairs={{0,1},{1,0},{2,3},{3,2},{4,5},{5,4},{6,7},{7,6},{8,9},{9,8},{10,11... | collective-permute-start | bytes 394760 | tf_op jit(solution)/shard_map/ppermute | solution.py:81
  183.1 8.3 %collective-permute-start.13 = (f32[257,128]{1,0:T(8,128)S(1)}, f32[257,128]{1,0:T(8,128)S(1)}, u32[]{:S(2)}, u32[]{:S(2)}) collective-permute-start(f32[257,128]{1,0:T(8,128)S(1)} %add.48), channel_id=1, source_target_pairs={{0,2},{1,3},{2,0},{3,1},{4,6},{5,7},{6,4},{7,5},{8,10},{9,11},{10,... | collective-permute-start | bytes 394760 | tf_op jit(solution)/shard_map/ppermute | solution.py:81
  191.4 5.8 %collective-permute-start.14 = (f32[257,128]{1,0:T(8,128)S(1)}, f32[257,128]{1,0:T(8,128)S(1)}, u32[]{:S(2)}, u32[]{:S(2)}) collective-permute-start(f32[257,128]{1,0:T(8,128)S(1)} %add.49), channel_id=1, source_target_pairs={{0,4},{1,5},{2,6},{3,7},{4,0},{5,1},{6,2},{7,3},{8,12},{9,13},{10,... | collective-permute-start | bytes 394760 | tf_op jit(solution)/shard_map/ppermute | solution.py:81
  197.2 6.6 %collective-permute-start.15 = (f32[257,128]{1,0:T(8,128)S(1)}, f32[257,128]{1,0:T(8,128)S(1)}, u32[]{:S(2)}, u32[]{:S(2)}) collective-permute-start(f32[257,128]{1,0:T(8,128)S(1)} %add.50), channel_id=1, source_target_pairs={{0,8},{1,9},{2,10},{3,11},{4,12},{5,13},{6,14},{7,15},{8,0},{9,1},... | collective-permute-start | bytes 394760 | tf_op jit(solution)/shard_map/ppermute | solution.py:81
  220.5 3.5 %copy-start.1 = (bf16[8192,256]{1,0:T(8,128)(2,1)S(1)}, bf16[8192,256]{1,0:T(8,128)(2,1)}, u32[]{:S(2)}) copy-start(bf16[8192,256]{1,0:T(8,128)(2,1)} %copy-done) | copy-start | bytes 12582916
  224.0 3.9 %copy-start.3 = (f32[256,256]{1,0:T(8,128)}, f32[256,256]{1,0:T(8,128)S(1)}, u32[]{:S(2)}) copy-start(f32[256,256]{1,0:T(8,128)S(1)} %fusion.16) | copy-start | bytes 786436

commit v3 on v1

--- a/solution.py
+++ b/solution.py
@@ -4,17 +4,30 @@
 from jax.sharding import PartitionSpec as P
 
 
-def padded(block, sides, width):
-    for axis, dim in sides:
+def halo_pieces(block, width):
+    lat_size, elev_size = block.shape[0], block.shape[1]
+    low_lat = slice(lat_size - width, lat_size)
+    high_lat = slice(0, width)
+    low_elev = slice(elev_size - width, elev_size)
+    high_elev = slice(0, width)
+
+    def shift(piece, axis, step):
         count = lax.axis_size(axis)
-        forward = [(i, i + 1) for i in range(count - 1)]
-        backward = [(target, source) for source, target in forward]
-        low = lax.ppermute(
-            lax.slice_in_dim(block, block.shape[dim] - width, None, axis=dim), axis, forward
-        )
-        high = lax.ppermute(lax.slice_in_dim(block, 0, width, axis=dim), axis, backward)
-        block = jnp.concatenate([low, block, high], axis=dim)
-    return block
+        pairs = [(i, i + step) for i in range(count) if 0 <= i + step < count]
+        return lax.ppermute(piece, axis, pairs)
+
+    north = shift(block[low_lat], "lat", 1)
+    south = shift(block[high_lat], "lat", -1)
+    west = shift(block[:, low_elev], "elev", 1)
+    east = shift(block[:, high_elev], "elev", -1)
+    north_west = shift(west[low_lat], "lat", 1)
+    north_east = shift(east[low_lat], "lat", 1)
+    south_west = shift(west[high_lat], "lat", -1)
+    south_east = shift(east[high_lat], "lat", -1)
+    top = jnp.concatenate([north_west, north, north_east], axis=1)
+    middle = jnp.concatenate([west, block, east], axis=1)
+    bottom = jnp.concatenate([south_west, south, south_east], axis=1)
+    return jnp.concatenate([top, middle, bottom], axis=0)
 
 
 def time_matrix(time_taps, frames):
@@ -89,11 +102,14 @@
     shifted = gram_sum[None] + levels[:, None, None] * identity[None]
     scale = 2.0 / (2.0 * levels + total_trace)
     inverse = scale[:, None, None] * identity[None]
-    for _ in range(steps):
+
+    def refine(_, inverse):
         product = jnp.einsum("bij,bjk->bik", shifted, inverse, precision=lax.Precision.HIGHEST)
-        inverse = 2.0 * inverse - jnp.einsum(
+        return 2.0 * inverse - jnp.einsum(
             "bij,bjk->bik", inverse, product, precision=lax.Precision.HIGHEST
         )
+
+    inverse = lax.fori_loop(0, steps, refine, inverse)
     resolvents = levels[:, None, None] * inverse
     return resolvents[0] - resolvents[1]
 
@@ -101,7 +117,7 @@
 def body(volume, lat_taps, elev_taps, time_taps, clutter_rank, noise_rank):
     lat_count, elev_count, depth, columns = volume.shape
     matrix = time_matrix(time_taps, columns // 2)
-    extended = padded(volume, (("lat", 0), ("elev", 1)), 3)
+    extended = halo_pieces(volume, 3)
     row_block = filtered_rows(extended, lat_taps, elev_taps, matrix, lat_count, elev_count)
     local_gram = lax.dot_general(
         row_block, row_block, (((0,), (0,)), ((), ())), preferred_element_type=jnp.float32

time: 235 us -> 205 us (0.87)
  waiting for transfers between devices: 80.5 us -> 60.7 us
  starting transfers between devices: 61.6 us -> 49.1 us
  matrix products: 24.6 us -> 27.3 us
    ppermute x4 -> x8, waiting for transfers between devices: 48.5 us -> 27.5 us  [shift(): return lax.ppermute(piece, axis, pairs)]
    ppermute x8, starting transfers between devices: 52.4 us -> 32.6 us  [butterfly_sum(): block = block + lax.ppermute(block, axis, pairs)]
    ppermute x4 -> x8, starting transfers between devices: 9.13 us -> 16.4 us  [shift(): return lax.ppermute(piece, axis, pairs)]
    unnamed x19 -> x25, local copies, waits for them, and re-layouts: 5.65 us -> 4.25 us
    slice x2 -> x4, local copies, waits for them, and re-layouts: 5.06 us -> 6.27 us  [the longest x1 4.09 us: halo_pieces(): east = shift(block[:, high_elev], 'elev', -1)]
    concatenate x1 -> x2, other arithmetic: 11 us -> 10.7 us  [the longest x1 10 us: halo_pieces(): return jnp.concatenate([top, middle, bottom], axis=0)]
  transfers between devices with their start and end apart: 12 -> 16, of which waited for: 12 -> 11; matrix products, arithmetic and copies ran while one was open for 1% -> 3% of each run, Pallas kernels for 0% -> 0%
where the time goes in v3:
time: 205 us; the launch traced here: 203 us
  waiting for transfers between devices  60.7 us (30%)
  starting transfers between devices  49.1 us (24%)
  other arithmetic  49.1 us (24%)
  matrix products  27.3 us (13%)
  local copies, waits for them, and re-layouts  14.1 us (7%)
  between operations  2.4 us (1%)
    ppermute x8, waiting for transfers between devices, butterfly_sum(): block = block + lax.ppermute(block, axis, pairs)  33.3 us
    ppermute x8, starting transfers between devices, butterfly_sum(): block = block + lax.ppermute(block, axis, pairs)  32.6 us
    ppermute x8, waiting for transfers between devices, shift(): return lax.ppermute(piece, axis, pairs)  27.5 us
    add x1, other arithmetic, smooth(): lat_sum + lat_taps[index_tap] * extended[index_tap:index_tap + lat_count]...  24.9 us
    ppermute x8, starting transfers between devices, shift(): return lax.ppermute(piece, axis, pairs)  16.4 us
    convert_element_type x1, other arithmetic, filtered_rows(): smooth(extended, lat_taps, elev_taps, lat_count, elev_count)  11.3 us
    concatenate x1, other arithmetic, halo_pieces(): return jnp.concatenate([top, middle, bottom], axis=0)  10 us
    dot_general x13, matrix products, refine(): jnp.einsum('bij,bjk->bik', shifted, inverse, precision=lax.Precision.HIGH...  9.86 us
  transfers between devices with their start and end apart: 16, of which 11 were waited for; matrix products, arithmetic and copies ran while one was open for 3% of the time, Pallas kernels for 0%

profile of v3, /device:TPU:2, one launch (start us, length us, event | category | flops | bytes accessed | tf_op | source)
XLA Modules:
  0.0 203.1 jit_solution(15636224263014906604)
XLA Ops:
  0.7 4.1 %fusion.26 = (bf16[8,3,128,256]{3,2,1,0:T(8,128)(2,1)}, bf16[8,3,128,256]{3,2,1,0:T(8,128)(2,1)}) fusion(bf16[8,8,128,256]{3,2,1,0:T(8,128)(2,1)} %param.8), kind=kLoop, calls=%fused_computation.65 | loop fusion | bytes 6291456 | tf_op jit(solution)/shard_map/slice | solution.py:22
  4.8 3.4 %collective-permute-start = (bf16[8,3,128,256]{3,2,1,0:T(8,128)(2,1)}, bf16[8,3,128,256]{3,2,1,0:T(8,128)(2,1)S(1)}, u32[]{:S(2)}, u32[]{:S(2)}) collective-permute-start(bf16[8,3,128,256]{3,2,1,0:T(8,128)(2,1)} %get-tuple-element.68), channel_id=1, source_target_pairs={{0,1},{1,2},{2,3},{3,4},{4,5},{5,6},{6,7},{7,8},{8,9},{9,10},{10,1... | collective-permute-start | bytes 4718600 | tf_op jit(solution)/shard_map/ppermute | solution.py:17
  8.2 2.5 %collective-permute-start.3 = (bf16[8,3,128,256]{3,2,1,0:T(8,128)(2,1)}, bf16[8,3,128,256]{3,2,1,0:T(8,128)(2,1)S(1)}, u32[]{:S(2)}, u32[]{:S(2)}) collective-permute-start(bf16[8,3,128,256]{3,2,1,0:T(8,128)(2,1)} %get-tuple-element.67), channel_id=1, source_target_pairs={{1,0},{2,1},{3,2},{4,3},{5,4},{6,5},{7,6},{8,7},{9,8},{10,9},{11,1... | collective-permute-start | bytes 4718600 | tf_op jit(solution)/shard_map/ppermute | solution.py:17
  10.7 2.0 fusion.25
  12.7 2.4 %collective-permute-start.2 = (bf16[3,8,128,256]{3,2,1,0:T(8,128)(2,1)}, bf16[3,8,128,256]{3,2,1,0:T(8,128)(2,1)}, u32[]{:S(2)}, u32[]{:S(2)}) collective-permute-start(bf16[3,8,128,256]{3,2,1,0:T(8,128)(2,1)} %get-tuple-element.65), channel_id=1, source_target_pairs={{0,16},{16,32},{32,48},{48,64},{64,80},{80,96},{96,112},{112,128},... | collective-permute-start | bytes 4718600 | tf_op jit(solution)/shard_map/ppermute | solution.py:17
  18.9 24.1 %collective-permute-done = bf16[8,3,128,256]{3,2,1,0:T(8,128)(2,1)S(1)} collective-permute-done((bf16[8,3,128,256]{3,2,1,0:T(8,128)(2,1)}, bf16[8,3,128,256]{3,2,1,0:T(8,128)(2,1)S(1)}, u32[]{:S(2)}, u32[]{:S(2)}) %collective-permute-start) | collective-permute-done | bytes 1572896 | tf_op jit(solution)/shard_map/ppermute | solution.py:17
  43.1 1.3 collective-permute-start.1
  44.4 1.7 collective-permute-done.3
  46.2 2.9 %collective-permute-start.4 = (bf16[3,3,128,256]{3,2,1,0:T(8,128)(2,1)S(1)}, bf16[3,3,128,256]{3,2,1,0:T(8,128)(2,1)S(1)}, u32[]{:S(2)}, u32[]{:S(2)}) collective-permute-start(bf16[3,3,128,256]{3,2,1,0:T(8,128)(2,1)S(1)} %get-tuple-element.71), channel_id=1, source_target_pairs={{0,16},{16,32},{32,48},{48,64},{64,80},{80,96},{96,112},{112,128},... | collective-permute-start | bytes 1769480 | tf_op jit(solution)/shard_map/ppermute | solution.py:17
  50.4 1.3 collective-permute-start.7
  51.7 1.6 constant_dynamic-update-slice_fusion.2
  53.8 1.7 collective-permute-done.7
  55.5 10.0 %pad_maximum_fusion = (bf16[11,14,128,256]{3,2,1,0:T(8,128)(2,1)}, bf16[11,14,128,256]{3,2,1,0:T(8,128)(2,1)}) fusion(bf16[8,14,128,256]{3,2,1,0:T(8,128)(2,1)S(1)} %constant_dynamic-update-slice_fusion, bf16[3,3,128,256]{3,2,1,0:T(8,128)(2,1)S(1)} %collective-permute-done.4, bf16[3,8,128,256]{3,2,1,0:T(8,128)(2,1)} %collective-permute-done.2, ...), kind=kLoop, calls=%fused_computation.13 | loop fusion | flops 30277632 | bytes 33030144 | tf_op jit(solution)/shard_map/concatenate | solution.py:30
  65.5 24.9 %multiply_add_fusion = f32[8,14,128,256]{3,2,1,0:T(8,128)S(1)} fusion(bf16[8,14,128,256]{3,2,1,0:T(8,128)(2,1)S(1)} %constant_dynamic-update-slice_fusion, bf16[11,14,128,256]{3,2,1,0:T(8,128)(2,1)} %get-tuple-element.64, bf16[11,14,128,256]{3,2,1,0:T(8,128)(2,1)} %get-tuple-element.63, f32[]{:T(128)} %bitcast.7, f32[]{:T(128)} %bitcast.6, f32[]{:T(128)} %bitcast.5, ...), kind=kLoop, calls=%fused_computation.10 | loop fusion | flops 73400320 | bytes 66060316 | tf_op jit(solution)/shard_map/add | solution.py:49
  90.4 11.3 %fusion.10 = bf16[8,8,128,256]{3,2,1,0:T(8,128)(2,1)S(1)} fusion(f32[8,14,128,256]{3,2,1,0:T(8,128)S(1)} %multiply_add_fusion, f32[]{:T(128)} %bitcast.13, f32[]{:T(128)} %bitcast.12, f32[]{:T(128)} %bitcast.11, f32[]{:T(128)} %bitcast.10, f32[]{:T(128)} %bitcast.9, f32[]{:T(128)} %bitcast.8, f32[]{:T(128)} %bitcast), kind=kLoop, calls=%fused_computation.17 | loop fusion | flops 29360128 | bytes 62914588 | tf_op jit(solution)/shard_map/convert_element_type | solution.py:59
  103.0 2.0 copy-done
  107.6 12.3 %collective-permute-start.8 = (f32[257,128]{1,0:T(8,128)S(1)}, f32[257,128]{1,0:T(8,128)S(1)}, u32[]{:S(2)}, u32[]{:S(2)}) collective-permute-start(f32[257,128]{1,0:T(8,128)S(1)} %pad_maximum_fusion.1), channel_id=1, source_target_pairs={{0,16},{16,0},{32,48},{48,32},{64,80},{80,64},{96,112},{112,96},{1... | collective-permute-start | bytes 394760 | tf_op jit(solution)/shard_map/ppermute | solution.py:70
  120.9 2.2 %collective-permute-start.9 = (f32[257,128]{1,0:T(8,128)S(1)}, f32[257,128]{1,0:T(8,128)S(1)}, u32[]{:S(2)}, u32[]{:S(2)}) collective-permute-start(f32[257,128]{1,0:T(8,128)S(1)} %fusion.23), channel_id=1, source_target_pairs={{0,32},{16,48},{32,0},{48,16},{64,96},{80,112},{96,64},{112,80},{1... | collective-permute-start | bytes 394760 | tf_op jit(solution)/shard_map/ppermute | solution.py:70
  123.0 4.1 %collective-permute-done.9 = f32[257,128]{1,0:T(8,128)S(1)} collective-permute-done((f32[257,128]{1,0:T(8,128)S(1)}, f32[257,128]{1,0:T(8,128)S(1)}, u32[]{:S(2)}, u32[]{:S(2)}) %collective-permute-start.9) | collective-permute-done | bytes 131616 | tf_op jit(solution)/shard_map/ppermute | solution.py:70
  127.2 5.8 %collective-permute-start.10 = (f32[257,128]{1,0:T(8,128)S(1)}, f32[257,128]{1,0:T(8,128)S(1)}, u32[]{:S(2)}, u32[]{:S(2)}) collective-permute-start(f32[257,128]{1,0:T(8,128)S(1)} %add.96), channel_id=1, source_target_pairs={{0,64},{16,80},{32,96},{48,112},{64,0},{80,16},{96,32},{112,48},{1... | collective-permute-start | bytes 394760 | tf_op jit(solution)/shard_map/ppermute | solution.py:70
  132.9 6.4 %collective-permute-done.10 = f32[257,128]{1,0:T(8,128)S(1)} collective-permute-done((f32[257,128]{1,0:T(8,128)S(1)}, f32[257,128]{1,0:T(8,128)S(1)}, u32[]{:S(2)}, u32[]{:S(2)}) %collective-permute-start.10) | collective-permute-done | bytes 131616 | tf_op jit(solution)/shard_map/ppermute | solution.py:70
  139.4 2.7 %collective-permute-start.11 = (f32[257,128]{1,0:T(8,128)S(1)}, f32[257,128]{1,0:T(8,128)S(1)}, u32[]{:S(2)}, u32[]{:S(2)}) collective-permute-start(f32[257,128]{1,0:T(8,128)S(1)} %add.97), channel_id=1, source_target_pairs={{0,128},{16,144},{32,160},{48,176},{64,192},{80,208},{96,224},{112... | collective-permute-start | bytes 394760 | tf_op jit(solution)/shard_map/ppermute | solution.py:70
  142.1 8.3 %collective-permute-done.11 = f32[257,128]{1,0:T(8,128)S(1)} collective-permute-done((f32[257,128]{1,0:T(8,128)S(1)}, f32[257,128]{1,0:T(8,128)S(1)}, u32[]{:S(2)}, u32[]{:S(2)}) %collective-permute-start.11) | collective-permute-done | bytes 131616 | tf_op jit(solution)/shard_map/ppermute | solution.py:70
  151.2 4.9 %collective-permute-done.12 = f32[257,128]{1,0:T(8,128)S(1)} collective-permute-done((f32[257,128]{1,0:T(8,128)S(1)}, f32[257,128]{1,0:T(8,128)S(1)}, u32[]{:S(2)}, u32[]{:S(2)}) %collective-permute-start.12) | collective-permute-done | bytes 131616 | tf_op jit(solution)/shard_map/ppermute | solution.py:70
  156.1 4.3 %collective-permute-start.13 = (f32[257,128]{1,0:T(8,128)S(1)}, f32[257,128]{1,0:T(8,128)S(1)}, u32[]{:S(2)}, u32[]{:S(2)}) collective-permute-start(f32[257,128]{1,0:T(8,128)S(1)} %add.99), channel_id=1, source_target_pairs={{0,2},{1,3},{2,0},{3,1},{4,6},{5,7},{6,4},{7,5},{8,10},{9,11},{10,... | collective-permute-start | bytes 394760 | tf_op jit(solution)/shard_map/ppermute | solution.py:70
  160.4 3.0 %collective-permute-done.13 = f32[257,128]{1,0:T(8,128)S(1)} collective-permute-done((f32[257,128]{1,0:T(8,128)S(1)}, f32[257,128]{1,0:T(8,128)S(1)}, u32[]{:S(2)}, u32[]{:S(2)}) %collective-permute-start.13) | collective-permute-done | bytes 131616 | tf_op jit(solution)/shard_map/ppermute | solution.py:70
  163.4 1.7 collective-permute-start.14
  165.1 3.4 %collective-permute-done.14 = f32[257,128]{1,0:T(8,128)S(1)} collective-permute-done((f32[257,128]{1,0:T(8,128)S(1)}, f32[257,128]{1,0:T(8,128)S(1)}, u32[]{:S(2)}, u32[]{:S(2)}) %collective-permute-start.14) | collective-permute-done | bytes 131616 | tf_op jit(solution)/shard_map/ppermute | solution.py:70
  168.5 3.0 %collective-permute-start.15 = (f32[257,128]{1,0:T(8,128)S(1)}, f32[257,128]{1,0:T(8,128)S(1)}, u32[]{:S(2)}, u32[]{:S(2)}) collective-permute-start(f32[257,128]{1,0:T(8,128)S(1)} %add.101), channel_id=1, source_target_pairs={{0,8},{1,9},{2,10},{3,11},{4,12},{5,13},{6,14},{7,15},{8,0},{9,1},... | collective-permute-start | bytes 394760 | tf_op jit(solution)/shard_map/ppermute | solution.py:70
  173.0 2.1 %collective-permute-done.15 = f32[257,128]{1,0:T(8,128)S(1)} collective-permute-done((f32[257,128]{1,0:T(8,128)S(1)}, f32[257,128]{1,0:T(8,128)S(1)}, u32[]{:S(2)}, u32[]{:S(2)}) %collective-permute-start.15) | collective-permute-done | bytes 131616 | tf_op jit(solution)/shard_map/ppermute | solution.py:70
  177.1 19.5 %while.11 = (s32[]{:T(128)}, f32[2,256,256]{1,2,0:T(8,128)S(1)}, f32[256,256]{1,0:T(8,128)S(1)}, f32[2]{0:T(128)S(1)}, f32[256,256]{1,0:T(8,128)S(1)}, /*index=5*/s32[]{:T(128)}) while((s32[]{:T(128)}, f32[2,256,256]{1,2,0:T(8,128)S(1)}, f32[256,256]{1,0:T(8,128)S(1)}, f32[2]{0:T(128)S(1)}, f32[256,256]{1,0:T(8,128)S(1)}, ...), condition=%wide.region_3.4_spmd.clone, body=%wide.region_2.3_spmd.clone.sunk | while | flops 805830656 | bytes 4194381 | solution.py:112
  197.0 6.2 %multiply_reduce_fusion = (f32[8192]{0:T(1024)}, bf16[8192,256]{1,0:T(8,128)(2,1)}) fusion(bf16[8192,256]{1,0:T(8,128)(2,1)} %copy-done, f32[256,256]{1,0:T(8,128)S(1)} %fusion.16), kind=kOutput, calls=%fused_computation.29 | convolution fusion | flops 1082187776 | bytes 8683520 | tf_op jit(solution)/shard_map/dot_general | solution.py:127
  (108 shorter events, 32.6 us)
Async XLA Ops:
  0.6 10.1 %copy-start.1 = (bf16[8,8,128,256]{3,2,1,0:T(8,128)(2,1)S(1)}, bf16[8,8,128,256]{3,2,1,0:T(8,128)(2,1)}, u32[]{:S(2)}) copy-start(bf16[8,8,128,256]{3,2,1,0:T(8,128)(2,1)} %param.8) | copy-start | bytes 12582916
  0.6 15.8 %copy-start.7 = (f32[7]{0:T(128)S(1)}, f32[7]{0:T(128)}, u32[]{:S(2)}) copy-start(f32[7]{0:T(128)} %param.9) | copy-start | bytes 88
  0.7 16.5 %copy-start.8 = (f32[7]{0:T(128)S(1)}, f32[7]{0:T(128)}, u32[]{:S(2)}) copy-start(f32[7]{0:T(128)} %param.10) | copy-start | bytes 88
  0.7 17.2 %copy-start.9 = (bf16[32]{0:T(256)(128)(2,1)S(1)}, bf16[32]{0:T(256)(128)(2,1)}, u32[]{:S(2)}) copy-start(bf16[32]{0:T(256)(128)(2,1)} %param.11) | copy-start | bytes 196
  4.8 38.2 %collective-permute-start = (bf16[8,3,128,256]{3,2,1,0:T(8,128)(2,1)}, bf16[8,3,128,256]{3,2,1,0:T(8,128)(2,1)S(1)}, u32[]{:S(2)}, u32[]{:S(2)}) collective-permute-start(bf16[8,3,128,256]{3,2,1,0:T(8,128)(2,1)} %get-tuple-element.68), channel_id=1, source_target_pairs={{0,1},{1,2},{2,3},{3,4},{4,5},{5,6},{6,7},{7,8},{8,9},{9,10},{10,1... | collective-permute-start | bytes 4718600 | tf_op jit(solution)/shard_map/ppermute | solution.py:17
  8.2 38.0 %collective-permute-start.3 = (bf16[8,3,128,256]{3,2,1,0:T(8,128)(2,1)}, bf16[8,3,128,256]{3,2,1,0:T(8,128)(2,1)S(1)}, u32[]{:S(2)}, u32[]{:S(2)}) collective-permute-start(bf16[8,3,128,256]{3,2,1,0:T(8,128)(2,1)} %get-tuple-element.67), channel_id=1, source_target_pairs={{1,0},{2,1},{3,2},{4,3},{5,4},{6,5},{7,6},{8,7},{9,8},{10,9},{11,1... | collective-permute-start | bytes 4718600 | tf_op jit(solution)/shard_map/ppermute | solution.py:17
  12.7 37.7 %collective-permute-start.2 = (bf16[3,8,128,256]{3,2,1,0:T(8,128)(2,1)}, bf16[3,8,128,256]{3,2,1,0:T(8,128)(2,1)}, u32[]{:S(2)}, u32[]{:S(2)}) collective-permute-start(bf16[3,8,128,256]{3,2,1,0:T(8,128)(2,1)} %get-tuple-element.65), channel_id=1, source_target_pairs={{0,16},{16,32},{32,48},{48,64},{64,80},{80,96},{96,112},{112,128},... | collective-permute-start | bytes 4718600 | tf_op jit(solution)/shard_map/ppermute | solution.py:17
  15.2 38.6 %collective-permute-start.6 = (bf16[3,8,128,256]{3,2,1,0:T(8,128)(2,1)}, bf16[3,8,128,256]{3,2,1,0:T(8,128)(2,1)}, u32[]{:S(2)}, u32[]{:S(2)}) collective-permute-start(bf16[3,8,128,256]{3,2,1,0:T(8,128)(2,1)} %get-tuple-element.66), channel_id=1, source_target_pairs={{16,0},{32,16},{48,32},{64,48},{80,64},{96,80},{112,96},{128,112},... | collective-permute-start | bytes 4718600 | tf_op jit(solution)/shard_map/ppermute | solution.py:17
  18.0 35.3 %copy-start.2 = (bf16[8,8,128,256]{3,2,1,0:T(8,128)(2,1)S(1)}, bf16[8,8,128,256]{3,2,1,0:T(8,128)(2,1)}, u32[]{:S(2)}) copy-start(bf16[8,8,128,256]{3,2,1,0:T(8,128)(2,1)} %param.8) | copy-start | bytes 12582916
  43.0 8.7 %copy-start.3 = (bf16[8,3,128,256]{3,2,1,0:T(8,128)(2,1)}, bf16[8,3,128,256]{3,2,1,0:T(8,128)(2,1)S(1)}, u32[]{:S(2)}) copy-start(bf16[8,3,128,256]{3,2,1,0:T(8,128)(2,1)S(1)} %collective-permute-done) | copy-start | bytes 4718596
  43.1 10.7 %collective-permute-start.1 = (bf16[3,3,128,256]{3,2,1,0:T(8,128)(2,1)S(1)}, bf16[3,3,128,256]{3,2,1,0:T(8,128)(2,1)S(1)}, u32[]{:S(2)}, u32[]{:S(2)}) collective-permute-start(bf16[3,3,128,256]{3,2,1,0:T(8,128)(2,1)S(1)} %get-tuple-element.69), channel_id=1, source_target_pairs={{0,16},{16,32},{32,48},{48,64},{64,80},{80,96},{96,112},{112,128},... | collective-permute-start | bytes 1769480 | tf_op jit(solution)/shard_map/ppermute | solution.py:17
  46.1 4.3 %copy-start.4 = (bf16[8,3,128,256]{3,2,1,0:T(8,128)(2,1)}, bf16[8,3,128,256]{3,2,1,0:T(8,128)(2,1)S(1)}, u32[]{:S(2)}) copy-start(bf16[8,3,128,256]{3,2,1,0:T(8,128)(2,1)S(1)} %collective-permute-done.3) | copy-start | bytes 4718596
  46.2 7.6 %collective-permute-start.4 = (bf16[3,3,128,256]{3,2,1,0:T(8,128)(2,1)S(1)}, bf16[3,3,128,256]{3,2,1,0:T(8,128)(2,1)S(1)}, u32[]{:S(2)}, u32[]{:S(2)}) collective-permute-start(bf16[3,3,128,256]{3,2,1,0:T(8,128)(2,1)S(1)} %get-tuple-element.71), channel_id=1, source_target_pairs={{0,16},{16,32},{32,48},{48,64},{64,80},{80,96},{96,112},{112,128},... | collective-permute-start | bytes 1769480 | tf_op jit(solution)/shard_map/ppermute | solution.py:17
  49.1 4.7 %collective-permute-start.5 = (bf16[3,3,128,256]{3,2,1,0:T(8,128)(2,1)S(1)}, bf16[3,3,128,256]{3,2,1,0:T(8,128)(2,1)S(1)}, u32[]{:S(2)}, u32[]{:S(2)}) collective-permute-start(bf16[3,3,128,256]{3,2,1,0:T(8,128)(2,1)S(1)} %get-tuple-element.70), channel_id=1, source_target_pairs={{16,0},{32,16},{48,32},{64,48},{80,64},{96,80},{112,96},{128,112},... | collective-permute-start | bytes 1769480 | tf_op jit(solution)/shard_map/ppermute | solution.py:17
  50.4 5.1 %collective-permute-start.7 = (bf16[3,3,128,256]{3,2,1,0:T(8,128)(2,1)S(1)}, bf16[3,3,128,256]{3,2,1,0:T(8,128)(2,1)S(1)}, u32[]{:S(2)}, u32[]{:S(2)}) collective-permute-start(bf16[3,3,128,256]{3,2,1,0:T(8,128)(2,1)S(1)} %get-tuple-element.72), channel_id=1, source_target_pairs={{16,0},{32,16},{48,32},{64,48},{80,64},{96,80},{112,96},{128,112},... | collective-permute-start | bytes 1769480 | tf_op jit(solution)/shard_map/ppermute | solution.py:17
  51.7 2.0 copy-start.5
  103.0 2.0 copy-start
  107.6 13.3 %collective-permute-start.8 = (f32[257,128]{1,0:T(8,128)S(1)}, f32[257,128]{1,0:T(8,128)S(1)}, u32[]{:S(2)}, u32[]{:S(2)}) collective-permute-start(f32[257,128]{1,0:T(8,128)S(1)} %pad_maximum_fusion.1), channel_id=1, source_target_pairs={{0,16},{16,0},{32,48},{48,32},{64,80},{80,64},{96,112},{112,96},{1... | collective-permute-start | bytes 394760 | tf_op jit(solution)/shard_map/ppermute | solution.py:70
  120.9 6.3 %collective-permute-start.9 = (f32[257,128]{1,0:T(8,128)S(1)}, f32[257,128]{1,0:T(8,128)S(1)}, u32[]{:S(2)}, u32[]{:S(2)}) collective-permute-start(f32[257,128]{1,0:T(8,128)S(1)} %fusion.23), channel_id=1, source_target_pairs={{0,32},{16,48},{32,0},{48,16},{64,96},{80,112},{96,64},{112,80},{1... | collective-permute-start | bytes 394760 | tf_op jit(solution)/shard_map/ppermute | solution.py:70
  127.2 12.2 %collective-permute-start.10 = (f32[257,128]{1,0:T(8,128)S(1)}, f32[257,128]{1,0:T(8,128)S(1)}, u32[]{:S(2)}, u32[]{:S(2)}) collective-permute-start(f32[257,128]{1,0:T(8,128)S(1)} %add.96), channel_id=1, source_target_pairs={{0,64},{16,80},{32,96},{48,112},{64,0},{80,16},{96,32},{112,48},{1... | collective-permute-start | bytes 394760 | tf_op jit(solution)/shard_map/ppermute | solution.py:70
  139.4 11.1 %collective-permute-start.11 = (f32[257,128]{1,0:T(8,128)S(1)}, f32[257,128]{1,0:T(8,128)S(1)}, u32[]{:S(2)}, u32[]{:S(2)}) collective-permute-start(f32[257,128]{1,0:T(8,128)S(1)} %add.97), channel_id=1, source_target_pairs={{0,128},{16,144},{32,160},{48,176},{64,192},{80,208},{96,224},{112... | collective-permute-start | bytes 394760 | tf_op jit(solution)/shard_map/ppermute | solution.py:70
  150.5 5.6 %collective-permute-start.12 = (f32[257,128]{1,0:T(8,128)S(1)}, f32[257,128]{1,0:T(8,128)S(1)}, u32[]{:S(2)}, u32[]{:S(2)}) collective-permute-start(f32[257,128]{1,0:T(8,128)S(1)} %add.98), channel_id=1, source_target_pairs={{0,1},{1,0},{2,3},{3,2},{4,5},{5,4},{6,7},{7,6},{8,9},{9,8},{10,11... | collective-permute-start | bytes 394760 | tf_op jit(solution)/shard_map/ppermute | solution.py:70
  156.1 7.3 %collective-permute-start.13 = (f32[257,128]{1,0:T(8,128)S(1)}, f32[257,128]{1,0:T(8,128)S(1)}, u32[]{:S(2)}, u32[]{:S(2)}) collective-permute-start(f32[257,128]{1,0:T(8,128)S(1)} %add.99), channel_id=1, source_target_pairs={{0,2},{1,3},{2,0},{3,1},{4,6},{5,7},{6,4},{7,5},{8,10},{9,11},{10,... | collective-permute-start | bytes 394760 | tf_op jit(solution)/shard_map/ppermute | solution.py:70
  163.4 5.1 %collective-permute-start.14 = (f32[257,128]{1,0:T(8,128)S(1)}, f32[257,128]{1,0:T(8,128)S(1)}, u32[]{:S(2)}, u32[]{:S(2)}) collective-permute-start(f32[257,128]{1,0:T(8,128)S(1)} %add.100), channel_id=1, source_target_pairs={{0,4},{1,5},{2,6},{3,7},{4,0},{5,1},{6,2},{7,3},{8,12},{9,13},{10,... | collective-permute-start | bytes 394760 | tf_op jit(solution)/shard_map/ppermute | solution.py:70
  168.5 6.6 %collective-permute-start.15 = (f32[257,128]{1,0:T(8,128)S(1)}, f32[257,128]{1,0:T(8,128)S(1)}, u32[]{:S(2)}, u32[]{:S(2)}) collective-permute-start(f32[257,128]{1,0:T(8,128)S(1)} %add.101), channel_id=1, source_target_pairs={{0,8},{1,9},{2,10},{3,11},{4,12},{5,13},{6,14},{7,15},{8,0},{9,1},... | collective-permute-start | bytes 394760 | tf_op jit(solution)/shard_map/ppermute | solution.py:70
  197.0 6.2 %copy-start.6 = (f32[256,256]{1,0:T(8,128)}, f32[256,256]{1,0:T(8,128)S(1)}, u32[]{:S(2)}) copy-start(f32[256,256]{1,0:T(8,128)S(1)} %fusion.16) | copy-start | bytes 786436

commit v4 on v3

--- a/solution.py
+++ b/solution.py
@@ -24,10 +24,10 @@
     north_east = shift(east[low_lat], "lat", 1)
     south_west = shift(west[high_lat], "lat", -1)
     south_east = shift(east[high_lat], "lat", -1)
-    top = jnp.concatenate([north_west, north, north_east], axis=1)
-    middle = jnp.concatenate([west, block, east], axis=1)
-    bottom = jnp.concatenate([south_west, south, south_east], axis=1)
-    return jnp.concatenate([top, middle, bottom], axis=0)
+    center = jnp.concatenate([north, block, south], axis=0)
+    left = jnp.concatenate([north_west, west, south_west], axis=0)
+    right = jnp.concatenate([north_east, east, south_east], axis=0)
+    return left, center, right
 
 
 def time_matrix(time_taps, frames):
@@ -43,20 +43,29 @@
     return paired.astype(jnp.bfloat16)
 
 
-def smooth(extended, lat_taps, elev_taps, lat_count, elev_count):
+def lat_pass(extended, lat_taps, lat_count):
     lat_sum = lat_taps[0] * extended[0:lat_count].astype(jnp.float32)
     for index_tap in range(1, 7):
         lat_sum = lat_sum + lat_taps[index_tap] * extended[
             index_tap : index_tap + lat_count
         ].astype(jnp.float32)
+    return lat_sum
+
+
+def smooth(pieces, lat_taps, elev_taps, lat_count, elev_count):
+    left, center, right = pieces
+    middle = lat_pass(center, lat_taps, lat_count)
+    lat_sum = jnp.concatenate(
+        [lat_pass(left, lat_taps, lat_count), middle, lat_pass(right, lat_taps, lat_count)], axis=1
+    )
     result = elev_taps[0] * lat_sum[:, 0:elev_count]
     for index_tap in range(1, 7):
         result = result + elev_taps[index_tap] * lat_sum[:, index_tap : index_tap + elev_count]
     return result
 
 
-def filtered_rows(extended, lat_taps, elev_taps, matrix, lat_count, elev_count):
-    smoothed = smooth(extended, lat_taps, elev_taps, lat_count, elev_count).astype(jnp.bfloat16)
+def filtered_rows(pieces, lat_taps, elev_taps, matrix, lat_count, elev_count):
+    smoothed = smooth(pieces, lat_taps, elev_taps, lat_count, elev_count).astype(jnp.bfloat16)
     flat_rows = smoothed.reshape(-1, matrix.shape[0])
     return jnp.dot(flat_rows, matrix, preferred_element_type=jnp.float32).astype(jnp.bfloat16)
 

time: 205 us -> 202 us (0.985)
  local copies, waits for them, and re-layouts: 14.1 us -> 22.3 us
  other arithmetic: 49.1 us -> 44.5 us
  starting transfers between devices: 49.1 us -> 45 us
  waiting for transfers between devices: 60.7 us -> 56.7 us
  matrix products: 27.3 us -> 29.5 us
    concatenate x1 -> x0, other arithmetic: 10 us -> none  [halo_pieces(): return jnp.concatenate([top, middle, bottom], axis=0)]
    ppermute x8, starting transfers between devices: 32.6 us -> 24.7 us  [butterfly_sum(): block = block + lax.ppermute(block, axis, pairs)]
    concatenate x1 -> x6, local copies, waits for them, and re-layouts: 0.1 us -> 5.7 us  [the longest x2 2.58 us: halo_pieces(): center = jnp.concatenate([north, block, south], axis=0)]
    ppermute x8, starting transfers between devices: 16.4 us -> 20.2 us  [shift(): return lax.ppermute(piece, axis, pairs)]
    ppermute x8, waiting for transfers between devices: 27.5 us -> 23.9 us  [shift(): return lax.ppermute(piece, axis, pairs)]
    convert_element_type x1, other arithmetic: 11.3 us -> 14.6 us  [filtered_rows(): smooth(pieces, lat_taps, elev_taps, lat_count, elev_count)]
    dot_general x1, matrix products: 1.26 us -> 3.44 us  [filtered_rows(): jnp.dot(flat_rows, matrix, preferred_element_type=jnp.float32)]
    add x1 -> x3, other arithmetic: 24.9 us -> 27 us  [lat_pass(): lat_sum + lat_taps[index_tap] * extended[index_tap:index_tap + lat_count]...]
  transfers between devices with their start and end apart: 16 -> 16, of which waited for: 11 -> 9; matrix products, arithmetic and copies ran while one was open for 3% -> 17% of each run, Pallas kernels for 0% -> 0%
where the time goes in v4:
time: 202 us; the launch traced here: 201 us
  waiting for transfers between devices  56.7 us (28%)
  starting transfers between devices  45 us (22%)
  other arithmetic  44.5 us (22%)
  matrix products  29.5 us (15%)
  local copies, waits for them, and re-layouts  22.3 us (11%)
  between operations  2.38 us (1%)
    ppermute x8, waiting for transfers between devices, butterfly_sum(): block = block + lax.ppermute(block, axis, pairs)  32.9 us
    add x3, other arithmetic, lat_pass(): lat_sum + lat_taps[index_tap] * extended[index_tap:index_tap + lat_count]...  27 us
    ppermute x8, starting transfers between devices, butterfly_sum(): block = block + lax.ppermute(block, axis, pairs)  24.7 us
    ppermute x8, waiting for transfers between devices, shift(): return lax.ppermute(piece, axis, pairs)  23.9 us
    ppermute x8, starting transfers between devices, shift(): return lax.ppermute(piece, axis, pairs)  20.2 us
    convert_element_type x1, other arithmetic, filtered_rows(): smooth(pieces, lat_taps, elev_taps, lat_count, elev_count)  14.6 us
    dot_general x13, matrix products, refine(): jnp.einsum('bij,bjk->bik', shifted, inverse, precision=lax.Precision.HIGH...  9.86 us
    dot_general x13, matrix products, refine(): jnp.einsum('bij,bjk->bik', inverse, product, precision=lax.Precision.HIGH...  8.7 us
  transfers between devices with their start and end apart: 16, of which 9 were waited for; matrix products, arithmetic and copies ran while one was open for 17% of the time, Pallas kernels for 0%

profile of v4, /device:TPU:2, one launch (start us, length us, event | category | flops | bytes accessed | tf_op | source)
XLA Modules:
  0.0 200.7 jit_solution(2871830964668729398)
XLA Ops:
  0.6 4.0 %fusion.35 = (bf16[8,3,128,256]{3,2,1,0:T(8,128)(2,1)}, bf16[8,3,128,256]{3,2,1,0:T(8,128)(2,1)}) fusion(bf16[8,8,128,256]{3,2,1,0:T(8,128)(2,1)} %param.8), kind=kLoop, calls=%fused_computation.86 | loop fusion | bytes 6291456 | tf_op jit(solution)/shard_map/slice | solution.py:21
  4.7 4.1 %collective-permute-start.5 = (bf16[8,3,128,256]{3,2,1,0:T(8,128)(2,1)}, bf16[8,3,128,256]{3,2,1,0:T(8,128)(2,1)S(1)}, u32[]{:S(2)}, u32[]{:S(2)}) collective-permute-start(bf16[8,3,128,256]{3,2,1,0:T(8,128)(2,1)} %get-tuple-element.64), channel_id=1, source_target_pairs={{1,0},{2,1},{3,2},{4,3},{5,4},{6,5},{7,6},{8,7},{9,8},{10,9},{11,1... | collective-permute-start | bytes 4718600 | tf_op jit(solution)/shard_map/ppermute | solution.py:17
  8.9 2.1 %collective-permute-start = (bf16[8,3,128,256]{3,2,1,0:T(8,128)(2,1)}, bf16[8,3,128,256]{3,2,1,0:T(8,128)(2,1)S(1)}, u32[]{:S(2)}, u32[]{:S(2)}) collective-permute-start(bf16[8,3,128,256]{3,2,1,0:T(8,128)(2,1)} %get-tuple-element.63), channel_id=1, source_target_pairs={{0,1},{1,2},{2,3},{3,4},{4,5},{5,6},{6,7},{7,8},{8,9},{9,10},{10,1... | collective-permute-start | bytes 4718600 | tf_op jit(solution)/shard_map/ppermute | solution.py:17
  10.9 2.0 %fusion.36 = (bf16[3,8,128,256]{3,2,1,0:T(8,128)(2,1)}, bf16[3,8,128,256]{3,2,1,0:T(8,128)(2,1)}) fusion(bf16[8,8,128,256]{3,2,1,0:T(8,128)(2,1)S(1)} %copy-done.1), kind=kLoop, calls=%fused_computation.87 | loop fusion | bytes 6291456 | tf_op jit(solution)/shard_map/slice | solution.py:19
  13.0 2.4 %collective-permute-start.3 = (bf16[3,8,128,256]{3,2,1,0:T(8,128)(2,1)}, bf16[3,8,128,256]{3,2,1,0:T(8,128)(2,1)}, u32[]{:S(2)}, u32[]{:S(2)}) collective-permute-start(bf16[3,8,128,256]{3,2,1,0:T(8,128)(2,1)} %get-tuple-element.67), channel_id=1, source_target_pairs={{0,16},{16,32},{32,48},{48,64},{64,80},{80,96},{96,112},{112,128},... | collective-permute-start | bytes 4718600 | tf_op jit(solution)/shard_map/ppermute | solution.py:17
  19.1 23.8 %collective-permute-done.5 = bf16[8,3,128,256]{3,2,1,0:T(8,128)(2,1)S(1)} collective-permute-done((bf16[8,3,128,256]{3,2,1,0:T(8,128)(2,1)}, bf16[8,3,128,256]{3,2,1,0:T(8,128)(2,1)S(1)}, u32[]{:S(2)}, u32[]{:S(2)}) %collective-permute-start.5) | collective-permute-done | bytes 1572896 | tf_op jit(solution)/shard_map/ppermute | solution.py:17
  44.1 2.4 %collective-permute-start.6 = (bf16[3,3,128,256]{3,2,1,0:T(8,128)(2,1)}, bf16[3,3,128,256]{3,2,1,0:T(8,128)(2,1)}, u32[]{:S(2)}, u32[]{:S(2)}) collective-permute-start(bf16[3,3,128,256]{3,2,1,0:T(8,128)(2,1)} %get-tuple-element.75), channel_id=1, source_target_pairs={{0,16},{16,32},{32,48},{48,64},{64,80},{80,96},{96,112},{112,128},... | collective-permute-start | bytes 1769480 | tf_op jit(solution)/shard_map/ppermute | solution.py:17
  48.9 5.2 %collective-permute-start.1 = (bf16[3,3,128,256]{3,2,1,0:T(8,128)(2,1)}, bf16[3,3,128,256]{3,2,1,0:T(8,128)(2,1)}, u32[]{:S(2)}, u32[]{:S(2)}) collective-permute-start(bf16[3,3,128,256]{3,2,1,0:T(8,128)(2,1)} %get-tuple-element.71), channel_id=1, source_target_pairs={{0,16},{16,32},{32,48},{48,64},{64,80},{80,96},{96,112},{112,128},... | collective-permute-start | bytes 1769480 | tf_op jit(solution)/shard_map/ppermute | solution.py:17
  54.1 1.5 collective-permute-start.2
  55.6 1.5 constant_dynamic-update-slice_fusion.5
  58.2 1.5 constant_dynamic-update-slice_fusion.6
  59.7 11.3 %multiply_add_fusion = f32[8,8,128,256]{3,2,1,0:T(8,128)} fusion(bf16[8,8,128,256]{3,2,1,0:T(8,128)(2,1)S(1)} %copy-done.2, bf16[11,8,128,256]{3,2,1,0:T(8,128)(2,1)S(1)} %constant_dynamic-update-slice_fusion.6, bf16[11,8,128,256]{3,2,1,0:T(8,128)(2,1)S(1)} %get-tuple-element.65, f32[]{:T(128)} %bitcast.7, f32[]{:T(128)} %bitcast.6, f32[]{:T(128)} %bitcast.5, ...), kind=kLoop, calls=%fused_computation.40 | loop fusion | flops 41943040 | bytes 37748764 | tf_op jit(solution)/shard_map/add | solution.py:49
  75.2 7.6 %multiply_add_fusion.1 = f32[8,3,128,256]{3,2,1,0:T(8,128)} fusion(bf16[8,3,128,256]{3,2,1,0:T(8,128)(2,1)S(1)} %collective-permute-done.5, bf16[11,3,128,256]{3,2,1,0:T(8,128)(2,1)S(1)} %constant_dynamic-update-slice_fusion.10, bf16[11,3,128,256]{3,2,1,0:T(8,128)(2,1)S(1)} %get-tuple-element.73, f32[]{:T(128)} %bitcast.7, f32[]{:T(128)} %bitcast.6, ...), kind=kLoop, calls=%fused_computation.41 | loop fusion | flops 15728640 | bytes 14155804 | tf_op jit(solution)/shard_map/add | solution.py:49
  84.0 8.1 %multiply_add_fusion.2 = f32[8,3,128,256]{3,2,1,0:T(8,128)} fusion(bf16[8,3,128,256]{3,2,1,0:T(8,128)(2,1)S(1)} %copy-done.4, bf16[11,3,128,256]{3,2,1,0:T(8,128)(2,1)S(1)} %constant_dynamic-update-slice_fusion.2, bf16[11,3,128,256]{3,2,1,0:T(8,128)(2,1)S(1)} %get-tuple-element.69, f32[]{:T(128)} %bitcast.7, f32[]{:T(128)} %bitcast.6, f32[]{:T(128)} %bitcast.5, ...), kind=kLoop, calls=%fused_computation.42 | loop fusion | flops 15728640 | bytes 14155804 | tf_op jit(solution)/shard_map/add | solution.py:49
  92.2 14.6 %fusion.13 = bf16[8,8,128,256]{3,2,1,0:T(8,128)(2,1)} fusion(f32[8,8,128,256]{3,2,1,0:T(8,128)S(1)} %bitcast.60, f32[8,3,128,256]{3,2,1,0:T(8,128)} %multiply_add_fusion.1, f32[8,3,128,256]{3,2,1,0:T(8,128)} %multiply_add_fusion.2, f32[]{:T(128)} %bitcast.13, f32[]{:T(128)} %bitcast.12, f32[]{:T(128)} %bitcast.11, f32[]{:T(128)} %bitcast.10, f32[]{:T(128)} %bitcast.9, ...), kind=kLoop, calls=%fused_computation.24 | loop fusion | flops 41943040 | bytes 18874396 | tf_op jit(solution)/shard_map/convert_element_type | solution.py:68
  106.8 3.4 %convolution_convert_fusion.1 = bf16[8192,256]{1,0:T(8,128)(2,1)S(1)} fusion(bf16[8192,256]{1,0:T(8,128)(2,1)} %bitcast.61, bf16[32,8,2,128]{3,2,1,0:T(2,128)(2,1)S(1)} %bitcast.62), kind=kOutput, calls=%fused_computation.19 | convolution fusion | flops 1075838976 | bytes 8519680 | tf_op jit(solution)/shard_map/dot_general | solution.py:70
  113.5 1.6 collective-permute-start.8
  116.2 2.1 %collective-permute-start.9 = (f32[257,128]{1,0:T(8,128)S(1)}, f32[257,128]{1,0:T(8,128)S(1)}, u32[]{:S(2)}, u32[]{:S(2)}) collective-permute-start(f32[257,128]{1,0:T(8,128)S(1)} %fusion.33), channel_id=1, source_target_pairs={{0,32},{16,48},{32,0},{48,16},{64,96},{80,112},{96,64},{112,80},{1... | collective-permute-start | bytes 394760 | tf_op jit(solution)/shard_map/ppermute | solution.py:79
  118.2 4.0 %collective-permute-done.9 = f32[257,128]{1,0:T(8,128)S(1)} collective-permute-done((f32[257,128]{1,0:T(8,128)S(1)}, f32[257,128]{1,0:T(8,128)S(1)}, u32[]{:S(2)}, u32[]{:S(2)}) %collective-permute-start.9) | collective-permute-done | bytes 131616 | tf_op jit(solution)/shard_map/ppermute | solution.py:79
  122.3 5.8 %collective-permute-start.10 = (f32[257,128]{1,0:T(8,128)S(1)}, f32[257,128]{1,0:T(8,128)S(1)}, u32[]{:S(2)}, u32[]{:S(2)}) collective-permute-start(f32[257,128]{1,0:T(8,128)S(1)} %add.144), channel_id=1, source_target_pairs={{0,64},{16,80},{32,96},{48,112},{64,0},{80,16},{96,32},{112,48},{1... | collective-permute-start | bytes 394760 | tf_op jit(solution)/shard_map/ppermute | solution.py:79
  128.1 6.4 %collective-permute-done.10 = f32[257,128]{1,0:T(8,128)S(1)} collective-permute-done((f32[257,128]{1,0:T(8,128)S(1)}, f32[257,128]{1,0:T(8,128)S(1)}, u32[]{:S(2)}, u32[]{:S(2)}) %collective-permute-start.10) | collective-permute-done | bytes 131616 | tf_op jit(solution)/shard_map/ppermute | solution.py:79
  134.5 6.0 %collective-permute-start.11 = (f32[257,128]{1,0:T(8,128)S(1)}, f32[257,128]{1,0:T(8,128)S(1)}, u32[]{:S(2)}, u32[]{:S(2)}) collective-permute-start(f32[257,128]{1,0:T(8,128)S(1)} %add.145), channel_id=1, source_target_pairs={{0,128},{16,144},{32,160},{48,176},{64,192},{80,208},{96,224},{112... | collective-permute-start | bytes 394760 | tf_op jit(solution)/shard_map/ppermute | solution.py:79
  140.6 6.7 %collective-permute-done.11 = f32[257,128]{1,0:T(8,128)S(1)} collective-permute-done((f32[257,128]{1,0:T(8,128)S(1)}, f32[257,128]{1,0:T(8,128)S(1)}, u32[]{:S(2)}, u32[]{:S(2)}) %collective-permute-start.11) | collective-permute-done | bytes 131616 | tf_op jit(solution)/shard_map/ppermute | solution.py:79
  147.9 4.5 %collective-permute-done.12 = f32[257,128]{1,0:T(8,128)S(1)} collective-permute-done((f32[257,128]{1,0:T(8,128)S(1)}, f32[257,128]{1,0:T(8,128)S(1)}, u32[]{:S(2)}, u32[]{:S(2)}) %collective-permute-start.12) | collective-permute-done | bytes 131616 | tf_op jit(solution)/shard_map/ppermute | solution.py:79
  152.4 4.3 %collective-permute-start.13 = (f32[257,128]{1,0:T(8,128)S(1)}, f32[257,128]{1,0:T(8,128)S(1)}, u32[]{:S(2)}, u32[]{:S(2)}) collective-permute-start(f32[257,128]{1,0:T(8,128)S(1)} %add.147), channel_id=1, source_target_pairs={{0,2},{1,3},{2,0},{3,1},{4,6},{5,7},{6,4},{7,5},{8,10},{9,11},{10,... | collective-permute-start | bytes 394760 | tf_op jit(solution)/shard_map/ppermute | solution.py:79
  156.7 3.0 %collective-permute-done.13 = f32[257,128]{1,0:T(8,128)S(1)} collective-permute-done((f32[257,128]{1,0:T(8,128)S(1)}, f32[257,128]{1,0:T(8,128)S(1)}, u32[]{:S(2)}, u32[]{:S(2)}) %collective-permute-start.13) | collective-permute-done | bytes 131616 | tf_op jit(solution)/shard_map/ppermute | solution.py:79
  159.7 1.7 collective-permute-start.14
  161.4 4.7 %collective-permute-done.14 = f32[257,128]{1,0:T(8,128)S(1)} collective-permute-done((f32[257,128]{1,0:T(8,128)S(1)}, f32[257,128]{1,0:T(8,128)S(1)}, u32[]{:S(2)}, u32[]{:S(2)}) %collective-permute-start.14) | collective-permute-done | bytes 131616 | tf_op jit(solution)/shard_map/ppermute | solution.py:79
  166.1 2.6 %collective-permute-start.15 = (f32[257,128]{1,0:T(8,128)S(1)}, f32[257,128]{1,0:T(8,128)S(1)}, u32[]{:S(2)}, u32[]{:S(2)}) collective-permute-start(f32[257,128]{1,0:T(8,128)S(1)} %add.149), channel_id=1, source_target_pairs={{0,8},{1,9},{2,10},{3,11},{4,12},{5,13},{6,14},{7,15},{8,0},{9,1},... | collective-permute-start | bytes 394760 | tf_op jit(solution)/shard_map/ppermute | solution.py:79
  170.1 2.6 %collective-permute-done.15 = f32[257,128]{1,0:T(8,128)S(1)} collective-permute-done((f32[257,128]{1,0:T(8,128)S(1)}, f32[257,128]{1,0:T(8,128)S(1)}, u32[]{:S(2)}, u32[]{:S(2)}) %collective-permute-start.15) | collective-permute-done | bytes 131616 | tf_op jit(solution)/shard_map/ppermute | solution.py:79
  174.7 19.5 %while.11 = (s32[]{:T(128)}, f32[2,256,256]{1,2,0:T(8,128)S(1)}, f32[256,256]{1,0:T(8,128)S(1)}, f32[2]{0:T(128)S(1)}, f32[256,256]{1,0:T(8,128)S(1)}, /*index=5*/s32[]{:T(128)}) while((s32[]{:T(128)}, f32[2,256,256]{1,2,0:T(8,128)S(1)}, f32[256,256]{1,0:T(8,128)S(1)}, f32[2]{0:T(128)S(1)}, f32[256,256]{1,0:T(8,128)S(1)}, ...), condition=%wide.region_3.4_spmd.clone, body=%wide.region_2.3_spmd.clone.sunk | while | flops 805830656 | bytes 4194381 | solution.py:121
  194.6 6.2 %multiply_reduce_fusion = (f32[8192]{0:T(1024)}, bf16[8192,256]{1,0:T(8,128)(2,1)}) fusion(bf16[8192,256]{1,0:T(8,128)(2,1)} %copy-done, f32[256,256]{1,0:T(8,128)S(1)} %fusion.26), kind=kOutput, calls=%fused_computation.39 | convolution fusion | flops 1082187776 | bytes 8683520 | tf_op jit(solution)/shard_map/dot_general | solution.py:136
  (118 shorter events, 40.0 us)
Async XLA Ops:
  0.6 10.3 %copy-start.1 = (bf16[8,8,128,256]{3,2,1,0:T(8,128)(2,1)S(1)}, bf16[8,8,128,256]{3,2,1,0:T(8,128)(2,1)}, u32[]{:S(2)}) copy-start(bf16[8,8,128,256]{3,2,1,0:T(8,128)(2,1)} %param.8) | copy-start | bytes 12582916
  4.7 38.2 %collective-permute-start.5 = (bf16[8,3,128,256]{3,2,1,0:T(8,128)(2,1)}, bf16[8,3,128,256]{3,2,1,0:T(8,128)(2,1)S(1)}, u32[]{:S(2)}, u32[]{:S(2)}) collective-permute-start(bf16[8,3,128,256]{3,2,1,0:T(8,128)(2,1)} %get-tuple-element.64), channel_id=1, source_target_pairs={{1,0},{2,1},{3,2},{4,3},{5,4},{6,5},{7,6},{8,7},{9,8},{10,9},{11,1... | collective-permute-start | bytes 4718600 | tf_op jit(solution)/shard_map/ppermute | solution.py:17
  8.8 7.9 %copy-start.6 = (f32[7]{0:T(128)S(1)}, f32[7]{0:T(128)}, u32[]{:S(2)}) copy-start(f32[7]{0:T(128)} %param.9) | copy-start | bytes 88
  8.8 8.5 %copy-start.7 = (f32[7]{0:T(128)S(1)}, f32[7]{0:T(128)}, u32[]{:S(2)}) copy-start(f32[7]{0:T(128)} %param.10) | copy-start | bytes 88
  8.9 9.2 %copy-start.8 = (bf16[32]{0:T(256)(128)(2,1)S(1)}, bf16[32]{0:T(256)(128)(2,1)}, u32[]{:S(2)}) copy-start(bf16[32]{0:T(256)(128)(2,1)} %param.11) | copy-start | bytes 196
  8.9 38.9 %collective-permute-start = (bf16[8,3,128,256]{3,2,1,0:T(8,128)(2,1)}, bf16[8,3,128,256]{3,2,1,0:T(8,128)(2,1)S(1)}, u32[]{:S(2)}, u32[]{:S(2)}) collective-permute-start(bf16[8,3,128,256]{3,2,1,0:T(8,128)(2,1)} %get-tuple-element.63), channel_id=1, source_target_pairs={{0,1},{1,2},{2,3},{3,4},{4,5},{5,6},{6,7},{7,8},{8,9},{9,10},{10,1... | collective-permute-start | bytes 4718600 | tf_op jit(solution)/shard_map/ppermute | solution.py:17
  13.0 41.1 %collective-permute-start.3 = (bf16[3,8,128,256]{3,2,1,0:T(8,128)(2,1)}, bf16[3,8,128,256]{3,2,1,0:T(8,128)(2,1)}, u32[]{:S(2)}, u32[]{:S(2)}) collective-permute-start(bf16[3,8,128,256]{3,2,1,0:T(8,128)(2,1)} %get-tuple-element.67), channel_id=1, source_target_pairs={{0,16},{16,32},{32,48},{48,64},{64,80},{80,96},{96,112},{112,128},... | collective-permute-start | bytes 4718600 | tf_op jit(solution)/shard_map/ppermute | solution.py:17
  15.4 42.8 %collective-permute-start.4 = (bf16[3,8,128,256]{3,2,1,0:T(8,128)(2,1)}, bf16[3,8,128,256]{3,2,1,0:T(8,128)(2,1)}, u32[]{:S(2)}, u32[]{:S(2)}) collective-permute-start(bf16[3,8,128,256]{3,2,1,0:T(8,128)(2,1)} %get-tuple-element.68), channel_id=1, source_target_pairs={{16,0},{32,16},{48,32},{64,48},{80,64},{96,80},{112,96},{128,112},... | collective-permute-start | bytes 4718600 | tf_op jit(solution)/shard_map/ppermute | solution.py:17
  44.1 13.0 %copy-start.2 = (bf16[8,8,128,256]{3,2,1,0:T(8,128)(2,1)S(1)}, bf16[8,8,128,256]{3,2,1,0:T(8,128)(2,1)}, u32[]{:S(2)}) copy-start(bf16[8,8,128,256]{3,2,1,0:T(8,128)(2,1)} %param.8) | copy-start | bytes 12582916
  44.1 27.0 %collective-permute-start.6 = (bf16[3,3,128,256]{3,2,1,0:T(8,128)(2,1)}, bf16[3,3,128,256]{3,2,1,0:T(8,128)(2,1)}, u32[]{:S(2)}, u32[]{:S(2)}) collective-permute-start(bf16[3,3,128,256]{3,2,1,0:T(8,128)(2,1)} %get-tuple-element.75), channel_id=1, source_target_pairs={{0,16},{16,32},{32,48},{48,64},{64,80},{80,96},{96,112},{112,128},... | collective-permute-start | bytes 1769480 | tf_op jit(solution)/shard_map/ppermute | solution.py:17
  46.4 27.6 %collective-permute-start.7 = (bf16[3,3,128,256]{3,2,1,0:T(8,128)(2,1)}, bf16[3,3,128,256]{3,2,1,0:T(8,128)(2,1)}, u32[]{:S(2)}, u32[]{:S(2)}) collective-permute-start(bf16[3,3,128,256]{3,2,1,0:T(8,128)(2,1)} %get-tuple-element.76), channel_id=1, source_target_pairs={{16,0},{32,16},{48,32},{64,48},{80,64},{96,80},{112,96},{128,112},... | collective-permute-start | bytes 1769480 | tf_op jit(solution)/shard_map/ppermute | solution.py:17
  47.7 25.9 %copy-start.3 = (bf16[8,3,128,256]{3,2,1,0:T(8,128)(2,1)}, bf16[8,3,128,256]{3,2,1,0:T(8,128)(2,1)S(1)}, u32[]{:S(2)}) copy-start(bf16[8,3,128,256]{3,2,1,0:T(8,128)(2,1)S(1)} %collective-permute-done) | copy-start | bytes 4718596
  48.9 23.2 %collective-permute-start.1 = (bf16[3,3,128,256]{3,2,1,0:T(8,128)(2,1)}, bf16[3,3,128,256]{3,2,1,0:T(8,128)(2,1)}, u32[]{:S(2)}, u32[]{:S(2)}) collective-permute-start(bf16[3,3,128,256]{3,2,1,0:T(8,128)(2,1)} %get-tuple-element.71), channel_id=1, source_target_pairs={{0,16},{16,32},{32,48},{48,64},{64,80},{80,96},{96,112},{112,128},... | collective-permute-start | bytes 1769480 | tf_op jit(solution)/shard_map/ppermute | solution.py:17
  54.1 28.6 %collective-permute-start.2 = (bf16[3,3,128,256]{3,2,1,0:T(8,128)(2,1)}, bf16[3,3,128,256]{3,2,1,0:T(8,128)(2,1)}, u32[]{:S(2)}, u32[]{:S(2)}) collective-permute-start(bf16[3,3,128,256]{3,2,1,0:T(8,128)(2,1)} %get-tuple-element.72), channel_id=1, source_target_pairs={{16,0},{32,16},{48,32},{64,48},{80,64},{96,80},{112,96},{128,112},... | collective-permute-start | bytes 1769480 | tf_op jit(solution)/shard_map/ppermute | solution.py:17
  75.2 8.9 %copy-start.4 = (bf16[8,3,128,256]{3,2,1,0:T(8,128)(2,1)S(1)}, bf16[8,3,128,256]{3,2,1,0:T(8,128)(2,1)}, u32[]{:S(2)}) copy-start(bf16[8,3,128,256]{3,2,1,0:T(8,128)(2,1)} %copy-done.3) | copy-start | bytes 4718596
  82.7 9.4 %slice-start = ((s8[8388608]{0:T(1024)(128)(4,1)}), s8[4194304]{0:T(1024)(128)(4,1)S(1)}, s32[]{:S(2)}) async-start(s8[8388608]{0:T(1024)(128)(4,1)} %bitcast.59), calls=%async_computation | async-start | bytes 8388608
  84.0 8.1 %slice-start.1 = ((s8[8388608]{0:T(1024)(128)(4,1)}), s8[4194304]{0:T(1024)(128)(4,1)S(1)}, s32[]{:S(2)}) async-start(s8[8388608]{0:T(1024)(128)(4,1)} %bitcast.59), calls=%async_computation.1 | async-start | bytes 8388608
  110.2 2.0 copy-start
  113.5 2.6 %collective-permute-start.8 = (f32[257,128]{1,0:T(8,128)S(1)}, f32[257,128]{1,0:T(8,128)S(1)}, u32[]{:S(2)}, u32[]{:S(2)}) collective-permute-start(f32[257,128]{1,0:T(8,128)S(1)} %pad_maximum_fusion.2), channel_id=1, source_target_pairs={{0,16},{16,0},{32,48},{48,32},{64,80},{80,64},{96,112},{112,96},{1... | collective-permute-start | bytes 394760 | tf_op jit(solution)/shard_map/ppermute | solution.py:79
  116.2 6.1 %collective-permute-start.9 = (f32[257,128]{1,0:T(8,128)S(1)}, f32[257,128]{1,0:T(8,128)S(1)}, u32[]{:S(2)}, u32[]{:S(2)}) collective-permute-start(f32[257,128]{1,0:T(8,128)S(1)} %fusion.33), channel_id=1, source_target_pairs={{0,32},{16,48},{32,0},{48,16},{64,96},{80,112},{96,64},{112,80},{1... | collective-permute-start | bytes 394760 | tf_op jit(solution)/shard_map/ppermute | solution.py:79
  122.3 12.2 %collective-permute-start.10 = (f32[257,128]{1,0:T(8,128)S(1)}, f32[257,128]{1,0:T(8,128)S(1)}, u32[]{:S(2)}, u32[]{:S(2)}) collective-permute-start(f32[257,128]{1,0:T(8,128)S(1)} %add.144), channel_id=1, source_target_pairs={{0,64},{16,80},{32,96},{48,112},{64,0},{80,16},{96,32},{112,48},{1... | collective-permute-start | bytes 394760 | tf_op jit(solution)/shard_map/ppermute | solution.py:79
  134.5 12.7 %collective-permute-start.11 = (f32[257,128]{1,0:T(8,128)S(1)}, f32[257,128]{1,0:T(8,128)S(1)}, u32[]{:S(2)}, u32[]{:S(2)}) collective-permute-start(f32[257,128]{1,0:T(8,128)S(1)} %add.145), channel_id=1, source_target_pairs={{0,128},{16,144},{32,160},{48,176},{64,192},{80,208},{96,224},{112... | collective-permute-start | bytes 394760 | tf_op jit(solution)/shard_map/ppermute | solution.py:79
  147.3 5.1 %collective-permute-start.12 = (f32[257,128]{1,0:T(8,128)S(1)}, f32[257,128]{1,0:T(8,128)S(1)}, u32[]{:S(2)}, u32[]{:S(2)}) collective-permute-start(f32[257,128]{1,0:T(8,128)S(1)} %add.146), channel_id=1, source_target_pairs={{0,1},{1,0},{2,3},{3,2},{4,5},{5,4},{6,7},{7,6},{8,9},{9,8},{10,11... | collective-permute-start | bytes 394760 | tf_op jit(solution)/shard_map/ppermute | solution.py:79
  152.4 7.3 %collective-permute-start.13 = (f32[257,128]{1,0:T(8,128)S(1)}, f32[257,128]{1,0:T(8,128)S(1)}, u32[]{:S(2)}, u32[]{:S(2)}) collective-permute-start(f32[257,128]{1,0:T(8,128)S(1)} %add.147), channel_id=1, source_target_pairs={{0,2},{1,3},{2,0},{3,1},{4,6},{5,7},{6,4},{7,5},{8,10},{9,11},{10,... | collective-permute-start | bytes 394760 | tf_op jit(solution)/shard_map/ppermute | solution.py:79
  159.7 6.4 %collective-permute-start.14 = (f32[257,128]{1,0:T(8,128)S(1)}, f32[257,128]{1,0:T(8,128)S(1)}, u32[]{:S(2)}, u32[]{:S(2)}) collective-permute-start(f32[257,128]{1,0:T(8,128)S(1)} %add.148), channel_id=1, source_target_pairs={{0,4},{1,5},{2,6},{3,7},{4,0},{5,1},{6,2},{7,3},{8,12},{9,13},{10,... | collective-permute-start | bytes 394760 | tf_op jit(solution)/shard_map/ppermute | solution.py:79
  166.1 6.6 %collective-permute-start.15 = (f32[257,128]{1,0:T(8,128)S(1)}, f32[257,128]{1,0:T(8,128)S(1)}, u32[]{:S(2)}, u32[]{:S(2)}) collective-permute-start(f32[257,128]{1,0:T(8,128)S(1)} %add.149), channel_id=1, source_target_pairs={{0,8},{1,9},{2,10},{3,11},{4,12},{5,13},{6,14},{7,15},{8,0},{9,1},... | collective-permute-start | bytes 394760 | tf_op jit(solution)/shard_map/ppermute | solution.py:79
  194.6 6.2 %copy-start.5 = (f32[256,256]{1,0:T(8,128)}, f32[256,256]{1,0:T(8,128)S(1)}, u32[]{:S(2)}) copy-start(f32[256,256]{1,0:T(8,128)S(1)} %fusion.26) | copy-start | bytes 786436

commit v5 on v4

--- a/solution.py
+++ b/solution.py
@@ -70,15 +70,31 @@
     return jnp.dot(flat_rows, matrix, preferred_element_type=jnp.float32).astype(jnp.bfloat16)
 
 
-def butterfly_sum(block):
-    for axis in ("lat", "elev"):
+def butterfly_sum(block, strides):
+    for axis, first in strides:
         count = lax.axis_size(axis)
-        stride = 1
+        stride = first
         while stride < count:
             pairs = [(i, i ^ stride) for i in range(count)]
             block = block + lax.ppermute(block, axis, pairs)
             stride *= 2
     return block
+
+
+def chip_split_sum(block):
+    rows = block.shape[0]
+    padded_rows = -(-rows // 16) * 16
+    block = jnp.pad(block, ((0, padded_rows - rows), (0, 0)))
+    swap = [(i, i ^ 1) for i in range(lax.axis_size("lat"))]
+    block = block + lax.ppermute(block, "lat", swap)
+    half = padded_rows // 2
+    core = lax.axis_index("lat") % 2
+    own = lax.dynamic_slice_in_dim(block, core * half, half, axis=0)
+    own = butterfly_sum(own, (("lat", 2), ("elev", 1)))
+    other = lax.ppermute(own, "lat", swap)
+    first = jnp.where(core == 0, own, other)
+    second = jnp.where(core == 0, other, own)
+    return jnp.concatenate([first, second], axis=0)[:rows]
 
 
 def packed_gram_sum(gram):
@@ -91,7 +107,7 @@
     keep_upper = row <= col
     merged = jnp.where(keep_upper, upper, lower)
     diagonal = jnp.diagonal(lower)[None, :]
-    packed = butterfly_sum(jnp.concatenate([side, merged, diagonal], axis=0))
+    packed = chip_split_sum(jnp.concatenate([side, merged, diagonal], axis=0))
     side = packed[:half]
     merged = packed[half : 2 * half]
     diagonal = packed[2 * half]
@@ -103,7 +119,7 @@
     )
 
 
-def band_filter(gram_sum, clutter_rank, noise_rank, steps=13):
+def band_filter(gram_sum, clutter_rank, noise_rank, steps=9):
     width = gram_sum.shape[0]
     identity = jnp.eye(width, dtype=jnp.float32)
     total_trace = jnp.sum(gram_sum * identity)
@@ -111,14 +127,20 @@
     shifted = gram_sum[None] + levels[:, None, None] * identity[None]
     scale = 2.0 / (2.0 * levels + total_trace)
     inverse = scale[:, None, None] * identity[None]
+    low = scale * levels
 
-    def refine(_, inverse):
+    def refine(_, carry):
+        inverse, low = carry
+        squeezed = low * (2.0 - low)
+        factor = 2.0 / (1.0 + squeezed)
         product = jnp.einsum("bij,bjk->bik", shifted, inverse, precision=lax.Precision.HIGHEST)
-        return 2.0 * inverse - jnp.einsum(
-            "bij,bjk->bik", inverse, product, precision=lax.Precision.HIGHEST
+        inverse = factor[:, None, None] * (
+            2.0 * inverse
+            - jnp.einsum("bij,bjk->bik", inverse, product, precision=lax.Precision.HIGHEST)
         )
+        return inverse, factor * squeezed
 
-    inverse = lax.fori_loop(0, steps, refine, inverse)
+    inverse, _ = lax.fori_loop(0, steps, refine, (inverse, low))
     resolvents = levels[:, None, None] * inverse
     return resolvents[0] - resolvents[1]
 

time: 202 us -> 183 us (0.906)
  waiting for transfers between devices: 56.7 us -> 47.4 us
  matrix products: 29.5 us -> 23.9 us
  local copies, waits for them, and re-layouts: 22.3 us -> 16.9 us
    ppermute x8 -> x7, waiting for transfers between devices: 32.9 us -> 20.9 us  [butterfly_sum(): block = block + lax.ppermute(block, axis, pairs)]
    dot_general x13 -> x9, matrix products: 9.86 us -> 6.83 us  [refine(): jnp.einsum('bij,bjk->bik', shifted, inverse, precision=lax.Precision.HIGH...]
    dot_general x13 -> x9, matrix products: 8.7 us -> 6.22 us  [refine(): jnp.einsum('bij,bjk->bik', inverse, product, precision=lax.Precision.HIGH...]
    unnamed x28 -> x23, local copies, waits for them, and re-layouts: 4.78 us -> 3.08 us
    ppermute x8 -> x7, starting transfers between devices: 24.7 us -> 23.5 us  [butterfly_sum(): block = block + lax.ppermute(block, axis, pairs)]
  transfers between devices with their start and end apart: 16 -> 17, of which waited for: 9 -> 9; matrix products, arithmetic and copies ran while one was open for 17% -> 17% of each run, Pallas kernels for 0% -> 0%
where the time goes in v5:
time: 183 us; the launch traced here: 180 us
  waiting for transfers between devices  47.4 us (26%)
  other arithmetic  44.7 us (24%)
  starting transfers between devices  44.2 us (24%)
  matrix products  23.9 us (13%)
  local copies, waits for them, and re-layouts  16.9 us (9%)
  between operations  2.4 us (1%)
    add x3, other arithmetic, lat_pass(): lat_sum + lat_taps[index_tap] * extended[index_tap:index_tap + lat_count]...  27.3 us
    ppermute x8, waiting for transfers between devices, shift(): return lax.ppermute(piece, axis, pairs)  25.5 us
    ppermute x7, starting transfers between devices, butterfly_sum(): block = block + lax.ppermute(block, axis, pairs)  23.5 us
    ppermute x7, waiting for transfers between devices, butterfly_sum(): block = block + lax.ppermute(block, axis, pairs)  20.9 us
    ppermute x8, starting transfers between devices, shift(): return lax.ppermute(piece, axis, pairs)  18.9 us
    convert_element_type x1, other arithmetic, filtered_rows(): smooth(pieces, lat_taps, elev_taps, lat_count, elev_count)  14.5 us
    dot_general x9, matrix products, refine(): jnp.einsum('bij,bjk->bik', shifted, inverse, precision=lax.Precision.HIGH...  6.83 us
    dot_general x9, matrix products, refine(): jnp.einsum('bij,bjk->bik', inverse, product, precision=lax.Precision.HIGH...  6.22 us
  transfers between devices with their start and end apart: 17, of which 9 were waited for; matrix products, arithmetic and copies ran while one was open for 17% of the time, Pallas kernels for 0%

profile of v5, /device:TPU:2, one launch (start us, length us, event | category | flops | bytes accessed | tf_op | source)
XLA Modules:
  0.0 179.8 jit_solution(4795523688728227267)
XLA Ops:
  0.6 2.2 %fusion.37 = (bf16[8,3,128,256]{3,2,1,0:T(8,128)(2,1)S(1)}, bf16[8,3,128,256]{3,2,1,0:T(8,128)(2,1)S(1)}) fusion(bf16[8,8,128,256]{3,2,1,0:T(8,128)(2,1)} %param.8), kind=kLoop, calls=%fused_computation.96 | loop fusion | bytes 6291456 | tf_op jit(solution)/shard_map/slice | solution.py:21
  2.9 4.2 %collective-permute-start.5 = (bf16[8,3,128,256]{3,2,1,0:T(8,128)(2,1)S(1)}, bf16[8,3,128,256]{3,2,1,0:T(8,128)(2,1)S(1)}, u32[]{:S(2)}, u32[]{:S(2)}) collective-permute-start(bf16[8,3,128,256]{3,2,1,0:T(8,128)(2,1)S(1)} %get-tuple-element.61), channel_id=1, source_target_pairs={{1,0},{2,1},{3,2},{4,3},{5,4},{6,5},{7,6},{8,7},{9,8},{10,9},{11,1... | collective-permute-start | bytes 4718600 | tf_op jit(solution)/shard_map/ppermute | solution.py:17
  7.1 2.1 %collective-permute-start = (bf16[8,3,128,256]{3,2,1,0:T(8,128)(2,1)S(1)}, bf16[8,3,128,256]{3,2,1,0:T(8,128)(2,1)S(1)}, u32[]{:S(2)}, u32[]{:S(2)}) collective-permute-start(bf16[8,3,128,256]{3,2,1,0:T(8,128)(2,1)S(1)} %get-tuple-element.60), channel_id=1, source_target_pairs={{0,1},{1,2},{2,3},{3,4},{4,5},{5,6},{6,7},{7,8},{8,9},{9,10},{10,1... | collective-permute-start | bytes 4718600 | tf_op jit(solution)/shard_map/ppermute | solution.py:17
  9.2 1.4 fusion.38
  10.6 1.4 collective-permute-start.3
  11.9 1.3 collective-permute-start.4
  15.5 25.4 %collective-permute-done.5 = bf16[8,3,128,256]{3,2,1,0:T(8,128)(2,1)S(1)} collective-permute-done((bf16[8,3,128,256]{3,2,1,0:T(8,128)(2,1)S(1)}, bf16[8,3,128,256]{3,2,1,0:T(8,128)(2,1)S(1)}, u32[]{:S(2)}, u32[]{:S(2)}) %collective-permute-start.5) | collective-permute-done | bytes 1572896 | tf_op jit(solution)/shard_map/ppermute | solution.py:17
  42.1 2.1 %collective-permute-start.6 = (bf16[3,3,128,256]{3,2,1,0:T(8,128)(2,1)}, bf16[3,3,128,256]{3,2,1,0:T(8,128)(2,1)}, u32[]{:S(2)}, u32[]{:S(2)}) collective-permute-start(bf16[3,3,128,256]{3,2,1,0:T(8,128)(2,1)} %get-tuple-element.72), channel_id=1, source_target_pairs={{0,16},{16,32},{32,48},{48,64},{64,80},{80,96},{96,112},{112,128},... | collective-permute-start | bytes 1769480 | tf_op jit(solution)/shard_map/ppermute | solution.py:17
  44.2 1.3 collective-permute-start.7
  46.7 5.2 %collective-permute-start.1 = (bf16[3,3,128,256]{3,2,1,0:T(8,128)(2,1)}, bf16[3,3,128,256]{3,2,1,0:T(8,128)(2,1)}, u32[]{:S(2)}, u32[]{:S(2)}) collective-permute-start(bf16[3,3,128,256]{3,2,1,0:T(8,128)(2,1)} %get-tuple-element.68), channel_id=1, source_target_pairs={{0,16},{16,32},{32,48},{48,64},{64,80},{80,96},{96,112},{112,128},... | collective-permute-start | bytes 1769480 | tf_op jit(solution)/shard_map/ppermute | solution.py:17
  51.8 1.5 collective-permute-start.2
  54.7 11.4 %multiply_add_fusion = f32[8,8,128,256]{3,2,1,0:T(8,128)} fusion(bf16[8,8,128,256]{3,2,1,0:T(8,128)(2,1)S(1)} %copy-done.1, bf16[11,8,128,256]{3,2,1,0:T(8,128)(2,1)S(1)} %constant_dynamic-update-slice_fusion.6, bf16[11,8,128,256]{3,2,1,0:T(8,128)(2,1)S(1)} %get-tuple-element.62, f32[]{:T(128)} %bitcast.7, f32[]{:T(128)} %bitcast.6, f32[]{:T(128)} %bitcast.5, ...), kind=kLoop, calls=%fused_computation.44 | loop fusion | flops 41943040 | bytes 37748764 | tf_op jit(solution)/shard_map/add | solution.py:49
  70.4 7.7 %multiply_add_fusion.1 = f32[8,3,128,256]{3,2,1,0:T(8,128)} fusion(bf16[8,3,128,256]{3,2,1,0:T(8,128)(2,1)S(1)} %collective-permute-done.5, bf16[11,3,128,256]{3,2,1,0:T(8,128)(2,1)S(1)} %constant_dynamic-update-slice_fusion.10, bf16[11,3,128,256]{3,2,1,0:T(8,128)(2,1)S(1)} %get-tuple-element.70, f32[]{:T(128)} %bitcast.7, f32[]{:T(128)} %bitcast.6, ...), kind=kLoop, calls=%fused_computation.45 | loop fusion | flops 15728640 | bytes 14155804 | tf_op jit(solution)/shard_map/add | solution.py:49
  79.4 8.3 %multiply_add_fusion.2 = f32[8,3,128,256]{3,2,1,0:T(8,128)} fusion(bf16[8,3,128,256]{3,2,1,0:T(8,128)(2,1)S(1)} %copy-done.3, bf16[11,3,128,256]{3,2,1,0:T(8,128)(2,1)S(1)} %constant_dynamic-update-slice_fusion.2, bf16[11,3,128,256]{3,2,1,0:T(8,128)(2,1)S(1)} %get-tuple-element.66, f32[]{:T(128)} %bitcast.7, f32[]{:T(128)} %bitcast.6, f32[]{:T(128)} %bitcast.5, ...), kind=kLoop, calls=%fused_computation.46 | loop fusion | flops 15728640 | bytes 14155804 | tf_op jit(solution)/shard_map/add | solution.py:49
  87.7 14.5 %fusion.15 = bf16[8,8,128,256]{3,2,1,0:T(8,128)(2,1)} fusion(f32[8,8,128,256]{3,2,1,0:T(8,128)S(1)} %bitcast.62, f32[8,3,128,256]{3,2,1,0:T(8,128)} %multiply_add_fusion.1, f32[8,3,128,256]{3,2,1,0:T(8,128)} %multiply_add_fusion.2, f32[]{:T(128)} %bitcast.13, f32[]{:T(128)} %bitcast.12, f32[]{:T(128)} %bitcast.11, f32[]{:T(128)} %bitcast.10, f32[]{:T(128)} %bitcast.9, ...), kind=kLoop, calls=%fused_computation.28 | loop fusion | flops 41943040 | bytes 18874396 | tf_op jit(solution)/shard_map/convert_element_type | solution.py:68
  102.1 3.4 %convolution_convert_fusion.1 = bf16[8192,256]{1,0:T(8,128)(2,1)S(1)} fusion(bf16[8192,256]{1,0:T(8,128)(2,1)} %bitcast.63, bf16[32,8,2,128]{3,2,1,0:T(2,128)(2,1)S(1)} %bitcast.64), kind=kOutput, calls=%fused_computation.23 | convolution fusion | flops 1075838976 | bytes 8519680 | tf_op jit(solution)/shard_map/dot_general | solution.py:70
  108.8 1.6 collective-permute-start.8
  111.5 2.1 %collective-permute-start.9 = (f32[136,128]{1,0:T(8,128)S(1)}, f32[136,128]{1,0:T(8,128)S(1)}, u32[]{:S(2)}, u32[]{:S(2)}) collective-permute-start(f32[136,128]{1,0:T(8,128)S(1)} %dynamic-slice_add_fusion), channel_id=1, source_target_pairs={{0,32},{16,48},{32,0},{48,16},{64,96},{80,112},{96,64},{112,80},{1... | collective-permute-start | bytes 208904 | tf_op jit(solution)/shard_map/ppermute | solution.py:79
  113.6 2.6 %collective-permute-done.9 = f32[136,128]{1,0:T(8,128)S(1)} collective-permute-done((f32[136,128]{1,0:T(8,128)S(1)}, f32[136,128]{1,0:T(8,128)S(1)}, u32[]{:S(2)}, u32[]{:S(2)}) %collective-permute-start.9) | collective-permute-done | bytes 69664 | tf_op jit(solution)/shard_map/ppermute | solution.py:79
  116.2 5.8 %collective-permute-start.10 = (f32[136,128]{1,0:T(8,128)S(1)}, f32[136,128]{1,0:T(8,128)S(1)}, u32[]{:S(2)}, u32[]{:S(2)}) collective-permute-start(f32[136,128]{1,0:T(8,128)S(1)} %add.158), channel_id=1, source_target_pairs={{0,64},{16,80},{32,96},{48,112},{64,0},{80,16},{96,32},{112,48},{1... | collective-permute-start | bytes 208904 | tf_op jit(solution)/shard_map/ppermute | solution.py:79
  122.0 3.8 %collective-permute-done.10 = f32[136,128]{1,0:T(8,128)S(1)} collective-permute-done((f32[136,128]{1,0:T(8,128)S(1)}, f32[136,128]{1,0:T(8,128)S(1)}, u32[]{:S(2)}, u32[]{:S(2)}) %collective-permute-start.10) | collective-permute-done | bytes 69664 | tf_op jit(solution)/shard_map/ppermute | solution.py:79
  125.8 5.8 %collective-permute-start.11 = (f32[136,128]{1,0:T(8,128)S(1)}, f32[136,128]{1,0:T(8,128)S(1)}, u32[]{:S(2)}, u32[]{:S(2)}) collective-permute-start(f32[136,128]{1,0:T(8,128)S(1)} %add.159), channel_id=1, source_target_pairs={{0,128},{16,144},{32,160},{48,176},{64,192},{80,208},{96,224},{112... | collective-permute-start | bytes 208904 | tf_op jit(solution)/shard_map/ppermute | solution.py:79
  131.6 3.1 %collective-permute-done.11 = f32[136,128]{1,0:T(8,128)S(1)} collective-permute-done((f32[136,128]{1,0:T(8,128)S(1)}, f32[136,128]{1,0:T(8,128)S(1)}, u32[]{:S(2)}, u32[]{:S(2)}) %collective-permute-start.11) | collective-permute-done | bytes 69664 | tf_op jit(solution)/shard_map/ppermute | solution.py:79
  135.3 3.8 %collective-permute-done.12 = f32[136,128]{1,0:T(8,128)S(1)} collective-permute-done((f32[136,128]{1,0:T(8,128)S(1)}, f32[136,128]{1,0:T(8,128)S(1)}, u32[]{:S(2)}, u32[]{:S(2)}) %collective-permute-start.12) | collective-permute-done | bytes 69664 | tf_op jit(solution)/shard_map/ppermute | solution.py:79
  139.1 4.3 %collective-permute-start.13 = (f32[136,128]{1,0:T(8,128)S(1)}, f32[136,128]{1,0:T(8,128)S(1)}, u32[]{:S(2)}, u32[]{:S(2)}) collective-permute-start(f32[136,128]{1,0:T(8,128)S(1)} %add.161), channel_id=1, source_target_pairs={{0,2},{1,3},{2,0},{3,1},{4,6},{5,7},{6,4},{7,5},{8,10},{9,11},{10,... | collective-permute-start | bytes 208904 | tf_op jit(solution)/shard_map/ppermute | solution.py:79
  143.5 2.3 %collective-permute-done.13 = f32[136,128]{1,0:T(8,128)S(1)} collective-permute-done((f32[136,128]{1,0:T(8,128)S(1)}, f32[136,128]{1,0:T(8,128)S(1)}, u32[]{:S(2)}, u32[]{:S(2)}) %collective-permute-start.13) | collective-permute-done | bytes 69664 | tf_op jit(solution)/shard_map/ppermute | solution.py:79
  145.8 1.7 collective-permute-start.14
  147.4 2.7 %collective-permute-done.14 = f32[136,128]{1,0:T(8,128)S(1)} collective-permute-done((f32[136,128]{1,0:T(8,128)S(1)}, f32[136,128]{1,0:T(8,128)S(1)}, u32[]{:S(2)}, u32[]{:S(2)}) %collective-permute-start.14) | collective-permute-done | bytes 69664 | tf_op jit(solution)/shard_map/ppermute | solution.py:79
  150.2 3.3 %collective-permute-start.15 = (f32[136,128]{1,0:T(8,128)S(1)}, f32[136,128]{1,0:T(8,128)S(1)}, u32[]{:S(2)}, u32[]{:S(2)}) collective-permute-start(f32[136,128]{1,0:T(8,128)S(1)} %add.163), channel_id=1, source_target_pairs={{0,8},{1,9},{2,10},{3,11},{4,12},{5,13},{6,14},{7,15},{8,0},{9,1},... | collective-permute-start | bytes 208904 | tf_op jit(solution)/shard_map/ppermute | solution.py:79
  153.5 2.6 %collective-permute-done.15 = f32[136,128]{1,0:T(8,128)S(1)} collective-permute-done((f32[136,128]{1,0:T(8,128)S(1)}, f32[136,128]{1,0:T(8,128)S(1)}, u32[]{:S(2)}, u32[]{:S(2)}) %collective-permute-start.15) | collective-permute-done | bytes 69664 | tf_op jit(solution)/shard_map/ppermute | solution.py:79
  159.4 13.9 %while.13 = (s32[]{:T(128)}, f32[2,256,256]{1,2,0:T(8,128)S(1)}, f32[2]{0:T(128)S(1)}, f32[256,256]{1,0:T(8,128)S(1)}, f32[2]{0:T(128)S(1)}, /*index=5*/f32[256,256]{1,0:T(8,128)S(1)}, s32[]{:T(128)}) while((s32[]{:T(128)}, f32[2,256,256]{1,2,0:T(8,128)S(1)}, f32[2]{0:T(128)S(1)}, f32[256,256]{1,0:T(8,128)S(1)}, f32[2]{0:T(128)S(1)}, ...), condition=%wide.region_3.4_spmd.clone, body=%wide.region_2.3_spmd.clone.sunk | while | flops 805961728 | bytes 4194421 | solution.py:143
  173.7 6.2 %multiply_reduce_fusion = (f32[8192]{0:T(1024)}, bf16[8192,256]{1,0:T(8,128)(2,1)}) fusion(bf16[8192,256]{1,0:T(8,128)(2,1)} %copy-done, f32[256,256]{1,0:T(8,128)S(1)} %fusion.28), kind=kOutput, calls=%fused_computation.43 | convolution fusion | flops 1082187776 | bytes 8683520 | tf_op jit(solution)/shard_map/dot_general | solution.py:158
  (113 shorter events, 32.2 us)
Async XLA Ops:
  0.6 8.5 %copy-start.1 = (bf16[8,8,128,256]{3,2,1,0:T(8,128)(2,1)S(1)}, bf16[8,8,128,256]{3,2,1,0:T(8,128)(2,1)}, u32[]{:S(2)}) copy-start(bf16[8,8,128,256]{3,2,1,0:T(8,128)(2,1)} %param.8) | copy-start | bytes 12582916
  2.9 38.0 %collective-permute-start.5 = (bf16[8,3,128,256]{3,2,1,0:T(8,128)(2,1)S(1)}, bf16[8,3,128,256]{3,2,1,0:T(8,128)(2,1)S(1)}, u32[]{:S(2)}, u32[]{:S(2)}) collective-permute-start(bf16[8,3,128,256]{3,2,1,0:T(8,128)(2,1)S(1)} %get-tuple-element.61), channel_id=1, source_target_pairs={{1,0},{2,1},{3,2},{4,3},{5,4},{6,5},{7,6},{8,7},{9,8},{10,9},{11,1... | collective-permute-start | bytes 4718600 | tf_op jit(solution)/shard_map/ppermute | solution.py:17
  7.0 6.2 %copy-start.5 = (f32[7]{0:T(128)S(1)}, f32[7]{0:T(128)}, u32[]{:S(2)}) copy-start(f32[7]{0:T(128)} %param.9) | copy-start | bytes 88
  7.1 6.9 %copy-start.6 = (f32[7]{0:T(128)S(1)}, f32[7]{0:T(128)}, u32[]{:S(2)}) copy-start(f32[7]{0:T(128)} %param.10) | copy-start | bytes 88
  7.1 7.5 %copy-start.7 = (bf16[32]{0:T(256)(128)(2,1)S(1)}, bf16[32]{0:T(256)(128)(2,1)}, u32[]{:S(2)}) copy-start(bf16[32]{0:T(256)(128)(2,1)} %param.11) | copy-start | bytes 196
  7.1 38.4 %collective-permute-start = (bf16[8,3,128,256]{3,2,1,0:T(8,128)(2,1)S(1)}, bf16[8,3,128,256]{3,2,1,0:T(8,128)(2,1)S(1)}, u32[]{:S(2)}, u32[]{:S(2)}) collective-permute-start(bf16[8,3,128,256]{3,2,1,0:T(8,128)(2,1)S(1)} %get-tuple-element.60), channel_id=1, source_target_pairs={{0,1},{1,2},{2,3},{3,4},{4,5},{5,6},{6,7},{7,8},{8,9},{9,10},{10,1... | collective-permute-start | bytes 4718600 | tf_op jit(solution)/shard_map/ppermute | solution.py:17
  10.6 41.3 %collective-permute-start.3 = (bf16[3,8,128,256]{3,2,1,0:T(8,128)(2,1)S(1)}, bf16[3,8,128,256]{3,2,1,0:T(8,128)(2,1)S(1)}, u32[]{:S(2)}, u32[]{:S(2)}) collective-permute-start(bf16[3,8,128,256]{3,2,1,0:T(8,128)(2,1)S(1)} %get-tuple-element.64), channel_id=1, source_target_pairs={{0,16},{16,32},{32,48},{48,64},{64,80},{80,96},{96,112},{112,128},... | collective-permute-start | bytes 4718600 | tf_op jit(solution)/shard_map/ppermute | solution.py:17
  11.9 42.6 %collective-permute-start.4 = (bf16[3,8,128,256]{3,2,1,0:T(8,128)(2,1)}, bf16[3,8,128,256]{3,2,1,0:T(8,128)(2,1)S(1)}, u32[]{:S(2)}, u32[]{:S(2)}) collective-permute-start(bf16[3,8,128,256]{3,2,1,0:T(8,128)(2,1)} %get-tuple-element.65), channel_id=1, source_target_pairs={{16,0},{32,16},{48,32},{64,48},{80,64},{96,80},{112,96},{128,112},... | collective-permute-start | bytes 4718600 | tf_op jit(solution)/shard_map/ppermute | solution.py:17
  42.1 24.0 %collective-permute-start.6 = (bf16[3,3,128,256]{3,2,1,0:T(8,128)(2,1)}, bf16[3,3,128,256]{3,2,1,0:T(8,128)(2,1)}, u32[]{:S(2)}, u32[]{:S(2)}) collective-permute-start(bf16[3,3,128,256]{3,2,1,0:T(8,128)(2,1)} %get-tuple-element.72), channel_id=1, source_target_pairs={{0,16},{16,32},{32,48},{48,64},{64,80},{80,96},{96,112},{112,128},... | collective-permute-start | bytes 1769480 | tf_op jit(solution)/shard_map/ppermute | solution.py:17
  44.2 25.1 %collective-permute-start.7 = (bf16[3,3,128,256]{3,2,1,0:T(8,128)(2,1)}, bf16[3,3,128,256]{3,2,1,0:T(8,128)(2,1)}, u32[]{:S(2)}, u32[]{:S(2)}) collective-permute-start(bf16[3,3,128,256]{3,2,1,0:T(8,128)(2,1)} %get-tuple-element.73), channel_id=1, source_target_pairs={{16,0},{32,16},{48,32},{64,48},{80,64},{96,80},{112,96},{128,112},... | collective-permute-start | bytes 1769480 | tf_op jit(solution)/shard_map/ppermute | solution.py:17
  45.5 23.3 %copy-start.2 = (bf16[8,3,128,256]{3,2,1,0:T(8,128)(2,1)}, bf16[8,3,128,256]{3,2,1,0:T(8,128)(2,1)S(1)}, u32[]{:S(2)}) copy-start(bf16[8,3,128,256]{3,2,1,0:T(8,128)(2,1)S(1)} %collective-permute-done) | copy-start | bytes 4718596
  46.7 20.6 %collective-permute-start.1 = (bf16[3,3,128,256]{3,2,1,0:T(8,128)(2,1)}, bf16[3,3,128,256]{3,2,1,0:T(8,128)(2,1)}, u32[]{:S(2)}, u32[]{:S(2)}) collective-permute-start(bf16[3,3,128,256]{3,2,1,0:T(8,128)(2,1)} %get-tuple-element.68), channel_id=1, source_target_pairs={{0,16},{16,32},{32,48},{48,64},{64,80},{80,96},{96,112},{112,128},... | collective-permute-start | bytes 1769480 | tf_op jit(solution)/shard_map/ppermute | solution.py:17
  51.8 26.3 %collective-permute-start.2 = (bf16[3,3,128,256]{3,2,1,0:T(8,128)(2,1)}, bf16[3,3,128,256]{3,2,1,0:T(8,128)(2,1)}, u32[]{:S(2)}, u32[]{:S(2)}) collective-permute-start(bf16[3,3,128,256]{3,2,1,0:T(8,128)(2,1)} %get-tuple-element.69), channel_id=1, source_target_pairs={{16,0},{32,16},{48,32},{64,48},{80,64},{96,80},{112,96},{128,112},... | collective-permute-start | bytes 1769480 | tf_op jit(solution)/shard_map/ppermute | solution.py:17
  70.4 8.9 %copy-start.3 = (bf16[8,3,128,256]{3,2,1,0:T(8,128)(2,1)S(1)}, bf16[8,3,128,256]{3,2,1,0:T(8,128)(2,1)}, u32[]{:S(2)}) copy-start(bf16[8,3,128,256]{3,2,1,0:T(8,128)(2,1)} %copy-done.2) | copy-start | bytes 4718596
  78.1 9.5 %slice-start = ((s8[8388608]{0:T(1024)(128)(4,1)}), s8[4194304]{0:T(1024)(128)(4,1)S(1)}, s32[]{:S(2)}) async-start(s8[8388608]{0:T(1024)(128)(4,1)} %bitcast.61), calls=%async_computation | async-start | bytes 8388608
  79.4 8.3 %slice-start.1 = ((s8[8388608]{0:T(1024)(128)(4,1)}), s8[4194304]{0:T(1024)(128)(4,1)S(1)}, s32[]{:S(2)}) async-start(s8[8388608]{0:T(1024)(128)(4,1)} %bitcast.61), calls=%async_computation.1 | async-start | bytes 8388608
  105.6 2.0 %copy-start = (bf16[8192,256]{1,0:T(8,128)(2,1)}, bf16[8192,256]{1,0:T(8,128)(2,1)S(1)}, u32[]{:S(2)}) copy-start(bf16[8192,256]{1,0:T(8,128)(2,1)S(1)} %convolution_convert_fusion.1) | copy-start | bytes 12582916
  108.8 2.6 %collective-permute-start.8 = (f32[272,128]{1,0:T(8,128)S(1)}, f32[272,128]{1,0:T(8,128)S(1)}, u32[]{:S(2)}, u32[]{:S(2)}) collective-permute-start(f32[272,128]{1,0:T(8,128)S(1)} %select_maximum_fusion), channel_id=1, source_target_pairs={{0,16},{16,0},{32,48},{48,32},{64,80},{80,64},{96,112},{112,96},{1... | collective-permute-start | bytes 417800 | tf_op jit(solution)/shard_map/ppermute | solution.py:89
  111.5 4.7 %collective-permute-start.9 = (f32[136,128]{1,0:T(8,128)S(1)}, f32[136,128]{1,0:T(8,128)S(1)}, u32[]{:S(2)}, u32[]{:S(2)}) collective-permute-start(f32[136,128]{1,0:T(8,128)S(1)} %dynamic-slice_add_fusion), channel_id=1, source_target_pairs={{0,32},{16,48},{32,0},{48,16},{64,96},{80,112},{96,64},{112,80},{1... | collective-permute-start | bytes 208904 | tf_op jit(solution)/shard_map/ppermute | solution.py:79
  116.2 9.6 %collective-permute-start.10 = (f32[136,128]{1,0:T(8,128)S(1)}, f32[136,128]{1,0:T(8,128)S(1)}, u32[]{:S(2)}, u32[]{:S(2)}) collective-permute-start(f32[136,128]{1,0:T(8,128)S(1)} %add.158), channel_id=1, source_target_pairs={{0,64},{16,80},{32,96},{48,112},{64,0},{80,16},{96,32},{112,48},{1... | collective-permute-start | bytes 208904 | tf_op jit(solution)/shard_map/ppermute | solution.py:79
  125.8 8.9 %collective-permute-start.11 = (f32[136,128]{1,0:T(8,128)S(1)}, f32[136,128]{1,0:T(8,128)S(1)}, u32[]{:S(2)}, u32[]{:S(2)}) collective-permute-start(f32[136,128]{1,0:T(8,128)S(1)} %add.159), channel_id=1, source_target_pairs={{0,128},{16,144},{32,160},{48,176},{64,192},{80,208},{96,224},{112... | collective-permute-start | bytes 208904 | tf_op jit(solution)/shard_map/ppermute | solution.py:79
  134.7 4.4 %collective-permute-start.12 = (f32[136,128]{1,0:T(8,128)S(1)}, f32[136,128]{1,0:T(8,128)S(1)}, u32[]{:S(2)}, u32[]{:S(2)}) collective-permute-start(f32[136,128]{1,0:T(8,128)S(1)} %add.160), channel_id=1, source_target_pairs={{0,1},{1,0},{2,3},{3,2},{4,5},{5,4},{6,7},{7,6},{8,9},{9,8},{10,11... | collective-permute-start | bytes 208904 | tf_op jit(solution)/shard_map/ppermute | solution.py:79
  139.1 6.6 %collective-permute-start.13 = (f32[136,128]{1,0:T(8,128)S(1)}, f32[136,128]{1,0:T(8,128)S(1)}, u32[]{:S(2)}, u32[]{:S(2)}) collective-permute-start(f32[136,128]{1,0:T(8,128)S(1)} %add.161), channel_id=1, source_target_pairs={{0,2},{1,3},{2,0},{3,1},{4,6},{5,7},{6,4},{7,5},{8,10},{9,11},{10,... | collective-permute-start | bytes 208904 | tf_op jit(solution)/shard_map/ppermute | solution.py:79
  145.8 4.4 %collective-permute-start.14 = (f32[136,128]{1,0:T(8,128)S(1)}, f32[136,128]{1,0:T(8,128)S(1)}, u32[]{:S(2)}, u32[]{:S(2)}) collective-permute-start(f32[136,128]{1,0:T(8,128)S(1)} %add.162), channel_id=1, source_target_pairs={{0,4},{1,5},{2,6},{3,7},{4,0},{5,1},{6,2},{7,3},{8,12},{9,13},{10,... | collective-permute-start | bytes 208904 | tf_op jit(solution)/shard_map/ppermute | solution.py:79
  150.2 5.9 %collective-permute-start.15 = (f32[136,128]{1,0:T(8,128)S(1)}, f32[136,128]{1,0:T(8,128)S(1)}, u32[]{:S(2)}, u32[]{:S(2)}) collective-permute-start(f32[136,128]{1,0:T(8,128)S(1)} %add.163), channel_id=1, source_target_pairs={{0,8},{1,9},{2,10},{3,11},{4,12},{5,13},{6,14},{7,15},{8,0},{9,1},... | collective-permute-start | bytes 208904 | tf_op jit(solution)/shard_map/ppermute | solution.py:79
  156.1 1.6 collective-permute-start.16
  173.7 6.2 %copy-start.4 = (f32[256,256]{1,0:T(8,128)}, f32[256,256]{1,0:T(8,128)S(1)}, u32[]{:S(2)}) copy-start(f32[256,256]{1,0:T(8,128)S(1)} %fusion.28) | copy-start | bytes 786436

commit v6 on v5

--- a/solution.py
+++ b/solution.py
@@ -70,15 +70,32 @@
     return jnp.dot(flat_rows, matrix, preferred_element_type=jnp.float32).astype(jnp.bfloat16)
 
 
-def butterfly_sum(block, strides):
-    for axis, first in strides:
+def butterfly_sum(block, groups):
+    for axis, strides in groups:
         count = lax.axis_size(axis)
-        stride = first
-        while stride < count:
-            pairs = [(i, i ^ stride) for i in range(count)]
-            block = block + lax.ppermute(block, axis, pairs)
+        received = []
+        for mask in strides:
+            if mask < count:
+                received.append(lax.ppermute(block, axis, [(i, i ^ mask) for i in range(count)]))
+        if len(received) == 3:
+            block = (block + received[0]) + (received[1] + received[2])
+        elif received:
+            block = block + received[0]
+    return block
+
+
+def radix_groups(axis, first):
+    count = lax.axis_size(axis)
+    groups = []
+    stride = first
+    while stride < count:
+        if 2 * stride < count:
+            groups.append((axis, (stride, 2 * stride, 3 * stride)))
+            stride *= 4
+        else:
+            groups.append((axis, (stride,)))
             stride *= 2
-    return block
+    return groups
 
 
 def chip_split_sum(block):
@@ -90,7 +107,7 @@
     half = padded_rows // 2
     core = lax.axis_index("lat") % 2
     own = lax.dynamic_slice_in_dim(block, core * half, half, axis=0)
-    own = butterfly_sum(own, (("lat", 2), ("elev", 1)))
+    own = butterfly_sum(own, radix_groups("lat", 2) + radix_groups("elev", 1))
     other = lax.ppermute(own, "lat", swap)
     first = jnp.where(core == 0, own, other)
     second = jnp.where(core == 0, other, own)

time: 183 us -> 177 us (0.967)
  waiting for transfers between devices: 47.4 us -> 42 us
    ppermute x7 -> x10, waiting for transfers between devices: 20.9 us -> 15.6 us  [butterfly_sum(): lax.ppermute(block, axis, [(i, i ^ mask) for i in range(count)])]
    ppermute x7 -> x10, starting transfers between devices: 23.5 us -> 22.9 us  [butterfly_sum(): lax.ppermute(block, axis, [(i, i ^ mask) for i in range(count)])]
  transfers between devices with their start and end apart: 17 -> 20, of which waited for: 9 -> 9; matrix products, arithmetic and copies ran while one was open for 17% -> 18% of each run, Pallas kernels for 0% -> 0%
where the time goes in v6:
time: 177 us; the launch traced here: 174 us
  other arithmetic  45.1 us (25%)
  starting transfers between devices  43.5 us (25%)
  waiting for transfers between devices  42 us (24%)
  matrix products  23.9 us (14%)
  local copies, waits for them, and re-layouts  16.9 us (10%)
  between operations  2.4 us (1%)
    add x3, other arithmetic, lat_pass(): lat_sum + lat_taps[index_tap] * extended[index_tap:index_tap + lat_count]...  27.8 us
    ppermute x8, waiting for transfers between devices, shift(): return lax.ppermute(piece, axis, pairs)  25.4 us
    ppermute x10, starting transfers between devices, butterfly_sum(): lax.ppermute(block, axis, [(i, i ^ mask) for i in range(count)])  22.9 us
    ppermute x8, starting transfers between devices, shift(): return lax.ppermute(piece, axis, pairs)  18.9 us
    ppermute x10, waiting for transfers between devices, butterfly_sum(): lax.ppermute(block, axis, [(i, i ^ mask) for i in range(count)])  15.6 us
    convert_element_type x1, other arithmetic, filtered_rows(): smooth(pieces, lat_taps, elev_taps, lat_count, elev_count)  14.5 us
    dot_general x9, matrix products, refine(): jnp.einsum('bij,bjk->bik', shifted, inverse, precision=lax.Precision.HIGH...  6.83 us
    dot_general x9, matrix products, refine(): jnp.einsum('bij,bjk->bik', inverse, product, precision=lax.Precision.HIGH...  6.22 us
  transfers between devices with their start and end apart: 20, of which 9 were waited for; matrix products, arithmetic and copies ran while one was open for 18% of the time, Pallas kernels for 0%

profile of v6, /device:TPU:2, one launch (start us, length us, event | category | flops | bytes accessed | tf_op | source)
XLA Modules:
  0.0 174.3 jit_solution(7509168901857208357)
XLA Ops:
  0.6 2.2 %fusion.37 = (bf16[8,3,128,256]{3,2,1,0:T(8,128)(2,1)S(1)}, bf16[8,3,128,256]{3,2,1,0:T(8,128)(2,1)S(1)}) fusion(bf16[8,8,128,256]{3,2,1,0:T(8,128)(2,1)} %param.8), kind=kLoop, calls=%fused_computation.99 | loop fusion | bytes 6291456 | tf_op jit(solution)/shard_map/slice | solution.py:21
  2.9 4.2 %collective-permute-start.5 = (bf16[8,3,128,256]{3,2,1,0:T(8,128)(2,1)S(1)}, bf16[8,3,128,256]{3,2,1,0:T(8,128)(2,1)S(1)}, u32[]{:S(2)}, u32[]{:S(2)}) collective-permute-start(bf16[8,3,128,256]{3,2,1,0:T(8,128)(2,1)S(1)} %get-tuple-element.61), channel_id=1, source_target_pairs={{1,0},{2,1},{3,2},{4,3},{5,4},{6,5},{7,6},{8,7},{9,8},{10,9},{11,1... | collective-permute-start | bytes 4718600 | tf_op jit(solution)/shard_map/ppermute | solution.py:17
  7.1 2.1 %collective-permute-start = (bf16[8,3,128,256]{3,2,1,0:T(8,128)(2,1)S(1)}, bf16[8,3,128,256]{3,2,1,0:T(8,128)(2,1)S(1)}, u32[]{:S(2)}, u32[]{:S(2)}) collective-permute-start(bf16[8,3,128,256]{3,2,1,0:T(8,128)(2,1)S(1)} %get-tuple-element.60), channel_id=1, source_target_pairs={{0,1},{1,2},{2,3},{3,4},{4,5},{5,6},{6,7},{7,8},{8,9},{9,10},{10,1... | collective-permute-start | bytes 4718600 | tf_op jit(solution)/shard_map/ppermute | solution.py:17
  9.2 1.4 fusion.38
  10.6 1.4 collective-permute-start.3
  11.9 1.3 collective-permute-start.4
  15.5 25.4 %collective-permute-done.5 = bf16[8,3,128,256]{3,2,1,0:T(8,128)(2,1)S(1)} collective-permute-done((bf16[8,3,128,256]{3,2,1,0:T(8,128)(2,1)S(1)}, bf16[8,3,128,256]{3,2,1,0:T(8,128)(2,1)S(1)}, u32[]{:S(2)}, u32[]{:S(2)}) %collective-permute-start.5) | collective-permute-done | bytes 1572896 | tf_op jit(solution)/shard_map/ppermute | solution.py:17
  42.1 2.1 %collective-permute-start.6 = (bf16[3,3,128,256]{3,2,1,0:T(8,128)(2,1)}, bf16[3,3,128,256]{3,2,1,0:T(8,128)(2,1)}, u32[]{:S(2)}, u32[]{:S(2)}) collective-permute-start(bf16[3,3,128,256]{3,2,1,0:T(8,128)(2,1)} %get-tuple-element.72), channel_id=1, source_target_pairs={{0,16},{16,32},{32,48},{48,64},{64,80},{80,96},{96,112},{112,128},... | collective-permute-start | bytes 1769480 | tf_op jit(solution)/shard_map/ppermute | solution.py:17
  44.2 1.3 collective-permute-start.7
  46.7 5.2 %collective-permute-start.1 = (bf16[3,3,128,256]{3,2,1,0:T(8,128)(2,1)}, bf16[3,3,128,256]{3,2,1,0:T(8,128)(2,1)}, u32[]{:S(2)}, u32[]{:S(2)}) collective-permute-start(bf16[3,3,128,256]{3,2,1,0:T(8,128)(2,1)} %get-tuple-element.68), channel_id=1, source_target_pairs={{0,16},{16,32},{32,48},{48,64},{64,80},{80,96},{96,112},{112,128},... | collective-permute-start | bytes 1769480 | tf_op jit(solution)/shard_map/ppermute | solution.py:17
  51.8 1.5 collective-permute-start.2
  54.7 11.6 %multiply_add_fusion = f32[8,8,128,256]{3,2,1,0:T(8,128)} fusion(bf16[8,8,128,256]{3,2,1,0:T(8,128)(2,1)S(1)} %copy-done.1, bf16[11,8,128,256]{3,2,1,0:T(8,128)(2,1)S(1)} %constant_dynamic-update-slice_fusion.6, bf16[11,8,128,256]{3,2,1,0:T(8,128)(2,1)S(1)} %get-tuple-element.62, f32[]{:T(128)} %bitcast.7, f32[]{:T(128)} %bitcast.6, f32[]{:T(128)} %bitcast.5, ...), kind=kLoop, calls=%fused_computation.44 | loop fusion | flops 41943040 | bytes 37748764 | tf_op jit(solution)/shard_map/add | solution.py:49
  70.6 7.8 %multiply_add_fusion.1 = f32[8,3,128,256]{3,2,1,0:T(8,128)} fusion(bf16[8,3,128,256]{3,2,1,0:T(8,128)(2,1)S(1)} %collective-permute-done.5, bf16[11,3,128,256]{3,2,1,0:T(8,128)(2,1)S(1)} %constant_dynamic-update-slice_fusion.10, bf16[11,3,128,256]{3,2,1,0:T(8,128)(2,1)S(1)} %get-tuple-element.70, f32[]{:T(128)} %bitcast.7, f32[]{:T(128)} %bitcast.6, ...), kind=kLoop, calls=%fused_computation.45 | loop fusion | flops 15728640 | bytes 14155804 | tf_op jit(solution)/shard_map/add | solution.py:49
  78.5 1.3 constant_dynamic-update-slice_fusion.2
  79.7 8.4 %multiply_add_fusion.2 = f32[8,3,128,256]{3,2,1,0:T(8,128)} fusion(bf16[8,3,128,256]{3,2,1,0:T(8,128)(2,1)S(1)} %copy-done.3, bf16[11,3,128,256]{3,2,1,0:T(8,128)(2,1)S(1)} %constant_dynamic-update-slice_fusion.2, bf16[11,3,128,256]{3,2,1,0:T(8,128)(2,1)S(1)} %get-tuple-element.66, f32[]{:T(128)} %bitcast.7, f32[]{:T(128)} %bitcast.6, f32[]{:T(128)} %bitcast.5, ...), kind=kLoop, calls=%fused_computation.46 | loop fusion | flops 15728640 | bytes 14155804 | tf_op jit(solution)/shard_map/add | solution.py:49
  88.1 14.5 %fusion.15 = bf16[8,8,128,256]{3,2,1,0:T(8,128)(2,1)} fusion(f32[8,8,128,256]{3,2,1,0:T(8,128)S(1)} %bitcast.62, f32[8,3,128,256]{3,2,1,0:T(8,128)} %multiply_add_fusion.1, f32[8,3,128,256]{3,2,1,0:T(8,128)} %multiply_add_fusion.2, f32[]{:T(128)} %bitcast.13, f32[]{:T(128)} %bitcast.12, f32[]{:T(128)} %bitcast.11, f32[]{:T(128)} %bitcast.10, f32[]{:T(128)} %bitcast.9, ...), kind=kLoop, calls=%fused_computation.28 | loop fusion | flops 41943040 | bytes 18874396 | tf_op jit(solution)/shard_map/convert_element_type | solution.py:68
  102.6 3.4 %convolution_convert_fusion.1 = bf16[8192,256]{1,0:T(8,128)(2,1)S(1)} fusion(bf16[8192,256]{1,0:T(8,128)(2,1)} %bitcast.63, bf16[32,8,2,128]{3,2,1,0:T(2,128)(2,1)S(1)} %bitcast.64), kind=kOutput, calls=%fused_computation.23 | convolution fusion | flops 1075838976 | bytes 8519680 | tf_op jit(solution)/shard_map/dot_general | solution.py:70
  106.1 1.3 fusion.45
  109.3 1.6 collective-permute-start.8
  112.0 3.4 %collective-permute-start.10 = (f32[136,128]{1,0:T(8,128)S(1)}, f32[136,128]{1,0:T(8,128)S(1)}, u32[]{:S(2)}, u32[]{:S(2)}) collective-permute-start(f32[136,128]{1,0:T(8,128)S(1)} %dynamic-slice_add_fusion), channel_id=1, source_target_pairs={{0,64},{16,80},{32,96},{48,112},{64,0},{80,16},{96,32},{112,48},{1... | collective-permute-start | bytes 208904 | tf_op jit(solution)/shard_map/ppermute | solution.py:79
  115.4 3.8 %collective-permute-start.11 = (f32[136,128]{1,0:T(8,128)S(1)}, f32[136,128]{1,0:T(8,128)S(1)}, u32[]{:S(2)}, u32[]{:S(2)}) collective-permute-start(f32[136,128]{1,0:T(8,128)S(1)} %dynamic-slice_add_fusion), channel_id=1, source_target_pairs={{0,96},{16,112},{32,64},{48,80},{64,32},{80,48},{96,0},{112,16},{1... | collective-permute-start | bytes 208904 | tf_op jit(solution)/shard_map/ppermute | solution.py:79
  119.7 4.0 %collective-permute-done.11 = f32[136,128]{1,0:T(8,128)S(1)} collective-permute-done((f32[136,128]{1,0:T(8,128)S(1)}, f32[136,128]{1,0:T(8,128)S(1)}, u32[]{:S(2)}, u32[]{:S(2)}) %collective-permute-start.11) | collective-permute-done | bytes 69664 | tf_op jit(solution)/shard_map/ppermute | solution.py:79
  124.7 5.3 %collective-permute-start.12 = (f32[136,128]{1,0:T(8,128)S(1)}, f32[136,128]{1,0:T(8,128)S(1)}, u32[]{:S(2)}, u32[]{:S(2)}) collective-permute-start(f32[136,128]{1,0:T(8,128)S(1)} %add_add_fusion.2), channel_id=1, source_target_pairs={{0,128},{16,144},{32,160},{48,176},{64,192},{80,208},{96,224},{112... | collective-permute-start | bytes 208904 | tf_op jit(solution)/shard_map/ppermute | solution.py:79
  130.0 3.0 %collective-permute-done.12 = f32[136,128]{1,0:T(8,128)S(1)} collective-permute-done((f32[136,128]{1,0:T(8,128)S(1)}, f32[136,128]{1,0:T(8,128)S(1)}, u32[]{:S(2)}, u32[]{:S(2)}) %collective-permute-start.12) | collective-permute-done | bytes 69664 | tf_op jit(solution)/shard_map/ppermute | solution.py:79
  133.0 4.3 %collective-permute-start.14 = (f32[136,128]{1,0:T(8,128)S(1)}, f32[136,128]{1,0:T(8,128)S(1)}, u32[]{:S(2)}, u32[]{:S(2)}) collective-permute-start(f32[136,128]{1,0:T(8,128)S(1)} %add.170), channel_id=1, source_target_pairs={{0,2},{1,3},{2,0},{3,1},{4,6},{5,7},{6,4},{7,5},{8,10},{9,11},{10,... | collective-permute-start | bytes 208904 | tf_op jit(solution)/shard_map/ppermute | solution.py:79
  137.3 1.3 collective-permute-start.13
  139.7 1.9 %collective-permute-done.15 = f32[136,128]{1,0:T(8,128)S(1)} collective-permute-done((f32[136,128]{1,0:T(8,128)S(1)}, f32[136,128]{1,0:T(8,128)S(1)}, u32[]{:S(2)}, u32[]{:S(2)}) %collective-permute-start.15) | collective-permute-done | bytes 69664 | tf_op jit(solution)/shard_map/ppermute | solution.py:79
  141.7 3.3 %collective-permute-start.17 = (f32[136,128]{1,0:T(8,128)S(1)}, f32[136,128]{1,0:T(8,128)S(1)}, u32[]{:S(2)}, u32[]{:S(2)}) collective-permute-start(f32[136,128]{1,0:T(8,128)S(1)} %add_add_fusion.1), channel_id=1, source_target_pairs={{0,8},{1,9},{2,10},{3,11},{4,12},{5,13},{6,14},{7,15},{8,0},{9,1},... | collective-permute-start | bytes 208904 | tf_op jit(solution)/shard_map/ppermute | solution.py:79
  146.0 1.7 collective-permute-done.17
  147.7 2.8 %collective-permute-done.18 = f32[136,128]{1,0:T(8,128)S(1)} collective-permute-done((f32[136,128]{1,0:T(8,128)S(1)}, f32[136,128]{1,0:T(8,128)S(1)}, u32[]{:S(2)}, u32[]{:S(2)}) %collective-permute-start.18) | collective-permute-done | bytes 69664 | tf_op jit(solution)/shard_map/ppermute | solution.py:79
  153.8 13.9 %while.13 = (s32[]{:T(128)}, f32[2,256,256]{1,2,0:T(8,128)S(1)}, f32[2]{0:T(128)S(1)}, f32[256,256]{1,0:T(8,128)S(1)}, f32[2]{0:T(128)S(1)}, /*index=5*/f32[256,256]{1,0:T(8,128)S(1)}, s32[]{:T(128)}) while((s32[]{:T(128)}, f32[2,256,256]{1,2,0:T(8,128)S(1)}, f32[2]{0:T(128)S(1)}, f32[256,256]{1,0:T(8,128)S(1)}, f32[2]{0:T(128)S(1)}, ...), condition=%wide.region_3.4_spmd.clone, body=%wide.region_2.3_spmd.clone.sunk | while | flops 805961728 | bytes 4194421 | solution.py:160
  168.1 6.2 %multiply_reduce_fusion = (f32[8192]{0:T(1024)}, bf16[8192,256]{1,0:T(8,128)(2,1)}) fusion(bf16[8192,256]{1,0:T(8,128)(2,1)} %copy-done, f32[256,256]{1,0:T(8,128)S(1)} %fusion.28), kind=kOutput, calls=%fused_computation.43 | convolution fusion | flops 1082187776 | bytes 8683520 | tf_op jit(solution)/shard_map/dot_general | solution.py:175
  (116 shorter events, 32.7 us)
Async XLA Ops:
  0.6 8.5 %copy-start.1 = (bf16[8,8,128,256]{3,2,1,0:T(8,128)(2,1)S(1)}, bf16[8,8,128,256]{3,2,1,0:T(8,128)(2,1)}, u32[]{:S(2)}) copy-start(bf16[8,8,128,256]{3,2,1,0:T(8,128)(2,1)} %param.8) | copy-start | bytes 12582916
  2.9 38.0 %collective-permute-start.5 = (bf16[8,3,128,256]{3,2,1,0:T(8,128)(2,1)S(1)}, bf16[8,3,128,256]{3,2,1,0:T(8,128)(2,1)S(1)}, u32[]{:S(2)}, u32[]{:S(2)}) collective-permute-start(bf16[8,3,128,256]{3,2,1,0:T(8,128)(2,1)S(1)} %get-tuple-element.61), channel_id=1, source_target_pairs={{1,0},{2,1},{3,2},{4,3},{5,4},{6,5},{7,6},{8,7},{9,8},{10,9},{11,1... | collective-permute-start | bytes 4718600 | tf_op jit(solution)/shard_map/ppermute | solution.py:17
  7.0 6.2 %copy-start.5 = (f32[7]{0:T(128)S(1)}, f32[7]{0:T(128)}, u32[]{:S(2)}) copy-start(f32[7]{0:T(128)} %param.9) | copy-start | bytes 88
  7.1 6.9 %copy-start.6 = (f32[7]{0:T(128)S(1)}, f32[7]{0:T(128)}, u32[]{:S(2)}) copy-start(f32[7]{0:T(128)} %param.10) | copy-start | bytes 88
  7.1 7.5 %copy-start.7 = (bf16[32]{0:T(256)(128)(2,1)S(1)}, bf16[32]{0:T(256)(128)(2,1)}, u32[]{:S(2)}) copy-start(bf16[32]{0:T(256)(128)(2,1)} %param.11) | copy-start | bytes 196
  7.1 38.4 %collective-permute-start = (bf16[8,3,128,256]{3,2,1,0:T(8,128)(2,1)S(1)}, bf16[8,3,128,256]{3,2,1,0:T(8,128)(2,1)S(1)}, u32[]{:S(2)}, u32[]{:S(2)}) collective-permute-start(bf16[8,3,128,256]{3,2,1,0:T(8,128)(2,1)S(1)} %get-tuple-element.60), channel_id=1, source_target_pairs={{0,1},{1,2},{2,3},{3,4},{4,5},{5,6},{6,7},{7,8},{8,9},{9,10},{10,1... | collective-permute-start | bytes 4718600 | tf_op jit(solution)/shard_map/ppermute | solution.py:17
  10.6 41.3 %collective-permute-start.3 = (bf16[3,8,128,256]{3,2,1,0:T(8,128)(2,1)S(1)}, bf16[3,8,128,256]{3,2,1,0:T(8,128)(2,1)S(1)}, u32[]{:S(2)}, u32[]{:S(2)}) collective-permute-start(bf16[3,8,128,256]{3,2,1,0:T(8,128)(2,1)S(1)} %get-tuple-element.64), channel_id=1, source_target_pairs={{0,16},{16,32},{32,48},{48,64},{64,80},{80,96},{96,112},{112,128},... | collective-permute-start | bytes 4718600 | tf_op jit(solution)/shard_map/ppermute | solution.py:17
  11.9 42.6 %collective-permute-start.4 = (bf16[3,8,128,256]{3,2,1,0:T(8,128)(2,1)}, bf16[3,8,128,256]{3,2,1,0:T(8,128)(2,1)S(1)}, u32[]{:S(2)}, u32[]{:S(2)}) collective-permute-start(bf16[3,8,128,256]{3,2,1,0:T(8,128)(2,1)} %get-tuple-element.65), channel_id=1, source_target_pairs={{16,0},{32,16},{48,32},{64,48},{80,64},{96,80},{112,96},{128,112},... | collective-permute-start | bytes 4718600 | tf_op jit(solution)/shard_map/ppermute | solution.py:17
  42.1 24.2 %collective-permute-start.6 = (bf16[3,3,128,256]{3,2,1,0:T(8,128)(2,1)}, bf16[3,3,128,256]{3,2,1,0:T(8,128)(2,1)}, u32[]{:S(2)}, u32[]{:S(2)}) collective-permute-start(bf16[3,3,128,256]{3,2,1,0:T(8,128)(2,1)} %get-tuple-element.72), channel_id=1, source_target_pairs={{0,16},{16,32},{32,48},{48,64},{64,80},{80,96},{96,112},{112,128},... | collective-permute-start | bytes 1769480 | tf_op jit(solution)/shard_map/ppermute | solution.py:17
  44.2 25.3 %collective-permute-start.7 = (bf16[3,3,128,256]{3,2,1,0:T(8,128)(2,1)}, bf16[3,3,128,256]{3,2,1,0:T(8,128)(2,1)}, u32[]{:S(2)}, u32[]{:S(2)}) collective-permute-start(bf16[3,3,128,256]{3,2,1,0:T(8,128)(2,1)} %get-tuple-element.73), channel_id=1, source_target_pairs={{16,0},{32,16},{48,32},{64,48},{80,64},{96,80},{112,96},{128,112},... | collective-permute-start | bytes 1769480 | tf_op jit(solution)/shard_map/ppermute | solution.py:17
  45.5 23.5 %copy-start.2 = (bf16[8,3,128,256]{3,2,1,0:T(8,128)(2,1)}, bf16[8,3,128,256]{3,2,1,0:T(8,128)(2,1)S(1)}, u32[]{:S(2)}) copy-start(bf16[8,3,128,256]{3,2,1,0:T(8,128)(2,1)S(1)} %collective-permute-done) | copy-start | bytes 4718596
  46.7 20.7 %collective-permute-start.1 = (bf16[3,3,128,256]{3,2,1,0:T(8,128)(2,1)}, bf16[3,3,128,256]{3,2,1,0:T(8,128)(2,1)}, u32[]{:S(2)}, u32[]{:S(2)}) collective-permute-start(bf16[3,3,128,256]{3,2,1,0:T(8,128)(2,1)} %get-tuple-element.68), channel_id=1, source_target_pairs={{0,16},{16,32},{32,48},{48,64},{64,80},{80,96},{96,112},{112,128},... | collective-permute-start | bytes 1769480 | tf_op jit(solution)/shard_map/ppermute | solution.py:17
  51.8 26.6 %collective-permute-start.2 = (bf16[3,3,128,256]{3,2,1,0:T(8,128)(2,1)}, bf16[3,3,128,256]{3,2,1,0:T(8,128)(2,1)}, u32[]{:S(2)}, u32[]{:S(2)}) collective-permute-start(bf16[3,3,128,256]{3,2,1,0:T(8,128)(2,1)} %get-tuple-element.69), channel_id=1, source_target_pairs={{16,0},{32,16},{48,32},{64,48},{80,64},{96,80},{112,96},{128,112},... | collective-permute-start | bytes 1769480 | tf_op jit(solution)/shard_map/ppermute | solution.py:17
  70.6 9.1 %copy-start.3 = (bf16[8,3,128,256]{3,2,1,0:T(8,128)(2,1)S(1)}, bf16[8,3,128,256]{3,2,1,0:T(8,128)(2,1)}, u32[]{:S(2)}) copy-start(bf16[8,3,128,256]{3,2,1,0:T(8,128)(2,1)} %copy-done.2) | copy-start | bytes 4718596
  78.4 9.7 %slice-start = ((s8[8388608]{0:T(1024)(128)(4,1)}), s8[4194304]{0:T(1024)(128)(4,1)S(1)}, s32[]{:S(2)}) async-start(s8[8388608]{0:T(1024)(128)(4,1)} %bitcast.61), calls=%async_computation | async-start | bytes 8388608
  79.7 8.4 %slice-start.1 = ((s8[8388608]{0:T(1024)(128)(4,1)}), s8[4194304]{0:T(1024)(128)(4,1)S(1)}, s32[]{:S(2)}) async-start(s8[8388608]{0:T(1024)(128)(4,1)} %bitcast.61), calls=%async_computation.1 | async-start | bytes 8388608
  106.1 2.0 %copy-start = (bf16[8192,256]{1,0:T(8,128)(2,1)}, bf16[8192,256]{1,0:T(8,128)(2,1)S(1)}, u32[]{:S(2)}) copy-start(bf16[8192,256]{1,0:T(8,128)(2,1)S(1)} %convolution_convert_fusion.1) | copy-start | bytes 12582916
  109.3 2.6 %collective-permute-start.8 = (f32[272,128]{1,0:T(8,128)S(1)}, f32[272,128]{1,0:T(8,128)S(1)}, u32[]{:S(2)}, u32[]{:S(2)}) collective-permute-start(f32[272,128]{1,0:T(8,128)S(1)} %select_maximum_fusion), channel_id=1, source_target_pairs={{0,16},{16,0},{32,48},{48,32},{64,80},{80,64},{96,112},{112,96},{1... | collective-permute-start | bytes 417800 | tf_op jit(solution)/shard_map/ppermute | solution.py:106
  112.0 7.7 %collective-permute-start.10 = (f32[136,128]{1,0:T(8,128)S(1)}, f32[136,128]{1,0:T(8,128)S(1)}, u32[]{:S(2)}, u32[]{:S(2)}) collective-permute-start(f32[136,128]{1,0:T(8,128)S(1)} %dynamic-slice_add_fusion), channel_id=1, source_target_pairs={{0,64},{16,80},{32,96},{48,112},{64,0},{80,16},{96,32},{112,48},{1... | collective-permute-start | bytes 208904 | tf_op jit(solution)/shard_map/ppermute | solution.py:79
  115.4 8.2 %collective-permute-start.11 = (f32[136,128]{1,0:T(8,128)S(1)}, f32[136,128]{1,0:T(8,128)S(1)}, u32[]{:S(2)}, u32[]{:S(2)}) collective-permute-start(f32[136,128]{1,0:T(8,128)S(1)} %dynamic-slice_add_fusion), channel_id=1, source_target_pairs={{0,96},{16,112},{32,64},{48,80},{64,32},{80,48},{96,0},{112,16},{1... | collective-permute-start | bytes 208904 | tf_op jit(solution)/shard_map/ppermute | solution.py:79
  119.2 5.5 %collective-permute-start.9 = (f32[136,128]{1,0:T(8,128)S(1)}, f32[136,128]{1,0:T(8,128)S(1)}, u32[]{:S(2)}, u32[]{:S(2)}) collective-permute-start(f32[136,128]{1,0:T(8,128)S(1)} %dynamic-slice_add_fusion), channel_id=1, source_target_pairs={{0,32},{16,48},{32,0},{48,16},{64,96},{80,112},{96,64},{112,80},{1... | collective-permute-start | bytes 208904 | tf_op jit(solution)/shard_map/ppermute | solution.py:79
  124.7 8.3 %collective-permute-start.12 = (f32[136,128]{1,0:T(8,128)S(1)}, f32[136,128]{1,0:T(8,128)S(1)}, u32[]{:S(2)}, u32[]{:S(2)}) collective-permute-start(f32[136,128]{1,0:T(8,128)S(1)} %add_add_fusion.2), channel_id=1, source_target_pairs={{0,128},{16,144},{32,160},{48,176},{64,192},{80,208},{96,224},{112... | collective-permute-start | bytes 208904 | tf_op jit(solution)/shard_map/ppermute | solution.py:79
  133.0 6.7 %collective-permute-start.14 = (f32[136,128]{1,0:T(8,128)S(1)}, f32[136,128]{1,0:T(8,128)S(1)}, u32[]{:S(2)}, u32[]{:S(2)}) collective-permute-start(f32[136,128]{1,0:T(8,128)S(1)} %add.170), channel_id=1, source_target_pairs={{0,2},{1,3},{2,0},{3,1},{4,6},{5,7},{6,4},{7,5},{8,10},{9,11},{10,... | collective-permute-start | bytes 208904 | tf_op jit(solution)/shard_map/ppermute | solution.py:79
  137.3 4.3 %collective-permute-start.15 = (f32[136,128]{1,0:T(8,128)S(1)}, f32[136,128]{1,0:T(8,128)S(1)}, u32[]{:S(2)}, u32[]{:S(2)}) collective-permute-start(f32[136,128]{1,0:T(8,128)S(1)} %add.170), channel_id=1, source_target_pairs={{0,3},{1,2},{2,1},{3,0},{4,7},{5,6},{6,5},{7,4},{8,11},{9,10},{10,... | collective-permute-start | bytes 208904 | tf_op jit(solution)/shard_map/ppermute | solution.py:79
  137.3 4.3 %collective-permute-start.13 = (f32[136,128]{1,0:T(8,128)S(1)}, f32[136,128]{1,0:T(8,128)S(1)}, u32[]{:S(2)}, u32[]{:S(2)}) collective-permute-start(f32[136,128]{1,0:T(8,128)S(1)} %add.170), channel_id=1, source_target_pairs={{0,1},{1,0},{2,3},{3,2},{4,5},{5,4},{6,7},{7,6},{8,9},{9,8},{10,11... | collective-permute-start | bytes 208904 | tf_op jit(solution)/shard_map/ppermute | solution.py:79
  141.7 6.0 %collective-permute-start.17 = (f32[136,128]{1,0:T(8,128)S(1)}, f32[136,128]{1,0:T(8,128)S(1)}, u32[]{:S(2)}, u32[]{:S(2)}) collective-permute-start(f32[136,128]{1,0:T(8,128)S(1)} %add_add_fusion.1), channel_id=1, source_target_pairs={{0,8},{1,9},{2,10},{3,11},{4,12},{5,13},{6,14},{7,15},{8,0},{9,1},... | collective-permute-start | bytes 208904 | tf_op jit(solution)/shard_map/ppermute | solution.py:79
  145.0 5.5 %collective-permute-start.18 = (f32[136,128]{1,0:T(8,128)S(1)}, f32[136,128]{1,0:T(8,128)S(1)}, u32[]{:S(2)}, u32[]{:S(2)}) collective-permute-start(f32[136,128]{1,0:T(8,128)S(1)} %add_add_fusion.1), channel_id=1, source_target_pairs={{0,12},{1,13},{2,14},{3,15},{4,8},{5,9},{6,10},{7,11},{8,4},{9,5},... | collective-permute-start | bytes 208904 | tf_op jit(solution)/shard_map/ppermute | solution.py:79
  146.0 4.5 %collective-permute-start.16 = (f32[136,128]{1,0:T(8,128)S(1)}, f32[136,128]{1,0:T(8,128)S(1)}, u32[]{:S(2)}, u32[]{:S(2)}) collective-permute-start(f32[136,128]{1,0:T(8,128)S(1)} %add_add_fusion.1), channel_id=1, source_target_pairs={{0,4},{1,5},{2,6},{3,7},{4,0},{5,1},{6,2},{7,3},{8,12},{9,13},{10,... | collective-permute-start | bytes 208904 | tf_op jit(solution)/shard_map/ppermute | solution.py:79
  150.5 1.6 collective-permute-start.19
  168.1 6.2 %copy-start.4 = (f32[256,256]{1,0:T(8,128)}, f32[256,256]{1,0:T(8,128)S(1)}, u32[]{:S(2)}) copy-start(f32[256,256]{1,0:T(8,128)S(1)} %fusion.28) | copy-start | bytes 786436

commit v7 on v6

--- a/solution.py
+++ b/solution.py
@@ -1,6 +1,8 @@
 import jax
 import jax.numpy as jnp
 from jax import lax
+from jax.experimental import pallas as pl
+from jax.experimental.pallas import tpu as pltpu
 from jax.sharding import PartitionSpec as P
 
 
@@ -52,20 +54,67 @@
     return lat_sum
 
 
-def smooth(pieces, lat_taps, elev_taps, lat_count, elev_count):
+def edge_smooth_kernel(lat_ref, elev_ref, middle_ref, left_ref, right_ref, out_ref):
+    lat_taps = [lat_ref[i] for i in range(7)]
+    elev_taps = [elev_ref[i] for i in range(7)]
+    lat_count, elev_count = out_ref.shape[0], out_ref.shape[1]
+
+    def side_rows(side_ref):
+        rows = [side_ref[k].astype(jnp.float32) for k in range(side_ref.shape[0])]
+        sums = []
+        for l in range(lat_count):
+            total = lat_taps[0] * rows[l]
+            for i in range(1, 7):
+                total = total + lat_taps[i] * rows[l + i]
+            sums.append(total)
+        return sums
+
+    left = side_rows(left_ref)
+    right = side_rows(right_ref)
+    width = left_ref.shape[1]
+    for l in range(lat_count):
+        columns = [left[l][k] for k in range(width)]
+        columns += [middle_ref[l, k] for k in range(elev_count)]
+        columns += [right[l][k] for k in range(width)]
+        for e in range(elev_count):
+            total = elev_taps[0] * columns[e]
+            for j in range(1, 7):
+                total = total + elev_taps[j] * columns[e + j]
+            out_ref[l, e] = total.astype(out_ref.dtype)
+
+
+def edge_smooth(middle, left, right, lat_taps, elev_taps, tile=16):
+    lat_count, elev_count, depth, columns = middle.shape
+    tile = tile if depth % tile == 0 else depth
+    rows, width = left.shape[0], left.shape[1]
+    smem = pl.BlockSpec(memory_space=pltpu.SMEM)
+    return pl.pallas_call(
+        edge_smooth_kernel,
+        out_shape=jax.ShapeDtypeStruct(middle.shape, jnp.bfloat16),
+        grid=(depth // tile,),
+        in_specs=[
+            smem,
+            smem,
+            pl.BlockSpec((lat_count, elev_count, tile, columns), lambda k: (0, 0, k, 0)),
+            pl.BlockSpec((rows, width, tile, columns), lambda k: (0, 0, k, 0)),
+            pl.BlockSpec((rows, width, tile, columns), lambda k: (0, 0, k, 0)),
+        ],
+        out_specs=pl.BlockSpec((lat_count, elev_count, tile, columns), lambda k: (0, 0, k, 0)),
+        interpret=INTERPRET,
+    )(lat_taps, elev_taps, middle, left, right)
+
+
+INTERPRET = False
+
+
+def smooth(pieces, lat_taps, elev_taps, lat_count):
     left, center, right = pieces
     middle = lat_pass(center, lat_taps, lat_count)
-    lat_sum = jnp.concatenate(
-        [lat_pass(left, lat_taps, lat_count), middle, lat_pass(right, lat_taps, lat_count)], axis=1
-    )
-    result = elev_taps[0] * lat_sum[:, 0:elev_count]
-    for index_tap in range(1, 7):
-        result = result + elev_taps[index_tap] * lat_sum[:, index_tap : index_tap + elev_count]
-    return result
-
-
-def filtered_rows(pieces, lat_taps, elev_taps, matrix, lat_count, elev_count):
-    smoothed = smooth(pieces, lat_taps, elev_taps, lat_count, elev_count).astype(jnp.bfloat16)
+    return edge_smooth(middle, left, right, lat_taps, elev_taps)
+
+
+def filtered_rows(pieces, lat_taps, elev_taps, matrix, lat_count):
+    smoothed = smooth(pieces, lat_taps, elev_taps, lat_count)
     flat_rows = smoothed.reshape(-1, matrix.shape[0])
     return jnp.dot(flat_rows, matrix, preferred_element_type=jnp.float32).astype(jnp.bfloat16)
 
@@ -166,7 +215,7 @@
     lat_count, elev_count, depth, columns = volume.shape
     matrix = time_matrix(time_taps, columns // 2)
     extended = halo_pieces(volume, 3)
-    row_block = filtered_rows(extended, lat_taps, elev_taps, matrix, lat_count, elev_count)
+    row_block = filtered_rows(extended, lat_taps, elev_taps, matrix, lat_count)
     local_gram = lax.dot_general(
         row_block, row_block, (((0,), (0,)), ((), ())), preferred_element_type=jnp.float32
     )

time: 177 us -> 160 us (0.904)
  other arithmetic: 45.1 us -> 20.7 us
  Pallas kernels: 0 us -> 11.8 us
  local copies, waits for them, and re-layouts: 16.9 us -> 10.8 us
  waiting for transfers between devices: 42 us -> 44.5 us
    add x3 -> x1, other arithmetic: 27.8 us -> 11.5 us  [lat_pass(): lat_sum + lat_taps[index_tap] * extended[index_tap:index_tap + lat_count]...]
    convert_element_type x1 -> x0, other arithmetic: 14.5 us -> none  [filtered_rows(): smooth(pieces, lat_taps, elev_taps, lat_count, elev_count)]
    pallas_call x0 -> x1, Pallas kernels: none -> 11.8 us  [edge_smooth(): pl.pallas_call(edge_smooth_kernel, out_shape=jax.ShapeDtypeStruct(middle....]
    concatenate x0 -> x2, other arithmetic: none -> 6.33 us  [the longest x1 3.18 us: halo_pieces(): right = jnp.concatenate([north_east, east, south_east], axis=0)]
    concatenate x4 -> x0, local copies, waits for them, and re-layouts: 3.3 us -> none  [the longest x2 1.72 us: halo_pieces(): left = jnp.concatenate([north_west, west, south_west], axis=0)]
    unnamed x23 -> x11, local copies, waits for them, and re-layouts: 3.08 us -> 0.84 us
  transfers between devices with their start and end apart: 20 -> 20, of which waited for: 9 -> 11; matrix products, arithmetic and copies ran while one was open for 18% -> 14% of each run, Pallas kernels for 0% -> 0%
where the time goes in v7:
time: 160 us; the launch traced here: 157 us
  waiting for transfers between devices  44.5 us (28%)
  starting transfers between devices  42.5 us (27%)
  matrix products  23.9 us (15%)
  other arithmetic  20.7 us (13%)
  Pallas kernels  11.8 us (7%)
  local copies, waits for them, and re-layouts  10.8 us (7%)
  between operations  2.3 us (1%)
    ppermute x8, waiting for transfers between devices, shift(): return lax.ppermute(piece, axis, pairs)  26.4 us
    ppermute x10, starting transfers between devices, butterfly_sum(): lax.ppermute(block, axis, [(i, i ^ mask) for i in range(count)])  22.3 us
    ppermute x8, starting transfers between devices, shift(): return lax.ppermute(piece, axis, pairs)  18.5 us
    ppermute x10, waiting for transfers between devices, butterfly_sum(): lax.ppermute(block, axis, [(i, i ^ mask) for i in range(count)])  16 us
    pallas_call x1, Pallas kernels, edge_smooth(): pl.pallas_call(edge_smooth_kernel, out_shape=jax.ShapeDtypeStruct(middle....  11.8 us
    add x1, other arithmetic, lat_pass(): lat_sum + lat_taps[index_tap] * extended[index_tap:index_tap + lat_count]...  11.5 us
    dot_general x9, matrix products, refine(): jnp.einsum('bij,bjk->bik', shifted, inverse, precision=lax.Precision.HIGH...  6.83 us
    dot_general x9, matrix products, refine(): jnp.einsum('bij,bjk->bik', inverse, product, precision=lax.Precision.HIGH...  6.22 us
  transfers between devices with their start and end apart: 20, of which 11 were waited for; matrix products, arithmetic and copies ran while one was open for 14% of the time, Pallas kernels for 0%

profile of v7, /device:TPU:2, one launch (start us, length us, event | category | flops | bytes accessed | tf_op | source)
XLA Modules:
  0.0 156.8 jit_solution(1686919283361346443)
XLA Ops:
  0.6 2.2 %fusion.20 = (bf16[8,3,128,256]{3,2,1,0:T(8,128)(2,1)S(1)}, bf16[8,3,128,256]{3,2,1,0:T(8,128)(2,1)S(1)}) fusion(bf16[8,8,128,256]{3,2,1,0:T(8,128)(2,1)} %param.8), kind=kLoop, calls=%fused_computation.64 | loop fusion | bytes 6291456 | tf_op jit(solution)/shard_map/slice | solution.py:24
  2.9 3.4 %collective-permute-start.2 = (bf16[8,3,128,256]{3,2,1,0:T(8,128)(2,1)S(1)}, bf16[8,3,128,256]{3,2,1,0:T(8,128)(2,1)S(1)}, u32[]{:S(2)}, u32[]{:S(2)}) collective-permute-start(bf16[8,3,128,256]{3,2,1,0:T(8,128)(2,1)S(1)} %get-tuple-element.61), channel_id=1, source_target_pairs={{0,1},{1,2},{2,3},{3,4},{4,5},{5,6},{6,7},{7,8},{8,9},{9,10},{10,1... | collective-permute-start | bytes 4718600 | tf_op jit(solution)/shard_map/ppermute | solution.py:19
  6.3 2.5 %collective-permute-start.5 = (bf16[8,3,128,256]{3,2,1,0:T(8,128)(2,1)S(1)}, bf16[8,3,128,256]{3,2,1,0:T(8,128)(2,1)S(1)}, u32[]{:S(2)}, u32[]{:S(2)}) collective-permute-start(bf16[8,3,128,256]{3,2,1,0:T(8,128)(2,1)S(1)} %get-tuple-element.60), channel_id=1, source_target_pairs={{1,0},{2,1},{3,2},{4,3},{5,4},{6,5},{7,6},{8,7},{9,8},{10,9},{11,1... | collective-permute-start | bytes 4718600 | tf_op jit(solution)/shard_map/ppermute | solution.py:19
  8.9 1.4 fusion.21
  10.3 1.4 collective-permute-start
  11.7 1.3 collective-permute-start.1
  14.6 26.3 %collective-permute-done.2 = bf16[8,3,128,256]{3,2,1,0:T(8,128)(2,1)S(1)} collective-permute-done((bf16[8,3,128,256]{3,2,1,0:T(8,128)(2,1)S(1)}, bf16[8,3,128,256]{3,2,1,0:T(8,128)(2,1)S(1)}, u32[]{:S(2)}, u32[]{:S(2)}) %collective-permute-start.2) | collective-permute-done | bytes 1572896 | tf_op jit(solution)/shard_map/ppermute | solution.py:19
  42.1 2.1 %collective-permute-start.3 = (bf16[3,3,128,256]{3,2,1,0:T(8,128)(2,1)}, bf16[3,3,128,256]{3,2,1,0:T(8,128)(2,1)}, u32[]{:S(2)}, u32[]{:S(2)}) collective-permute-start(bf16[3,3,128,256]{3,2,1,0:T(8,128)(2,1)} %get-tuple-element.68), channel_id=1, source_target_pairs={{0,16},{16,32},{32,48},{48,64},{64,80},{80,96},{96,112},{112,128},... | collective-permute-start | bytes 1769480 | tf_op jit(solution)/shard_map/ppermute | solution.py:19
  44.2 1.3 collective-permute-start.4
  46.7 5.2 %collective-permute-start.6 = (bf16[3,3,128,256]{3,2,1,0:T(8,128)(2,1)}, bf16[3,3,128,256]{3,2,1,0:T(8,128)(2,1)}, u32[]{:S(2)}, u32[]{:S(2)}) collective-permute-start(bf16[3,3,128,256]{3,2,1,0:T(8,128)(2,1)} %get-tuple-element.66), channel_id=1, source_target_pairs={{0,16},{16,32},{32,48},{48,64},{64,80},{80,96},{96,112},{112,128},... | collective-permute-start | bytes 1769480 | tf_op jit(solution)/shard_map/ppermute | solution.py:19
  51.9 1.3 collective-permute-start.7
  54.5 11.5 %multiply_add_fusion.middle_ref = f32[8,8,128,256]{3,2,1,0:T(8,128)} fusion(bf16[8,8,128,256]{3,2,1,0:T(8,128)(2,1)S(1)} %copy-done.1, bf16[11,8,128,256]{3,2,1,0:T(8,128)(2,1)S(1)} %constant_dynamic-update-slice_fusion.2, bf16[11,8,128,256]{3,2,1,0:T(8,128)(2,1)S(1)} %get-tuple-element.62, f32[]{:T(128)} %bitcast.6, f32[]{:T(128)} %bitcast.5, f32[]{:T(128)} %bitcast.4, ...), kind=kLoop, calls=%fused_computation.17 | loop fusion | flops 41943040 | bytes 37748764 | tf_op jit(solution)/shard_map/add | solution.py:51
  66.1 3.2 %pad_maximum_fusion.left_ref = bf16[14,3,128,256]{3,2,1,0:T(8,128)(2,1)} fusion(bf16[3,3,128,256]{3,2,1,0:T(8,128)(2,1)} %collective-permute-done.4, bf16[8,3,128,256]{3,2,1,0:T(8,128)(2,1)S(1)} %collective-permute-done.2, bf16[3,3,128,256]{3,2,1,0:T(8,128)(2,1)} %collective-permute-done.3), kind=kLoop, calls=%fused_computation.18 | loop fusion | flops 2752512 | bytes 5505024 | tf_op jit(solution)/shard_map/concatenate | solution.py:30
  69.2 3.2 %pad_maximum_fusion.1.right_ref = bf16[14,3,128,256]{3,2,1,0:T(8,128)(2,1)} fusion(bf16[3,3,128,256]{3,2,1,0:T(8,128)(2,1)} %collective-permute-done.7, bf16[8,3,128,256]{3,2,1,0:T(8,128)(2,1)S(1)} %collective-permute-done.5, bf16[3,3,128,256]{3,2,1,0:T(8,128)(2,1)} %collective-permute-done.6), kind=kLoop, calls=%fused_computation.19 | loop fusion | flops 2752512 | bytes 5505024 | tf_op jit(solution)/shard_map/concatenate | solution.py:31
  72.4 11.8 %shard_map.85 = bf16[8,8,128,256]{3,2,1,0:T(8,128)(2,1)} custom-call(f32[7]{0:T(128)} %lat_ref.1, f32[7]{0:T(128)} %elev_ref.1, f32[8,8,128,256]{3,2,1,0:T(8,128)} %multiply_add_fusion.middle_ref, bf16[14,3,128,256]{3,2,1,0:T(8,128)(2,1)} %pad_maximum_fusion.left_ref, bf16[14,3,128,256]{3,2,1,0:T(8,128)(2,1)} %pad_maximum_fusion.1.right_ref), custom_call_target="tpu_custom_call" | custom-call | tf_op jit(solution)/shard_map/pallas_call | solution.py:91
  84.2 3.4 %convolution_convert_fusion.1 = bf16[8192,256]{1,0:T(8,128)(2,1)S(1)} fusion(bf16[8192,256]{1,0:T(8,128)(2,1)} %bitcast.54, bf16[32,8,2,128]{3,2,1,0:T(2,128)(2,1)S(1)} %bitcast.55), kind=kOutput, calls=%fused_computation.15 | convolution fusion | flops 1075838976 | bytes 8519680 | tf_op jit(solution)/shard_map/dot_general | solution.py:119
  87.6 1.3 fusion.27
  90.9 1.7 %collective-permute-start.8 = (f32[272,128]{1,0:T(8,128)S(1)}, f32[272,128]{1,0:T(8,128)S(1)}, u32[]{:S(2)}, u32[]{:S(2)}) collective-permute-start(f32[272,128]{1,0:T(8,128)S(1)} %select_maximum_fusion), channel_id=1, source_target_pairs={{0,16},{16,0},{32,48},{48,32},{64,80},{80,64},{96,112},{112,96},{1... | collective-permute-start | bytes 417800 | tf_op jit(solution)/shard_map/ppermute | solution.py:155
  93.6 3.4 %collective-permute-start.10 = (f32[136,128]{1,0:T(8,128)S(1)}, f32[136,128]{1,0:T(8,128)S(1)}, u32[]{:S(2)}, u32[]{:S(2)}) collective-permute-start(f32[136,128]{1,0:T(8,128)S(1)} %dynamic-slice_add_fusion), channel_id=1, source_target_pairs={{0,64},{16,80},{32,96},{48,112},{64,0},{80,16},{96,32},{112,48},{1... | collective-permute-start | bytes 208904 | tf_op jit(solution)/shard_map/ppermute | solution.py:128
  97.0 3.8 %collective-permute-start.11 = (f32[136,128]{1,0:T(8,128)S(1)}, f32[136,128]{1,0:T(8,128)S(1)}, u32[]{:S(2)}, u32[]{:S(2)}) collective-permute-start(f32[136,128]{1,0:T(8,128)S(1)} %dynamic-slice_add_fusion), channel_id=1, source_target_pairs={{0,96},{16,112},{32,64},{48,80},{64,32},{80,48},{96,0},{112,16},{1... | collective-permute-start | bytes 208904 | tf_op jit(solution)/shard_map/ppermute | solution.py:128
  101.3 4.0 %collective-permute-done.11 = f32[136,128]{1,0:T(8,128)S(1)} collective-permute-done((f32[136,128]{1,0:T(8,128)S(1)}, f32[136,128]{1,0:T(8,128)S(1)}, u32[]{:S(2)}, u32[]{:S(2)}) %collective-permute-start.11) | collective-permute-done | bytes 69664 | tf_op jit(solution)/shard_map/ppermute | solution.py:128
  106.3 5.3 %collective-permute-start.12 = (f32[136,128]{1,0:T(8,128)S(1)}, f32[136,128]{1,0:T(8,128)S(1)}, u32[]{:S(2)}, u32[]{:S(2)}) collective-permute-start(f32[136,128]{1,0:T(8,128)S(1)} %add_add_fusion.2), channel_id=1, source_target_pairs={{0,128},{16,144},{32,160},{48,176},{64,192},{80,208},{96,224},{112... | collective-permute-start | bytes 208904 | tf_op jit(solution)/shard_map/ppermute | solution.py:128
  111.6 3.0 %collective-permute-done.12 = f32[136,128]{1,0:T(8,128)S(1)} collective-permute-done((f32[136,128]{1,0:T(8,128)S(1)}, f32[136,128]{1,0:T(8,128)S(1)}, u32[]{:S(2)}, u32[]{:S(2)}) %collective-permute-start.12) | collective-permute-done | bytes 69664 | tf_op jit(solution)/shard_map/ppermute | solution.py:128
  114.7 2.9 %collective-permute-start.14 = (f32[136,128]{1,0:T(8,128)S(1)}, f32[136,128]{1,0:T(8,128)S(1)}, u32[]{:S(2)}, u32[]{:S(2)}) collective-permute-start(f32[136,128]{1,0:T(8,128)S(1)} %add.98), channel_id=1, source_target_pairs={{0,2},{1,3},{2,0},{3,1},{4,6},{5,7},{6,4},{7,5},{8,10},{9,11},{10,... | collective-permute-start | bytes 208904 | tf_op jit(solution)/shard_map/ppermute | solution.py:128
  118.2 1.4 collective-permute-done.13
  120.7 1.3 collective-permute-done.15
  122.0 2.9 %collective-permute-start.16 = (f32[136,128]{1,0:T(8,128)S(1)}, f32[136,128]{1,0:T(8,128)S(1)}, u32[]{:S(2)}, u32[]{:S(2)}) collective-permute-start(f32[136,128]{1,0:T(8,128)S(1)} %add_add_fusion.1), channel_id=1, source_target_pairs={{0,4},{1,5},{2,6},{3,7},{4,0},{5,1},{6,2},{7,3},{8,12},{9,13},{10,... | collective-permute-start | bytes 208904 | tf_op jit(solution)/shard_map/ppermute | solution.py:128
  124.8 2.9 %collective-permute-start.17 = (f32[136,128]{1,0:T(8,128)S(1)}, f32[136,128]{1,0:T(8,128)S(1)}, u32[]{:S(2)}, u32[]{:S(2)}) collective-permute-start(f32[136,128]{1,0:T(8,128)S(1)} %add_add_fusion.1), channel_id=1, source_target_pairs={{0,8},{1,9},{2,10},{3,11},{4,12},{5,13},{6,14},{7,15},{8,0},{9,1},... | collective-permute-start | bytes 208904 | tf_op jit(solution)/shard_map/ppermute | solution.py:128
  129.1 1.7 %collective-permute-done.17 = f32[136,128]{1,0:T(8,128)S(1)} collective-permute-done((f32[136,128]{1,0:T(8,128)S(1)}, f32[136,128]{1,0:T(8,128)S(1)}, u32[]{:S(2)}, u32[]{:S(2)}) %collective-permute-start.17) | collective-permute-done | bytes 69664 | tf_op jit(solution)/shard_map/ppermute | solution.py:128
  130.8 2.5 %collective-permute-done.18 = f32[136,128]{1,0:T(8,128)S(1)} collective-permute-done((f32[136,128]{1,0:T(8,128)S(1)}, f32[136,128]{1,0:T(8,128)S(1)}, u32[]{:S(2)}, u32[]{:S(2)}) %collective-permute-start.18) | collective-permute-done | bytes 69664 | tf_op jit(solution)/shard_map/ppermute | solution.py:128
  136.4 13.9 %while.13 = (s32[]{:T(128)}, f32[2,256,256]{1,2,0:T(8,128)S(1)}, f32[2]{0:T(128)S(1)}, f32[256,256]{1,0:T(8,128)S(1)}, f32[2]{0:T(128)S(1)}, /*index=5*/f32[256,256]{1,0:T(8,128)S(1)}, s32[]{:T(128)}) while((s32[]{:T(128)}, f32[2,256,256]{1,2,0:T(8,128)S(1)}, f32[2]{0:T(128)S(1)}, f32[256,256]{1,0:T(8,128)S(1)}, f32[2]{0:T(128)S(1)}, ...), condition=%wide.region_3.4_spmd.clone, body=%wide.region_2.3_spmd.clone.sunk | while | flops 805961728 | bytes 4194421 | solution.py:209
  150.6 6.2 %multiply_reduce_fusion = (f32[8192]{0:T(1024)}, bf16[8192,256]{1,0:T(8,128)(2,1)}) fusion(bf16[8192,256]{1,0:T(8,128)(2,1)} %copy-done, f32[256,256]{1,0:T(8,128)S(1)} %fusion.11), kind=kOutput, calls=%fused_computation.16 | convolution fusion | flops 1082187776 | bytes 8683520 | tf_op jit(solution)/shard_map/dot_general | solution.py:224
  (98 shorter events, 28.5 us)
Async XLA Ops:
  0.6 8.2 %copy-start.1 = (bf16[8,8,128,256]{3,2,1,0:T(8,128)(2,1)S(1)}, bf16[8,8,128,256]{3,2,1,0:T(8,128)(2,1)}, u32[]{:S(2)}) copy-start(bf16[8,8,128,256]{3,2,1,0:T(8,128)(2,1)} %param.8) | copy-start | bytes 12582916
  2.9 10.1 %copy-start.3 = (f32[7]{0:T(128)S(1)}, f32[7]{0:T(128)}, u32[]{:S(2)}) copy-start(f32[7]{0:T(128)} %lat_ref.1) | copy-start | bytes 88
  2.9 10.8 %copy-start.4 = (bf16[32]{0:T(256)(128)(2,1)S(1)}, bf16[32]{0:T(256)(128)(2,1)}, u32[]{:S(2)}) copy-start(bf16[32]{0:T(256)(128)(2,1)} %param.11) | copy-start | bytes 196
  2.9 38.0 %collective-permute-start.2 = (bf16[8,3,128,256]{3,2,1,0:T(8,128)(2,1)S(1)}, bf16[8,3,128,256]{3,2,1,0:T(8,128)(2,1)S(1)}, u32[]{:S(2)}, u32[]{:S(2)}) collective-permute-start(bf16[8,3,128,256]{3,2,1,0:T(8,128)(2,1)S(1)} %get-tuple-element.61), channel_id=1, source_target_pairs={{0,1},{1,2},{2,3},{3,4},{4,5},{5,6},{6,7},{7,8},{8,9},{9,10},{10,1... | collective-permute-start | bytes 4718600 | tf_op jit(solution)/shard_map/ppermute | solution.py:19
  6.3 39.2 %collective-permute-start.5 = (bf16[8,3,128,256]{3,2,1,0:T(8,128)(2,1)S(1)}, bf16[8,3,128,256]{3,2,1,0:T(8,128)(2,1)S(1)}, u32[]{:S(2)}, u32[]{:S(2)}) collective-permute-start(bf16[8,3,128,256]{3,2,1,0:T(8,128)(2,1)S(1)} %get-tuple-element.60), channel_id=1, source_target_pairs={{1,0},{2,1},{3,2},{4,3},{5,4},{6,5},{7,6},{8,7},{9,8},{10,9},{11,1... | collective-permute-start | bytes 4718600 | tf_op jit(solution)/shard_map/ppermute | solution.py:19
  10.3 41.6 %collective-permute-start = (bf16[3,8,128,256]{3,2,1,0:T(8,128)(2,1)S(1)}, bf16[3,8,128,256]{3,2,1,0:T(8,128)(2,1)S(1)}, u32[]{:S(2)}, u32[]{:S(2)}) collective-permute-start(bf16[3,8,128,256]{3,2,1,0:T(8,128)(2,1)S(1)} %get-tuple-element.64), channel_id=1, source_target_pairs={{0,16},{16,32},{32,48},{48,64},{64,80},{80,96},{96,112},{112,128},... | collective-permute-start | bytes 4718600 | tf_op jit(solution)/shard_map/ppermute | solution.py:19
  11.7 42.7 %collective-permute-start.1 = (bf16[3,8,128,256]{3,2,1,0:T(8,128)(2,1)}, bf16[3,8,128,256]{3,2,1,0:T(8,128)(2,1)S(1)}, u32[]{:S(2)}, u32[]{:S(2)}) collective-permute-start(bf16[3,8,128,256]{3,2,1,0:T(8,128)(2,1)} %get-tuple-element.65), channel_id=1, source_target_pairs={{16,0},{32,16},{48,32},{64,48},{80,64},{96,80},{112,96},{128,112},... | collective-permute-start | bytes 4718600 | tf_op jit(solution)/shard_map/ppermute | solution.py:19
  42.1 24.0 %collective-permute-start.3 = (bf16[3,3,128,256]{3,2,1,0:T(8,128)(2,1)}, bf16[3,3,128,256]{3,2,1,0:T(8,128)(2,1)}, u32[]{:S(2)}, u32[]{:S(2)}) collective-permute-start(bf16[3,3,128,256]{3,2,1,0:T(8,128)(2,1)} %get-tuple-element.68), channel_id=1, source_target_pairs={{0,16},{16,32},{32,48},{48,64},{64,80},{80,96},{96,112},{112,128},... | collective-permute-start | bytes 1769480 | tf_op jit(solution)/shard_map/ppermute | solution.py:19
  44.2 21.9 %collective-permute-start.4 = (bf16[3,3,128,256]{3,2,1,0:T(8,128)(2,1)}, bf16[3,3,128,256]{3,2,1,0:T(8,128)(2,1)}, u32[]{:S(2)}, u32[]{:S(2)}) collective-permute-start(bf16[3,3,128,256]{3,2,1,0:T(8,128)(2,1)} %get-tuple-element.69), channel_id=1, source_target_pairs={{16,0},{32,16},{48,32},{64,48},{80,64},{96,80},{112,96},{128,112},... | collective-permute-start | bytes 1769480 | tf_op jit(solution)/shard_map/ppermute | solution.py:19
  46.7 22.5 %collective-permute-start.6 = (bf16[3,3,128,256]{3,2,1,0:T(8,128)(2,1)}, bf16[3,3,128,256]{3,2,1,0:T(8,128)(2,1)}, u32[]{:S(2)}, u32[]{:S(2)}) collective-permute-start(bf16[3,3,128,256]{3,2,1,0:T(8,128)(2,1)} %get-tuple-element.66), channel_id=1, source_target_pairs={{0,16},{16,32},{32,48},{48,64},{64,80},{80,96},{96,112},{112,128},... | collective-permute-start | bytes 1769480 | tf_op jit(solution)/shard_map/ppermute | solution.py:19
  51.9 17.4 %collective-permute-start.7 = (bf16[3,3,128,256]{3,2,1,0:T(8,128)(2,1)}, bf16[3,3,128,256]{3,2,1,0:T(8,128)(2,1)}, u32[]{:S(2)}, u32[]{:S(2)}) collective-permute-start(bf16[3,3,128,256]{3,2,1,0:T(8,128)(2,1)} %get-tuple-element.67), channel_id=1, source_target_pairs={{16,0},{32,16},{48,32},{64,48},{80,64},{96,80},{112,96},{128,112},... | collective-permute-start | bytes 1769480 | tf_op jit(solution)/shard_map/ppermute | solution.py:19
  87.6 2.0 %copy-start = (bf16[8192,256]{1,0:T(8,128)(2,1)}, bf16[8192,256]{1,0:T(8,128)(2,1)S(1)}, u32[]{:S(2)}) copy-start(bf16[8192,256]{1,0:T(8,128)(2,1)S(1)} %convolution_convert_fusion.1) | copy-start | bytes 12582916
  90.9 2.7 %collective-permute-start.8 = (f32[272,128]{1,0:T(8,128)S(1)}, f32[272,128]{1,0:T(8,128)S(1)}, u32[]{:S(2)}, u32[]{:S(2)}) collective-permute-start(f32[272,128]{1,0:T(8,128)S(1)} %select_maximum_fusion), channel_id=1, source_target_pairs={{0,16},{16,0},{32,48},{48,32},{64,80},{80,64},{96,112},{112,96},{1... | collective-permute-start | bytes 417800 | tf_op jit(solution)/shard_map/ppermute | solution.py:155
  93.6 7.7 %collective-permute-start.10 = (f32[136,128]{1,0:T(8,128)S(1)}, f32[136,128]{1,0:T(8,128)S(1)}, u32[]{:S(2)}, u32[]{:S(2)}) collective-permute-start(f32[136,128]{1,0:T(8,128)S(1)} %dynamic-slice_add_fusion), channel_id=1, source_target_pairs={{0,64},{16,80},{32,96},{48,112},{64,0},{80,16},{96,32},{112,48},{1... | collective-permute-start | bytes 208904 | tf_op jit(solution)/shard_map/ppermute | solution.py:128
  97.0 8.2 %collective-permute-start.11 = (f32[136,128]{1,0:T(8,128)S(1)}, f32[136,128]{1,0:T(8,128)S(1)}, u32[]{:S(2)}, u32[]{:S(2)}) collective-permute-start(f32[136,128]{1,0:T(8,128)S(1)} %dynamic-slice_add_fusion), channel_id=1, source_target_pairs={{0,96},{16,112},{32,64},{48,80},{64,32},{80,48},{96,0},{112,16},{1... | collective-permute-start | bytes 208904 | tf_op jit(solution)/shard_map/ppermute | solution.py:128
  100.8 5.5 %collective-permute-start.9 = (f32[136,128]{1,0:T(8,128)S(1)}, f32[136,128]{1,0:T(8,128)S(1)}, u32[]{:S(2)}, u32[]{:S(2)}) collective-permute-start(f32[136,128]{1,0:T(8,128)S(1)} %dynamic-slice_add_fusion), channel_id=1, source_target_pairs={{0,32},{16,48},{32,0},{48,16},{64,96},{80,112},{96,64},{112,80},{1... | collective-permute-start | bytes 208904 | tf_op jit(solution)/shard_map/ppermute | solution.py:128
  106.3 8.3 %collective-permute-start.12 = (f32[136,128]{1,0:T(8,128)S(1)}, f32[136,128]{1,0:T(8,128)S(1)}, u32[]{:S(2)}, u32[]{:S(2)}) collective-permute-start(f32[136,128]{1,0:T(8,128)S(1)} %add_add_fusion.2), channel_id=1, source_target_pairs={{0,128},{16,144},{32,160},{48,176},{64,192},{80,208},{96,224},{112... | collective-permute-start | bytes 208904 | tf_op jit(solution)/shard_map/ppermute | solution.py:128
  114.6 4.9 %collective-permute-start.13 = (f32[136,128]{1,0:T(8,128)S(1)}, f32[136,128]{1,0:T(8,128)S(1)}, u32[]{:S(2)}, u32[]{:S(2)}) collective-permute-start(f32[136,128]{1,0:T(8,128)S(1)} %add.98), channel_id=1, source_target_pairs={{0,1},{1,0},{2,3},{3,2},{4,5},{5,4},{6,7},{7,6},{8,9},{9,8},{10,11... | collective-permute-start | bytes 208904 | tf_op jit(solution)/shard_map/ppermute | solution.py:128
  114.7 6.0 %collective-permute-start.14 = (f32[136,128]{1,0:T(8,128)S(1)}, f32[136,128]{1,0:T(8,128)S(1)}, u32[]{:S(2)}, u32[]{:S(2)}) collective-permute-start(f32[136,128]{1,0:T(8,128)S(1)} %add.98), channel_id=1, source_target_pairs={{0,2},{1,3},{2,0},{3,1},{4,6},{5,7},{6,4},{7,5},{8,10},{9,11},{10,... | collective-permute-start | bytes 208904 | tf_op jit(solution)/shard_map/ppermute | solution.py:128
  117.6 4.3 %collective-permute-start.15 = (f32[136,128]{1,0:T(8,128)S(1)}, f32[136,128]{1,0:T(8,128)S(1)}, u32[]{:S(2)}, u32[]{:S(2)}) collective-permute-start(f32[136,128]{1,0:T(8,128)S(1)} %add.98), channel_id=1, source_target_pairs={{0,3},{1,2},{2,1},{3,0},{4,7},{5,6},{6,5},{7,4},{8,11},{9,10},{10,... | collective-permute-start | bytes 208904 | tf_op jit(solution)/shard_map/ppermute | solution.py:128
  122.0 7.1 %collective-permute-start.16 = (f32[136,128]{1,0:T(8,128)S(1)}, f32[136,128]{1,0:T(8,128)S(1)}, u32[]{:S(2)}, u32[]{:S(2)}) collective-permute-start(f32[136,128]{1,0:T(8,128)S(1)} %add_add_fusion.1), channel_id=1, source_target_pairs={{0,4},{1,5},{2,6},{3,7},{4,0},{5,1},{6,2},{7,3},{8,12},{9,13},{10,... | collective-permute-start | bytes 208904 | tf_op jit(solution)/shard_map/ppermute | solution.py:128
  124.8 5.9 %collective-permute-start.17 = (f32[136,128]{1,0:T(8,128)S(1)}, f32[136,128]{1,0:T(8,128)S(1)}, u32[]{:S(2)}, u32[]{:S(2)}) collective-permute-start(f32[136,128]{1,0:T(8,128)S(1)} %add_add_fusion.1), channel_id=1, source_target_pairs={{0,8},{1,9},{2,10},{3,11},{4,12},{5,13},{6,14},{7,15},{8,0},{9,1},... | collective-permute-start | bytes 208904 | tf_op jit(solution)/shard_map/ppermute | solution.py:128
  127.7 5.5 %collective-permute-start.18 = (f32[136,128]{1,0:T(8,128)S(1)}, f32[136,128]{1,0:T(8,128)S(1)}, u32[]{:S(2)}, u32[]{:S(2)}) collective-permute-start(f32[136,128]{1,0:T(8,128)S(1)} %add_add_fusion.1), channel_id=1, source_target_pairs={{0,12},{1,13},{2,14},{3,15},{4,8},{5,9},{6,10},{7,11},{8,4},{9,5},... | collective-permute-start | bytes 208904 | tf_op jit(solution)/shard_map/ppermute | solution.py:128
  133.3 1.3 collective-permute-start.19
  150.6 6.2 %copy-start.2 = (f32[256,256]{1,0:T(8,128)}, f32[256,256]{1,0:T(8,128)S(1)}, u32[]{:S(2)}) copy-start(f32[256,256]{1,0:T(8,128)S(1)} %fusion.11) | copy-start | bytes 786436

commit v8 on v7

--- a/solution.py
+++ b/solution.py
@@ -27,8 +27,8 @@
     south_west = shift(west[high_lat], "lat", -1)
     south_east = shift(east[high_lat], "lat", -1)
     center = jnp.concatenate([north, block, south], axis=0)
-    left = jnp.concatenate([north_west, west, south_west], axis=0)
-    right = jnp.concatenate([north_east, east, south_east], axis=0)
+    left = (north_west, west, south_west)
+    right = (north_east, east, south_east)
     return left, center, right
 
 
@@ -54,13 +54,15 @@
     return lat_sum
 
 
-def edge_smooth_kernel(lat_ref, elev_ref, middle_ref, left_ref, right_ref, out_ref):
+def edge_smooth_kernel(lat_ref, elev_ref, middle_ref, *refs):
+    out_ref = refs[-1]
+    left_refs, right_refs = refs[0:3], refs[3:6]
     lat_taps = [lat_ref[i] for i in range(7)]
     elev_taps = [elev_ref[i] for i in range(7)]
     lat_count, elev_count = out_ref.shape[0], out_ref.shape[1]
 
-    def side_rows(side_ref):
-        rows = [side_ref[k].astype(jnp.float32) for k in range(side_ref.shape[0])]
+    def side_rows(side_refs):
+        rows = [ref[k].astype(jnp.float32) for ref in side_refs for k in range(ref.shape[0])]
         sums = []
         for l in range(lat_count):
             total = lat_taps[0] * rows[l]
@@ -69,9 +71,9 @@
             sums.append(total)
         return sums
 
-    left = side_rows(left_ref)
-    right = side_rows(right_ref)
-    width = left_ref.shape[1]
+    left = side_rows(left_refs)
+    right = side_rows(right_refs)
+    width = left_refs[0].shape[1]
     for l in range(lat_count):
         columns = [left[l][k] for k in range(width)]
         columns += [middle_ref[l, k] for k in range(elev_count)]
@@ -84,24 +86,22 @@
 
 
 def edge_smooth(middle, left, right, lat_taps, elev_taps, tile=16):
-    lat_count, elev_count, depth, columns = middle.shape
+    _, _, depth, columns = middle.shape
     tile = tile if depth % tile == 0 else depth
-    rows, width = left.shape[0], left.shape[1]
     smem = pl.BlockSpec(memory_space=pltpu.SMEM)
+
+    def tiled(piece):
+        return pl.BlockSpec((piece.shape[0], piece.shape[1], tile, columns), lambda k: (0, 0, k, 0))
+
+    sides = (*left, *right)
     return pl.pallas_call(
         edge_smooth_kernel,
         out_shape=jax.ShapeDtypeStruct(middle.shape, jnp.bfloat16),
         grid=(depth // tile,),
-        in_specs=[
-            smem,
-            smem,
-            pl.BlockSpec((lat_count, elev_count, tile, columns), lambda k: (0, 0, k, 0)),
-            pl.BlockSpec((rows, width, tile, columns), lambda k: (0, 0, k, 0)),
-            pl.BlockSpec((rows, width, tile, columns), lambda k: (0, 0, k, 0)),
-        ],
-        out_specs=pl.BlockSpec((lat_count, elev_count, tile, columns), lambda k: (0, 0, k, 0)),
+        in_specs=[smem, smem, tiled(middle), *[tiled(piece) for piece in sides]],
+        out_specs=tiled(middle),
         interpret=INTERPRET,
-    )(lat_taps, elev_taps, middle, left, right)
+    )(lat_taps, elev_taps, middle, *sides)
 
 
 INTERPRET = False
@@ -185,7 +185,7 @@
     )
 
 
-def band_filter(gram_sum, clutter_rank, noise_rank, steps=9):
+def band_filter(gram_sum, clutter_rank, noise_rank, steps=9, coarse_steps=5):
     width = gram_sum.shape[0]
     identity = jnp.eye(width, dtype=jnp.float32)
     total_trace = jnp.sum(gram_sum * identity)
@@ -195,18 +195,21 @@
     inverse = scale[:, None, None] * identity[None]
     low = scale * levels
 
-    def refine(_, carry):
-        inverse, low = carry
-        squeezed = low * (2.0 - low)
-        factor = 2.0 / (1.0 + squeezed)
-        product = jnp.einsum("bij,bjk->bik", shifted, inverse, precision=lax.Precision.HIGHEST)
-        inverse = factor[:, None, None] * (
-            2.0 * inverse
-            - jnp.einsum("bij,bjk->bik", inverse, product, precision=lax.Precision.HIGHEST)
-        )
-        return inverse, factor * squeezed
-
-    inverse, _ = lax.fori_loop(0, steps, refine, (inverse, low))
+    def refine(precision):
+        def step(_, carry):
+            inverse, low = carry
+            squeezed = low * (2.0 - low)
+            factor = 2.0 / (1.0 + squeezed)
+            product = jnp.einsum("bij,bjk->bik", shifted, inverse, precision=precision)
+            inverse = factor[:, None, None] * (
+                2.0 * inverse - jnp.einsum("bij,bjk->bik", inverse, product, precision=precision)
+            )
+            return inverse, factor * squeezed
+
+        return step
+
+    carry = lax.fori_loop(0, coarse_steps, refine(lax.Precision.HIGH), (inverse, low))
+    inverse, _ = lax.fori_loop(coarse_steps, steps, refine(lax.Precision.HIGHEST), carry)
     resolvents = levels[:, None, None] * inverse
     return resolvents[0] - resolvents[1]
 

time: 160 us -> 151 us (0.944)
  the two profiles are of different devices: /device:TPU:2 before, /device:TPU:1 now
where the time goes in v8:
time: 151 us; the launch traced here: 150 us
  starting transfers between devices  50.5 us (33%)
  waiting for transfers between devices  39 us (26%)
  matrix products  21.3 us (14%)
  other arithmetic  14.4 us (10%)
  Pallas kernels  11.8 us (8%)
  local copies, waits for them, and re-layouts  10.8 us (7%)
  between operations  2.36 us (2%)
    ppermute x8, starting transfers between devices, shift(): return lax.ppermute(piece, axis, pairs)  24 us
    ppermute x8, waiting for transfers between devices, shift(): return lax.ppermute(piece, axis, pairs)  22.3 us
    ppermute x10, starting transfers between devices, butterfly_sum(): lax.ppermute(block, axis, [(i, i ^ mask) for i in range(count)])  21.1 us
    ppermute x10, waiting for transfers between devices, butterfly_sum(): lax.ppermute(block, axis, [(i, i ^ mask) for i in range(count)])  14.6 us
    pallas_call x1, Pallas kernels, edge_smooth(): pl.pallas_call(edge_smooth_kernel, out_shape=jax.ShapeDtypeStruct(middle....  11.8 us
    add x1, other arithmetic, lat_pass(): lat_sum + lat_taps[index_tap] * extended[index_tap:index_tap + lat_count]...  11.5 us
    dot_general x1, matrix products, body(): jnp.dot(row_block, weights.astype(jnp.bfloat16), preferred_element_type=j...  6.17 us
    dot_general x9, matrix products, step(): product = jnp.einsum('bij,bjk->bik', shifted, inverse, precision=precision)  5.51 us
  transfers between devices with their start and end apart: 20, of which 10 were waited for; matrix products, arithmetic and copies ran while one was open for 12% of the time, Pallas kernels for 0%

profile of v8, /device:TPU:1, one launch (start us, length us, event | category | flops | bytes accessed | tf_op | source)
XLA Modules:
  0.0 150.5 jit_solution(168529049323080590)
XLA Ops:
  0.6 2.2 %fusion.31 = (bf16[8,3,128,256]{3,2,1,0:T(8,128)(2,1)S(1)}, bf16[8,3,128,256]{3,2,1,0:T(8,128)(2,1)S(1)}) fusion(bf16[8,8,128,256]{3,2,1,0:T(8,128)(2,1)} %param.10), kind=kLoop, calls=%fused_computation.75 | loop fusion | bytes 6291456 | tf_op jit(solution)/shard_map/slice | solution.py:24
  2.9 4.0 %collective-permute-start.2 = (bf16[8,3,128,256]{3,2,1,0:T(8,128)(2,1)S(1)}, bf16[8,3,128,256]{3,2,1,0:T(8,128)(2,1)S(1)}, u32[]{:S(2)}, u32[]{:S(2)}) collective-permute-start(bf16[8,3,128,256]{3,2,1,0:T(8,128)(2,1)S(1)} %get-tuple-element.117), channel_id=1, source_target_pairs={{0,1},{1,2},{2,3},{3,4},{4,5},{5,6},{6,7},{7,8},{8,9},{9,10},{10,1... | collective-permute-start | bytes 4718600 | tf_op jit(solution)/shard_map/ppermute | solution.py:19
  7.0 1.3 collective-permute-start.5
  8.3 1.4 fusion.32
  9.7 4.4 %collective-permute-start = (bf16[3,8,128,256]{3,2,1,0:T(8,128)(2,1)S(1)}, bf16[3,8,128,256]{3,2,1,0:T(8,128)(2,1)S(1)}, u32[]{:S(2)}, u32[]{:S(2)}) collective-permute-start(bf16[3,8,128,256]{3,2,1,0:T(8,128)(2,1)S(1)} %get-tuple-element.120), channel_id=1, source_target_pairs={{0,16},{16,32},{32,48},{48,64},{64,80},{80,96},{96,112},{112,128},... | collective-permute-start | bytes 4718600 | tf_op jit(solution)/shard_map/ppermute | solution.py:19
  14.1 1.9 %collective-permute-start.1 = (bf16[3,8,128,256]{3,2,1,0:T(8,128)(2,1)}, bf16[3,8,128,256]{3,2,1,0:T(8,128)(2,1)S(1)}, u32[]{:S(2)}, u32[]{:S(2)}) collective-permute-start(bf16[3,8,128,256]{3,2,1,0:T(8,128)(2,1)} %get-tuple-element.121), channel_id=1, source_target_pairs={{16,0},{32,16},{48,32},{64,48},{80,64},{96,80},{112,96},{128,112},... | collective-permute-start | bytes 4718600 | tf_op jit(solution)/shard_map/ppermute | solution.py:19
  17.6 22.3 %collective-permute-done.2.refs_1_ = bf16[8,3,128,256]{3,2,1,0:T(8,128)(2,1)S(1)} collective-permute-done((bf16[8,3,128,256]{3,2,1,0:T(8,128)(2,1)S(1)}, bf16[8,3,128,256]{3,2,1,0:T(8,128)(2,1)S(1)}, u32[]{:S(2)}, u32[]{:S(2)}) %collective-permute-start.2) | collective-permute-done | bytes 1572896 | tf_op jit(solution)/shard_map/ppermute | solution.py:19
  41.1 4.9 %collective-permute-start.3 = (bf16[3,3,128,256]{3,2,1,0:T(8,128)(2,1)}, bf16[3,3,128,256]{3,2,1,0:T(8,128)(2,1)}, u32[]{:S(2)}, u32[]{:S(2)}) collective-permute-start(bf16[3,3,128,256]{3,2,1,0:T(8,128)(2,1)} %get-tuple-element.125), channel_id=1, source_target_pairs={{0,16},{16,32},{32,48},{48,64},{64,80},{80,96},{96,112},{112,128},... | collective-permute-start | bytes 1769480 | tf_op jit(solution)/shard_map/ppermute | solution.py:19
  46.0 1.9 %collective-permute-start.4 = (bf16[3,3,128,256]{3,2,1,0:T(8,128)(2,1)}, bf16[3,3,128,256]{3,2,1,0:T(8,128)(2,1)}, u32[]{:S(2)}, u32[]{:S(2)}) collective-permute-start(bf16[3,3,128,256]{3,2,1,0:T(8,128)(2,1)} %get-tuple-element.124), channel_id=1, source_target_pairs={{16,0},{32,16},{48,32},{64,48},{80,64},{96,80},{112,96},{128,112},... | collective-permute-start | bytes 1769480 | tf_op jit(solution)/shard_map/ppermute | solution.py:19
  49.1 3.6 %collective-permute-start.6 = (bf16[3,3,128,256]{3,2,1,0:T(8,128)(2,1)}, bf16[3,3,128,256]{3,2,1,0:T(8,128)(2,1)}, u32[]{:S(2)}, u32[]{:S(2)}) collective-permute-start(bf16[3,3,128,256]{3,2,1,0:T(8,128)(2,1)} %get-tuple-element.123), channel_id=1, source_target_pairs={{0,16},{16,32},{32,48},{48,64},{64,80},{80,96},{96,112},{112,128},... | collective-permute-start | bytes 1769480 | tf_op jit(solution)/shard_map/ppermute | solution.py:19
  52.8 1.9 %collective-permute-start.7 = (bf16[3,3,128,256]{3,2,1,0:T(8,128)(2,1)}, bf16[3,3,128,256]{3,2,1,0:T(8,128)(2,1)}, u32[]{:S(2)}, u32[]{:S(2)}) collective-permute-start(bf16[3,3,128,256]{3,2,1,0:T(8,128)(2,1)} %get-tuple-element.122), channel_id=1, source_target_pairs={{16,0},{32,16},{48,32},{64,48},{80,64},{96,80},{112,96},{128,112},... | collective-permute-start | bytes 1769480 | tf_op jit(solution)/shard_map/ppermute | solution.py:19
  56.1 11.5 %multiply_add_fusion.middle_ref = f32[8,8,128,256]{3,2,1,0:T(8,128)} fusion(bf16[8,8,128,256]{3,2,1,0:T(8,128)(2,1)S(1)} %copy-done.1, bf16[11,8,128,256]{3,2,1,0:T(8,128)(2,1)S(1)} %constant_dynamic-update-slice_fusion.2, bf16[11,8,128,256]{3,2,1,0:T(8,128)(2,1)S(1)} %get-tuple-element.118, f32[]{:T(128)} %bitcast.6, f32[]{:T(128)} %bitcast.5, f32[]{:T(128)} %bitcast.4, ...), kind=kLoop, calls=%fused_computation.30 | loop fusion | flops 41943040 | bytes 37748764 | tf_op jit(solution)/shard_map/add | solution.py:51
  67.7 11.8 %shard_map.85 = bf16[8,8,128,256]{3,2,1,0:T(8,128)(2,1)} custom-call(f32[7]{0:T(128)} %lat_ref.1, f32[7]{0:T(128)} %elev_ref.1, f32[8,8,128,256]{3,2,1,0:T(8,128)} %multiply_add_fusion.middle_ref, bf16[3,3,128,256]{3,2,1,0:T(8,128)(2,1)} %collective-permute-done.3.refs_0_, bf16[8,3,128,256]{3,2,1,0:T(8,128)(2,1)} %copy-done.2, ...), custom_call_target="tpu_custom_call" | custom-call | tf_op jit(solution)/shard_map/pallas_call | solution.py:97
  79.5 3.4 %convolution_convert_fusion.1 = bf16[8192,256]{1,0:T(8,128)(2,1)S(1)} fusion(bf16[8192,256]{1,0:T(8,128)(2,1)} %bitcast.71, bf16[32,8,2,128]{3,2,1,0:T(2,128)(2,1)S(1)} %bitcast.72), kind=kOutput, calls=%fused_computation.28 | convolution fusion | flops 1075838976 | bytes 8519680 | tf_op jit(solution)/shard_map/dot_general | solution.py:119
  82.9 1.3 fusion.38
  86.3 1.3 collective-permute-done.8
  87.7 3.1 %collective-permute-start.10 = (f32[136,128]{1,0:T(8,128)S(1)}, f32[136,128]{1,0:T(8,128)S(1)}, u32[]{:S(2)}, u32[]{:S(2)}) collective-permute-start(f32[136,128]{1,0:T(8,128)S(1)} %dynamic-slice_add_fusion), channel_id=1, source_target_pairs={{0,64},{16,80},{32,96},{48,112},{64,0},{80,16},{96,32},{112,48},{1... | collective-permute-start | bytes 208904 | tf_op jit(solution)/shard_map/ppermute | solution.py:128
  90.7 3.9 %collective-permute-start.11 = (f32[136,128]{1,0:T(8,128)S(1)}, f32[136,128]{1,0:T(8,128)S(1)}, u32[]{:S(2)}, u32[]{:S(2)}) collective-permute-start(f32[136,128]{1,0:T(8,128)S(1)} %dynamic-slice_add_fusion), channel_id=1, source_target_pairs={{0,96},{16,112},{32,64},{48,80},{64,32},{80,48},{96,0},{112,16},{1... | collective-permute-start | bytes 208904 | tf_op jit(solution)/shard_map/ppermute | solution.py:128
  94.8 3.6 %collective-permute-done.11 = f32[136,128]{1,0:T(8,128)S(1)} collective-permute-done((f32[136,128]{1,0:T(8,128)S(1)}, f32[136,128]{1,0:T(8,128)S(1)}, u32[]{:S(2)}, u32[]{:S(2)}) %collective-permute-start.11) | collective-permute-done | bytes 69664 | tf_op jit(solution)/shard_map/ppermute | solution.py:128
  98.4 1.4 collective-permute-done.9
  99.9 5.0 %collective-permute-start.12 = (f32[136,128]{1,0:T(8,128)S(1)}, f32[136,128]{1,0:T(8,128)S(1)}, u32[]{:S(2)}, u32[]{:S(2)}) collective-permute-start(f32[136,128]{1,0:T(8,128)S(1)} %add_add_fusion.2), channel_id=1, source_target_pairs={{0,128},{16,144},{32,160},{48,176},{64,192},{80,208},{96,224},{112... | collective-permute-start | bytes 208904 | tf_op jit(solution)/shard_map/ppermute | solution.py:128
  104.9 2.1 %collective-permute-done.12 = f32[136,128]{1,0:T(8,128)S(1)} collective-permute-done((f32[136,128]{1,0:T(8,128)S(1)}, f32[136,128]{1,0:T(8,128)S(1)}, u32[]{:S(2)}, u32[]{:S(2)}) %collective-permute-start.12) | collective-permute-done | bytes 69664 | tf_op jit(solution)/shard_map/ppermute | solution.py:128
  107.0 2.5 %collective-permute-start.13 = (f32[136,128]{1,0:T(8,128)S(1)}, f32[136,128]{1,0:T(8,128)S(1)}, u32[]{:S(2)}, u32[]{:S(2)}) collective-permute-start(f32[136,128]{1,0:T(8,128)S(1)} %add.104), channel_id=1, source_target_pairs={{0,1},{1,0},{2,3},{3,2},{4,5},{5,4},{6,7},{7,6},{8,9},{9,8},{10,11... | collective-permute-start | bytes 208904 | tf_op jit(solution)/shard_map/ppermute | solution.py:128
  109.5 2.5 %collective-permute-start.14 = (f32[136,128]{1,0:T(8,128)S(1)}, f32[136,128]{1,0:T(8,128)S(1)}, u32[]{:S(2)}, u32[]{:S(2)}) collective-permute-start(f32[136,128]{1,0:T(8,128)S(1)} %add.104), channel_id=1, source_target_pairs={{0,2},{1,3},{2,0},{3,1},{4,6},{5,7},{6,4},{7,5},{8,10},{9,11},{10,... | collective-permute-start | bytes 208904 | tf_op jit(solution)/shard_map/ppermute | solution.py:128
  112.0 2.4 %collective-permute-done.14 = f32[136,128]{1,0:T(8,128)S(1)} collective-permute-done((f32[136,128]{1,0:T(8,128)S(1)}, f32[136,128]{1,0:T(8,128)S(1)}, u32[]{:S(2)}, u32[]{:S(2)}) %collective-permute-start.14) | collective-permute-done | bytes 69664 | tf_op jit(solution)/shard_map/ppermute | solution.py:128
  114.4 2.7 %collective-permute-done.15 = f32[136,128]{1,0:T(8,128)S(1)} collective-permute-done((f32[136,128]{1,0:T(8,128)S(1)}, f32[136,128]{1,0:T(8,128)S(1)}, u32[]{:S(2)}, u32[]{:S(2)}) %collective-permute-start.15) | collective-permute-done | bytes 69664 | tf_op jit(solution)/shard_map/ppermute | solution.py:128
  117.7 2.6 %collective-permute-start.17 = (f32[136,128]{1,0:T(8,128)S(1)}, f32[136,128]{1,0:T(8,128)S(1)}, u32[]{:S(2)}, u32[]{:S(2)}) collective-permute-start(f32[136,128]{1,0:T(8,128)S(1)} %add_add_fusion.1), channel_id=1, source_target_pairs={{0,8},{1,9},{2,10},{3,11},{4,12},{5,13},{6,14},{7,15},{8,0},{9,1},... | collective-permute-start | bytes 208904 | tf_op jit(solution)/shard_map/ppermute | solution.py:128
  122.8 1.9 %collective-permute-done.18 = f32[136,128]{1,0:T(8,128)S(1)} collective-permute-done((f32[136,128]{1,0:T(8,128)S(1)}, f32[136,128]{1,0:T(8,128)S(1)}, u32[]{:S(2)}, u32[]{:S(2)}) %collective-permute-start.18) | collective-permute-done | bytes 69664 | tf_op jit(solution)/shard_map/ppermute | solution.py:128
  124.8 5.3 %collective-permute-start.19 = (f32[136,128]{1,0:T(8,128)S(1)}, f32[136,128]{1,0:T(8,128)S(1)}, u32[]{:S(2)}, u32[]{:S(2)}) collective-permute-start(f32[136,128]{1,0:T(8,128)S(1)} %add_add_fusion), channel_id=1, source_target_pairs={{0,16},{16,0},{32,48},{48,32},{64,80},{80,64},{96,112},{112,96},{1... | collective-permute-start | bytes 208904 | tf_op jit(solution)/shard_map/ppermute | solution.py:160
  132.7 5.0 %while.26 = (s32[]{:T(128)}, f32[2,256,256]{1,2,0:T(8,128)S(1)}, f32[2]{0:T(128)S(1)}, f32[256,256]{1,0:T(8,128)S(1)}, f32[2]{0:T(128)S(1)}, /*index=5*/f32[256,256]{1,0:T(8,128)S(1)}, s32[]{:T(128)}) while((s32[]{:T(128)}, f32[2,256,256]{1,2,0:T(8,128)S(1)}, f32[2]{0:T(128)S(1)}, f32[256,256]{1,0:T(8,128)S(1)}, f32[2]{0:T(128)S(1)}, ...), condition=%wide.region_3.4_spmd.clone, body=%wide.region_2.3_spmd.clone.sunk | while | flops 403308544 | bytes 4194421 | solution.py:211
  137.8 6.2 %while.27 = (s32[]{:T(128)}, f32[2,256,256]{1,2,0:T(8,128)S(1)}, f32[2]{0:T(128)S(1)}, f32[256,256]{1,0:T(8,128)S(1)}, f32[2]{0:T(128)S(1)}, /*index=5*/f32[256,256]{1,0:T(8,128)S(1)}, s32[]{:T(128)}) while((s32[]{:T(128)}, f32[2,256,256]{1,2,0:T(8,128)S(1)}, f32[2]{0:T(128)S(1)}, f32[256,256]{1,0:T(8,128)S(1)}, f32[2]{0:T(128)S(1)}, ...), condition=%wide.region_5.6_spmd.clone, body=%wide.region_4.5_spmd.clone.sunk | while | flops 805961728 | bytes 4194421 | solution.py:212
  144.3 6.2 %multiply_reduce_fusion = (f32[8192]{0:T(1024)}, bf16[8192,256]{1,0:T(8,128)(2,1)}) fusion(bf16[8192,256]{1,0:T(8,128)(2,1)} %copy-done, f32[256,256]{1,0:T(8,128)S(1)} %fusion.22), kind=kOutput, calls=%fused_computation.29 | convolution fusion | flops 1082187776 | bytes 8683520 | tf_op jit(solution)/shard_map/dot_general | solution.py:227
  (101 shorter events, 23.2 us)
Async XLA Ops:
  0.6 7.6 %copy-start.1 = (bf16[8,8,128,256]{3,2,1,0:T(8,128)(2,1)S(1)}, bf16[8,8,128,256]{3,2,1,0:T(8,128)(2,1)}, u32[]{:S(2)}) copy-start(bf16[8,8,128,256]{3,2,1,0:T(8,128)(2,1)} %param.10) | copy-start | bytes 12582916
  2.9 13.1 %copy-start.5 = (f32[7]{0:T(128)S(1)}, f32[7]{0:T(128)}, u32[]{:S(2)}) copy-start(f32[7]{0:T(128)} %lat_ref.1) | copy-start | bytes 88
  2.9 13.8 %copy-start.6 = (bf16[32]{0:T(256)(128)(2,1)S(1)}, bf16[32]{0:T(256)(128)(2,1)}, u32[]{:S(2)}) copy-start(bf16[32]{0:T(256)(128)(2,1)} %param.13) | copy-start | bytes 196
  2.9 37.0 %collective-permute-start.2 = (bf16[8,3,128,256]{3,2,1,0:T(8,128)(2,1)S(1)}, bf16[8,3,128,256]{3,2,1,0:T(8,128)(2,1)S(1)}, u32[]{:S(2)}, u32[]{:S(2)}) collective-permute-start(bf16[8,3,128,256]{3,2,1,0:T(8,128)(2,1)S(1)} %get-tuple-element.117), channel_id=1, source_target_pairs={{0,1},{1,2},{2,3},{3,4},{4,5},{5,6},{6,7},{7,8},{8,9},{9,10},{10,1... | collective-permute-start | bytes 4718600 | tf_op jit(solution)/shard_map/ppermute | solution.py:19
  7.0 41.0 %collective-permute-start.5 = (bf16[8,3,128,256]{3,2,1,0:T(8,128)(2,1)S(1)}, bf16[8,3,128,256]{3,2,1,0:T(8,128)(2,1)S(1)}, u32[]{:S(2)}, u32[]{:S(2)}) collective-permute-start(bf16[8,3,128,256]{3,2,1,0:T(8,128)(2,1)S(1)} %get-tuple-element.116), channel_id=1, source_target_pairs={{1,0},{2,1},{3,2},{4,3},{5,4},{6,5},{7,6},{8,7},{9,8},{10,9},{11,1... | collective-permute-start | bytes 4718600 | tf_op jit(solution)/shard_map/ppermute | solution.py:19
  9.7 43.1 %collective-permute-start = (bf16[3,8,128,256]{3,2,1,0:T(8,128)(2,1)S(1)}, bf16[3,8,128,256]{3,2,1,0:T(8,128)(2,1)S(1)}, u32[]{:S(2)}, u32[]{:S(2)}) collective-permute-start(bf16[3,8,128,256]{3,2,1,0:T(8,128)(2,1)S(1)} %get-tuple-element.120), channel_id=1, source_target_pairs={{0,16},{16,32},{32,48},{48,64},{64,80},{80,96},{96,112},{112,128},... | collective-permute-start | bytes 4718600 | tf_op jit(solution)/shard_map/ppermute | solution.py:19
  14.1 41.9 %collective-permute-start.1 = (bf16[3,8,128,256]{3,2,1,0:T(8,128)(2,1)}, bf16[3,8,128,256]{3,2,1,0:T(8,128)(2,1)S(1)}, u32[]{:S(2)}, u32[]{:S(2)}) collective-permute-start(bf16[3,8,128,256]{3,2,1,0:T(8,128)(2,1)} %get-tuple-element.121), channel_id=1, source_target_pairs={{16,0},{32,16},{48,32},{64,48},{80,64},{96,80},{112,96},{128,112},... | collective-permute-start | bytes 4718600 | tf_op jit(solution)/shard_map/ppermute | solution.py:19
  39.9 16.0 %copy-start.2 = (bf16[8,3,128,256]{3,2,1,0:T(8,128)(2,1)}, bf16[8,3,128,256]{3,2,1,0:T(8,128)(2,1)S(1)}, u32[]{:S(2)}) copy-start(bf16[8,3,128,256]{3,2,1,0:T(8,128)(2,1)S(1)} %collective-permute-done.2.refs_1_) | copy-start | bytes 4718596
  41.1 26.6 %collective-permute-start.3 = (bf16[3,3,128,256]{3,2,1,0:T(8,128)(2,1)}, bf16[3,3,128,256]{3,2,1,0:T(8,128)(2,1)}, u32[]{:S(2)}, u32[]{:S(2)}) collective-permute-start(bf16[3,3,128,256]{3,2,1,0:T(8,128)(2,1)} %get-tuple-element.125), channel_id=1, source_target_pairs={{0,16},{16,32},{32,48},{48,64},{64,80},{80,96},{96,112},{112,128},... | collective-permute-start | bytes 1769480 | tf_op jit(solution)/shard_map/ppermute | solution.py:19
  46.0 21.7 %collective-permute-start.4 = (bf16[3,3,128,256]{3,2,1,0:T(8,128)(2,1)}, bf16[3,3,128,256]{3,2,1,0:T(8,128)(2,1)}, u32[]{:S(2)}, u32[]{:S(2)}) collective-permute-start(bf16[3,3,128,256]{3,2,1,0:T(8,128)(2,1)} %get-tuple-element.124), channel_id=1, source_target_pairs={{16,0},{32,16},{48,32},{64,48},{80,64},{96,80},{112,96},{128,112},... | collective-permute-start | bytes 1769480 | tf_op jit(solution)/shard_map/ppermute | solution.py:19
  48.0 8.0 %copy-start.3 = (bf16[8,3,128,256]{3,2,1,0:T(8,128)(2,1)}, bf16[8,3,128,256]{3,2,1,0:T(8,128)(2,1)S(1)}, u32[]{:S(2)}) copy-start(bf16[8,3,128,256]{3,2,1,0:T(8,128)(2,1)S(1)} %collective-permute-done.5.refs_4_) | copy-start | bytes 4718596
  49.1 18.5 %collective-permute-start.6 = (bf16[3,3,128,256]{3,2,1,0:T(8,128)(2,1)}, bf16[3,3,128,256]{3,2,1,0:T(8,128)(2,1)}, u32[]{:S(2)}, u32[]{:S(2)}) collective-permute-start(bf16[3,3,128,256]{3,2,1,0:T(8,128)(2,1)} %get-tuple-element.123), channel_id=1, source_target_pairs={{0,16},{16,32},{32,48},{48,64},{64,80},{80,96},{96,112},{112,128},... | collective-permute-start | bytes 1769480 | tf_op jit(solution)/shard_map/ppermute | solution.py:19
  52.8 14.9 %collective-permute-start.7 = (bf16[3,3,128,256]{3,2,1,0:T(8,128)(2,1)}, bf16[3,3,128,256]{3,2,1,0:T(8,128)(2,1)}, u32[]{:S(2)}, u32[]{:S(2)}) collective-permute-start(bf16[3,3,128,256]{3,2,1,0:T(8,128)(2,1)} %get-tuple-element.122), channel_id=1, source_target_pairs={{16,0},{32,16},{48,32},{64,48},{80,64},{96,80},{112,96},{128,112},... | collective-permute-start | bytes 1769480 | tf_op jit(solution)/shard_map/ppermute | solution.py:19
  82.9 2.0 %copy-start = (bf16[8192,256]{1,0:T(8,128)(2,1)}, bf16[8192,256]{1,0:T(8,128)(2,1)S(1)}, u32[]{:S(2)}) copy-start(bf16[8192,256]{1,0:T(8,128)(2,1)S(1)} %convolution_convert_fusion.1) | copy-start | bytes 12582916
  86.2 1.4 collective-permute-start.8
  87.7 7.1 %collective-permute-start.10 = (f32[136,128]{1,0:T(8,128)S(1)}, f32[136,128]{1,0:T(8,128)S(1)}, u32[]{:S(2)}, u32[]{:S(2)}) collective-permute-start(f32[136,128]{1,0:T(8,128)S(1)} %dynamic-slice_add_fusion), channel_id=1, source_target_pairs={{0,64},{16,80},{32,96},{48,112},{64,0},{80,16},{96,32},{112,48},{1... | collective-permute-start | bytes 208904 | tf_op jit(solution)/shard_map/ppermute | solution.py:128
  90.7 7.7 %collective-permute-start.11 = (f32[136,128]{1,0:T(8,128)S(1)}, f32[136,128]{1,0:T(8,128)S(1)}, u32[]{:S(2)}, u32[]{:S(2)}) collective-permute-start(f32[136,128]{1,0:T(8,128)S(1)} %dynamic-slice_add_fusion), channel_id=1, source_target_pairs={{0,96},{16,112},{32,64},{48,80},{64,32},{80,48},{96,0},{112,16},{1... | collective-permute-start | bytes 208904 | tf_op jit(solution)/shard_map/ppermute | solution.py:128
  94.6 5.2 %collective-permute-start.9 = (f32[136,128]{1,0:T(8,128)S(1)}, f32[136,128]{1,0:T(8,128)S(1)}, u32[]{:S(2)}, u32[]{:S(2)}) collective-permute-start(f32[136,128]{1,0:T(8,128)S(1)} %dynamic-slice_add_fusion), channel_id=1, source_target_pairs={{0,32},{16,48},{32,0},{48,16},{64,96},{80,112},{96,64},{112,80},{1... | collective-permute-start | bytes 208904 | tf_op jit(solution)/shard_map/ppermute | solution.py:128
  99.9 7.2 %collective-permute-start.12 = (f32[136,128]{1,0:T(8,128)S(1)}, f32[136,128]{1,0:T(8,128)S(1)}, u32[]{:S(2)}, u32[]{:S(2)}) collective-permute-start(f32[136,128]{1,0:T(8,128)S(1)} %add_add_fusion.2), channel_id=1, source_target_pairs={{0,128},{16,144},{32,160},{48,176},{64,192},{80,208},{96,224},{112... | collective-permute-start | bytes 208904 | tf_op jit(solution)/shard_map/ppermute | solution.py:128
  107.0 5.0 %collective-permute-start.13 = (f32[136,128]{1,0:T(8,128)S(1)}, f32[136,128]{1,0:T(8,128)S(1)}, u32[]{:S(2)}, u32[]{:S(2)}) collective-permute-start(f32[136,128]{1,0:T(8,128)S(1)} %add.104), channel_id=1, source_target_pairs={{0,1},{1,0},{2,3},{3,2},{4,5},{5,4},{6,7},{7,6},{8,9},{9,8},{10,11... | collective-permute-start | bytes 208904 | tf_op jit(solution)/shard_map/ppermute | solution.py:128
  109.5 4.9 %collective-permute-start.14 = (f32[136,128]{1,0:T(8,128)S(1)}, f32[136,128]{1,0:T(8,128)S(1)}, u32[]{:S(2)}, u32[]{:S(2)}) collective-permute-start(f32[136,128]{1,0:T(8,128)S(1)} %add.104), channel_id=1, source_target_pairs={{0,2},{1,3},{2,0},{3,1},{4,6},{5,7},{6,4},{7,5},{8,10},{9,11},{10,... | collective-permute-start | bytes 208904 | tf_op jit(solution)/shard_map/ppermute | solution.py:128
  112.0 5.1 %collective-permute-start.15 = (f32[136,128]{1,0:T(8,128)S(1)}, f32[136,128]{1,0:T(8,128)S(1)}, u32[]{:S(2)}, u32[]{:S(2)}) collective-permute-start(f32[136,128]{1,0:T(8,128)S(1)} %add.104), channel_id=1, source_target_pairs={{0,3},{1,2},{2,1},{3,0},{4,7},{5,6},{6,5},{7,4},{8,11},{9,10},{10,... | collective-permute-start | bytes 208904 | tf_op jit(solution)/shard_map/ppermute | solution.py:128
  117.1 5.2 %collective-permute-start.16 = (f32[136,128]{1,0:T(8,128)S(1)}, f32[136,128]{1,0:T(8,128)S(1)}, u32[]{:S(2)}, u32[]{:S(2)}) collective-permute-start(f32[136,128]{1,0:T(8,128)S(1)} %add_add_fusion.1), channel_id=1, source_target_pairs={{0,4},{1,5},{2,6},{3,7},{4,0},{5,1},{6,2},{7,3},{8,12},{9,13},{10,... | collective-permute-start | bytes 208904 | tf_op jit(solution)/shard_map/ppermute | solution.py:128
  117.7 5.1 %collective-permute-start.17 = (f32[136,128]{1,0:T(8,128)S(1)}, f32[136,128]{1,0:T(8,128)S(1)}, u32[]{:S(2)}, u32[]{:S(2)}) collective-permute-start(f32[136,128]{1,0:T(8,128)S(1)} %add_add_fusion.1), channel_id=1, source_target_pairs={{0,8},{1,9},{2,10},{3,11},{4,12},{5,13},{6,14},{7,15},{8,0},{9,1},... | collective-permute-start | bytes 208904 | tf_op jit(solution)/shard_map/ppermute | solution.py:128
  120.4 4.4 %collective-permute-start.18 = (f32[136,128]{1,0:T(8,128)S(1)}, f32[136,128]{1,0:T(8,128)S(1)}, u32[]{:S(2)}, u32[]{:S(2)}) collective-permute-start(f32[136,128]{1,0:T(8,128)S(1)} %add_add_fusion.1), channel_id=1, source_target_pairs={{0,12},{1,13},{2,14},{3,15},{4,8},{5,9},{6,10},{7,11},{8,4},{9,5},... | collective-permute-start | bytes 208904 | tf_op jit(solution)/shard_map/ppermute | solution.py:128
  124.8 6.2 %collective-permute-start.19 = (f32[136,128]{1,0:T(8,128)S(1)}, f32[136,128]{1,0:T(8,128)S(1)}, u32[]{:S(2)}, u32[]{:S(2)}) collective-permute-start(f32[136,128]{1,0:T(8,128)S(1)} %add_add_fusion), channel_id=1, source_target_pairs={{0,16},{16,0},{32,48},{48,32},{64,80},{80,64},{96,112},{112,96},{1... | collective-permute-start | bytes 208904 | tf_op jit(solution)/shard_map/ppermute | solution.py:160
  144.3 6.2 %copy-start.4 = (f32[256,256]{1,0:T(8,128)}, f32[256,256]{1,0:T(8,128)S(1)}, u32[]{:S(2)}) copy-start(f32[256,256]{1,0:T(8,128)S(1)} %fusion.22) | copy-start | bytes 786436

commit v9 on v8

--- a/solution.py
+++ b/solution.py
@@ -26,7 +26,7 @@
     north_east = shift(east[low_lat], "lat", 1)
     south_west = shift(west[high_lat], "lat", -1)
     south_east = shift(east[high_lat], "lat", -1)
-    center = jnp.concatenate([north, block, south], axis=0)
+    center = (block, north, south)
     left = (north_west, west, south_west)
     right = (north_east, east, south_east)
     return left, center, right
@@ -45,13 +45,29 @@
     return paired.astype(jnp.bfloat16)
 
 
-def lat_pass(extended, lat_taps, lat_count):
-    lat_sum = lat_taps[0] * extended[0:lat_count].astype(jnp.float32)
-    for index_tap in range(1, 7):
-        lat_sum = lat_sum + lat_taps[index_tap] * extended[
-            index_tap : index_tap + lat_count
-        ].astype(jnp.float32)
-    return lat_sum
+def lat_rows(rows, lat_taps, lat_count):
+    sums = []
+    for l in range(lat_count):
+        total = lat_taps[0] * rows[l]
+        for i in range(1, 7):
+            total = total + lat_taps[i] * rows[l + i]
+        sums.append(total)
+    return sums
+
+
+def center_smooth_kernel(lat_ref, elev_ref, block_ref, north_ref, south_ref, out_ref):
+    lat_taps = [lat_ref[i] for i in range(7)]
+    elev_taps = [elev_ref[i] for i in range(7)]
+    lat_count, elev_count = out_ref.shape[0], out_ref.shape[1]
+    refs = (north_ref, block_ref, south_ref)
+    rows = [ref[k].astype(jnp.float32) for ref in refs for k in range(ref.shape[0])]
+    for l, row in enumerate(lat_rows(rows, lat_taps, lat_count)):
+        for e in range(elev_count):
+            taps = [j for j in range(7) if 0 <= e + j - 3 < elev_count]
+            total = elev_taps[taps[0]] * row[e + taps[0] - 3]
+            for j in taps[1:]:
+                total = total + elev_taps[j] * row[e + j - 3]
+            out_ref[l, e] = total
 
 
 def edge_smooth_kernel(lat_ref, elev_ref, middle_ref, *refs):
@@ -60,61 +76,55 @@
     lat_taps = [lat_ref[i] for i in range(7)]
     elev_taps = [elev_ref[i] for i in range(7)]
     lat_count, elev_count = out_ref.shape[0], out_ref.shape[1]
+    width = left_refs[0].shape[1]
 
     def side_rows(side_refs):
         rows = [ref[k].astype(jnp.float32) for ref in side_refs for k in range(ref.shape[0])]
-        sums = []
-        for l in range(lat_count):
-            total = lat_taps[0] * rows[l]
-            for i in range(1, 7):
-                total = total + lat_taps[i] * rows[l + i]
-            sums.append(total)
-        return sums
+        return lat_rows(rows, lat_taps, lat_count)
 
     left = side_rows(left_refs)
     right = side_rows(right_refs)
-    width = left_refs[0].shape[1]
     for l in range(lat_count):
-        columns = [left[l][k] for k in range(width)]
-        columns += [middle_ref[l, k] for k in range(elev_count)]
-        columns += [right[l][k] for k in range(width)]
         for e in range(elev_count):
-            total = elev_taps[0] * columns[e]
-            for j in range(1, 7):
-                total = total + elev_taps[j] * columns[e + j]
+            total = middle_ref[l, e]
+            for j in range(7):
+                column = e + j
+                if column < width:
+                    total = total + elev_taps[j] * left[l][column]
+                elif column >= width + elev_count:
+                    total = total + elev_taps[j] * right[l][column - width - elev_count]
             out_ref[l, e] = total.astype(out_ref.dtype)
 
 
-def edge_smooth(middle, left, right, lat_taps, elev_taps, tile=16):
-    _, _, depth, columns = middle.shape
+def tiled_call(kernel, pieces, out_dtype, lat_taps, elev_taps, tile=16):
+    _, _, depth, columns = pieces[0].shape
     tile = tile if depth % tile == 0 else depth
     smem = pl.BlockSpec(memory_space=pltpu.SMEM)
 
     def tiled(piece):
         return pl.BlockSpec((piece.shape[0], piece.shape[1], tile, columns), lambda k: (0, 0, k, 0))
 
-    sides = (*left, *right)
     return pl.pallas_call(
-        edge_smooth_kernel,
-        out_shape=jax.ShapeDtypeStruct(middle.shape, jnp.bfloat16),
+        kernel,
+        out_shape=jax.ShapeDtypeStruct(pieces[0].shape, out_dtype),
         grid=(depth // tile,),
-        in_specs=[smem, smem, tiled(middle), *[tiled(piece) for piece in sides]],
-        out_specs=tiled(middle),
+        in_specs=[smem, smem, *[tiled(piece) for piece in pieces]],
+        out_specs=tiled(pieces[0]),
         interpret=INTERPRET,
-    )(lat_taps, elev_taps, middle, *sides)
+    )(lat_taps, elev_taps, *pieces)
 
 
 INTERPRET = False
 
 
-def smooth(pieces, lat_taps, elev_taps, lat_count):
+def smooth(pieces, lat_taps, elev_taps):
     left, center, right = pieces
-    middle = lat_pass(center, lat_taps, lat_count)
-    return edge_smooth(middle, left, right, lat_taps, elev_taps)
-
-
-def filtered_rows(pieces, lat_taps, elev_taps, matrix, lat_count):
-    smoothed = smooth(pieces, lat_taps, elev_taps, lat_count)
+    middle = tiled_call(center_smooth_kernel, center, jnp.float32, lat_taps, elev_taps)
+    return tiled_call(edge_smooth_kernel, (middle, *left, *right), jnp.bfloat16, lat_taps, elev_taps)
+
+
+def filtered_rows(pieces, lat_taps, elev_taps, matrix):
+    smoothed = smooth(pieces, lat_taps, elev_taps)
     flat_rows = smoothed.reshape(-1, matrix.shape[0])
     return jnp.dot(flat_rows, matrix, preferred_element_type=jnp.float32).astype(jnp.bfloat16)
 
@@ -218,7 +228,7 @@
     lat_count, elev_count, depth, columns = volume.shape
     matrix = time_matrix(time_taps, columns // 2)
     extended = halo_pieces(volume, 3)
-    row_block = filtered_rows(extended, lat_taps, elev_taps, matrix, lat_count)
+    row_block = filtered_rows(extended, lat_taps, elev_taps, matrix)
     local_gram = lax.dot_general(
         row_block, row_block, (((0,), (0,)), ((), ())), preferred_element_type=jnp.float32
     )

time: 151 us -> 149 us (0.987)
  the two profiles are of different devices: /device:TPU:1 before, /device:TPU:2 now
where the time goes in v9:
time: 149 us; the launch traced here: 146 us
  waiting for transfers between devices  44.8 us (30%)
  starting transfers between devices  43.9 us (29%)
  Pallas kernels  21.8 us (15%)
  matrix products  21.3 us (14%)
  local copies, waits for them, and re-layouts  9.15 us (6%)
  other arithmetic  2.83 us (2%)
  between operations  2.32 us (2%)
    ppermute x8, waiting for transfers between devices, shift(): return lax.ppermute(piece, axis, pairs)  29 us
    ppermute x10, starting transfers between devices, butterfly_sum(): lax.ppermute(block, axis, [(i, i ^ mask) for i in range(count)])  23.7 us
    pallas_call x2, Pallas kernels, tiled_call(): pl.pallas_call(kernel, out_shape=jax.ShapeDtypeStruct(pieces[0].shape, ou...  21.8 us
    ppermute x8, starting transfers between devices, shift(): return lax.ppermute(piece, axis, pairs)  18.5 us
    ppermute x10, waiting for transfers between devices, butterfly_sum(): lax.ppermute(block, axis, [(i, i ^ mask) for i in range(count)])  14.8 us
    dot_general x1, matrix products, body(): jnp.dot(row_block, weights.astype(jnp.bfloat16), preferred_element_type=j...  6.16 us
    dot_general x9, matrix products, step(): product = jnp.einsum('bij,bjk->bik', shifted, inverse, precision=precision)  5.5 us
    dot_general x9, matrix products, step(): jnp.einsum('bij,bjk->bik', inverse, product, precision=precision)  4.88 us
  transfers between devices with their start and end apart: 20, of which 10 were waited for; matrix products, arithmetic and copies ran while one was open for 3% of the time, Pallas kernels for 8%

profile of v9, /device:TPU:2, one launch (start us, length us, event | category | flops | bytes accessed | tf_op | source)
XLA Modules:
  0.0 146.4 jit_solution(15796354105301257115)
XLA Ops:
  0.6 2.4 %fusion.31 = (bf16[8,3,128,256]{3,2,1,0:T(8,128)(2,1)S(1)}, bf16[8,3,128,256]{3,2,1,0:T(8,128)(2,1)S(1)}) fusion(bf16[8,8,128,256]{3,2,1,0:T(8,128)(2,1)} %block_ref.1), kind=kLoop, calls=%fused_computation.70 | loop fusion | bytes 6291456 | tf_op jit(solution)/shard_map/slice | solution.py:24
  3.0 3.4 %collective-permute-start.2 = (bf16[8,3,128,256]{3,2,1,0:T(8,128)(2,1)S(1)}, bf16[8,3,128,256]{3,2,1,0:T(8,128)(2,1)S(1)}, u32[]{:S(2)}, u32[]{:S(2)}) collective-permute-start(bf16[8,3,128,256]{3,2,1,0:T(8,128)(2,1)S(1)} %get-tuple-element.117), channel_id=1, source_target_pairs={{0,1},{1,2},{2,3},{3,4},{4,5},{5,6},{6,7},{7,8},{8,9},{9,10},{10,1... | collective-permute-start | bytes 4718600 | tf_op jit(solution)/shard_map/ppermute | solution.py:19
  6.5 2.5 %collective-permute-start.5 = (bf16[8,3,128,256]{3,2,1,0:T(8,128)(2,1)S(1)}, bf16[8,3,128,256]{3,2,1,0:T(8,128)(2,1)S(1)}, u32[]{:S(2)}, u32[]{:S(2)}) collective-permute-start(bf16[8,3,128,256]{3,2,1,0:T(8,128)(2,1)S(1)} %get-tuple-element.116), channel_id=1, source_target_pairs={{1,0},{2,1},{3,2},{4,3},{5,4},{6,5},{7,6},{8,7},{9,8},{10,9},{11,1... | collective-permute-start | bytes 4718600 | tf_op jit(solution)/shard_map/ppermute | solution.py:19
  9.4 1.4 collective-permute-start
  10.8 1.3 collective-permute-start.1
  12.1 29.0 %collective-permute-done.2.refs_1_ = bf16[8,3,128,256]{3,2,1,0:T(8,128)(2,1)S(1)} collective-permute-done((bf16[8,3,128,256]{3,2,1,0:T(8,128)(2,1)S(1)}, bf16[8,3,128,256]{3,2,1,0:T(8,128)(2,1)S(1)}, u32[]{:S(2)}, u32[]{:S(2)}) %collective-permute-start.2) | collective-permute-done | bytes 1572896 | tf_op jit(solution)/shard_map/ppermute | solution.py:19
  41.1 1.3 fusion.34
  42.4 2.1 %collective-permute-start.3 = (bf16[3,3,128,256]{3,2,1,0:T(8,128)(2,1)}, bf16[3,3,128,256]{3,2,1,0:T(8,128)(2,1)}, u32[]{:S(2)}, u32[]{:S(2)}) collective-permute-start(bf16[3,3,128,256]{3,2,1,0:T(8,128)(2,1)} %get-tuple-element.123), channel_id=1, source_target_pairs={{0,16},{16,32},{32,48},{48,64},{64,80},{80,96},{96,112},{112,128},... | collective-permute-start | bytes 1769480 | tf_op jit(solution)/shard_map/ppermute | solution.py:19
  44.4 1.3 collective-permute-start.4
  45.8 1.2 fusion.33
  47.0 5.2 %collective-permute-start.6 = (bf16[3,3,128,256]{3,2,1,0:T(8,128)(2,1)}, bf16[3,3,128,256]{3,2,1,0:T(8,128)(2,1)}, u32[]{:S(2)}, u32[]{:S(2)}) collective-permute-start(bf16[3,3,128,256]{3,2,1,0:T(8,128)(2,1)} %get-tuple-element.121), channel_id=1, source_target_pairs={{0,16},{16,32},{32,48},{48,64},{64,80},{80,96},{96,112},{112,128},... | collective-permute-start | bytes 1769480 | tf_op jit(solution)/shard_map/ppermute | solution.py:19
  53.3 1.3 collective-permute-start.7
  55.5 11.5 %shard_map.85.middle_ref = f32[8,8,128,256]{3,2,1,0:T(8,128)} custom-call(f32[7]{0:T(128)} %lat_ref.3, f32[7]{0:T(128)} %elev_ref.3, bf16[8,8,128,256]{3,2,1,0:T(8,128)(2,1)} %block_ref.1, bf16[3,8,128,256]{3,2,1,0:T(8,128)(2,1)} %copy-done.4, bf16[3,8,128,256]{3,2,1,0:T(8,128)(2,1)} %collective-permute-done.1.south_ref), custom_call_target="tpu_custom_call" | custom-call | tf_op jit(solution)/shard_map/pallas_call | solution.py:107
  67.1 10.3 %shard_map.86 = bf16[8,8,128,256]{3,2,1,0:T(8,128)(2,1)} custom-call(f32[7]{0:T(128)} %lat_ref.3, f32[7]{0:T(128)} %elev_ref.3, f32[8,8,128,256]{3,2,1,0:T(8,128)} %shard_map.85.middle_ref, bf16[3,3,128,256]{3,2,1,0:T(8,128)(2,1)} %collective-permute-done.3.refs_0_, bf16[8,3,128,256]{3,2,1,0:T(8,128)(2,1)} %copy-done.2, ...), custom_call_target="tpu_custom_call" | custom-call | tf_op jit(solution)/shard_map/pallas_call | solution.py:107
  77.4 3.4 %convolution_convert_fusion.1 = bf16[8192,256]{1,0:T(8,128)(2,1)S(1)} fusion(bf16[8192,256]{1,0:T(8,128)(2,1)} %bitcast.64, bf16[32,8,2,128]{3,2,1,0:T(2,128)(2,1)S(1)} %bitcast.65), kind=kOutput, calls=%fused_computation.28 | convolution fusion | flops 1075838976 | bytes 8519680 | tf_op jit(solution)/shard_map/dot_general | solution.py:129
  80.8 1.3 fusion.37
  82.8 1.2 gather_fusion
  84.1 1.7 %collective-permute-start.8 = (f32[272,128]{1,0:T(8,128)S(1)}, f32[272,128]{1,0:T(8,128)S(1)}, u32[]{:S(2)}, u32[]{:S(2)}) collective-permute-start(f32[272,128]{1,0:T(8,128)S(1)} %select_maximum_fusion), channel_id=1, source_target_pairs={{0,16},{16,0},{32,48},{48,32},{64,80},{80,64},{96,112},{112,96},{1... | collective-permute-start | bytes 417800 | tf_op jit(solution)/shard_map/ppermute | solution.py:165
  86.7 3.4 %collective-permute-start.10 = (f32[136,128]{1,0:T(8,128)S(1)}, f32[136,128]{1,0:T(8,128)S(1)}, u32[]{:S(2)}, u32[]{:S(2)}) collective-permute-start(f32[136,128]{1,0:T(8,128)S(1)} %dynamic-slice_add_fusion), channel_id=1, source_target_pairs={{0,64},{16,80},{32,96},{48,112},{64,0},{80,16},{96,32},{112,48},{1... | collective-permute-start | bytes 208904 | tf_op jit(solution)/shard_map/ppermute | solution.py:138
  90.2 3.8 %collective-permute-start.11 = (f32[136,128]{1,0:T(8,128)S(1)}, f32[136,128]{1,0:T(8,128)S(1)}, u32[]{:S(2)}, u32[]{:S(2)}) collective-permute-start(f32[136,128]{1,0:T(8,128)S(1)} %dynamic-slice_add_fusion), channel_id=1, source_target_pairs={{0,96},{16,112},{32,64},{48,80},{64,32},{80,48},{96,0},{112,16},{1... | collective-permute-start | bytes 208904 | tf_op jit(solution)/shard_map/ppermute | solution.py:138
  94.5 4.0 %collective-permute-done.11 = f32[136,128]{1,0:T(8,128)S(1)} collective-permute-done((f32[136,128]{1,0:T(8,128)S(1)}, f32[136,128]{1,0:T(8,128)S(1)}, u32[]{:S(2)}, u32[]{:S(2)}) %collective-permute-start.11) | collective-permute-done | bytes 69664 | tf_op jit(solution)/shard_map/ppermute | solution.py:138
  99.5 5.3 %collective-permute-start.12 = (f32[136,128]{1,0:T(8,128)S(1)}, f32[136,128]{1,0:T(8,128)S(1)}, u32[]{:S(2)}, u32[]{:S(2)}) collective-permute-start(f32[136,128]{1,0:T(8,128)S(1)} %add_add_fusion.2), channel_id=1, source_target_pairs={{0,128},{16,144},{32,160},{48,176},{64,192},{80,208},{96,224},{112... | collective-permute-start | bytes 208904 | tf_op jit(solution)/shard_map/ppermute | solution.py:138
  104.7 3.0 %collective-permute-done.12 = f32[136,128]{1,0:T(8,128)S(1)} collective-permute-done((f32[136,128]{1,0:T(8,128)S(1)}, f32[136,128]{1,0:T(8,128)S(1)}, u32[]{:S(2)}, u32[]{:S(2)}) %collective-permute-start.12) | collective-permute-done | bytes 69664 | tf_op jit(solution)/shard_map/ppermute | solution.py:138
  107.8 2.2 %collective-permute-start.14 = (f32[136,128]{1,0:T(8,128)S(1)}, f32[136,128]{1,0:T(8,128)S(1)}, u32[]{:S(2)}, u32[]{:S(2)}) collective-permute-start(f32[136,128]{1,0:T(8,128)S(1)} %add.80), channel_id=1, source_target_pairs={{0,2},{1,3},{2,0},{3,1},{4,6},{5,7},{6,4},{7,5},{8,10},{9,11},{10,... | collective-permute-start | bytes 208904 | tf_op jit(solution)/shard_map/ppermute | solution.py:138
  110.0 2.6 %collective-permute-start.13 = (f32[136,128]{1,0:T(8,128)S(1)}, f32[136,128]{1,0:T(8,128)S(1)}, u32[]{:S(2)}, u32[]{:S(2)}) collective-permute-start(f32[136,128]{1,0:T(8,128)S(1)} %add.80), channel_id=1, source_target_pairs={{0,1},{1,0},{2,3},{3,2},{4,5},{5,4},{6,7},{7,6},{8,9},{9,8},{10,11... | collective-permute-start | bytes 208904 | tf_op jit(solution)/shard_map/ppermute | solution.py:138
  112.6 1.5 collective-permute-done.14
  114.9 4.9 %collective-permute-start.17 = (f32[136,128]{1,0:T(8,128)S(1)}, f32[136,128]{1,0:T(8,128)S(1)}, u32[]{:S(2)}, u32[]{:S(2)}) collective-permute-start(f32[136,128]{1,0:T(8,128)S(1)} %add_add_fusion.1), channel_id=1, source_target_pairs={{0,8},{1,9},{2,10},{3,11},{4,12},{5,13},{6,14},{7,15},{8,0},{9,1},... | collective-permute-start | bytes 208904 | tf_op jit(solution)/shard_map/ppermute | solution.py:138
  120.8 1.3 collective-permute-done.17
  122.2 3.1 %collective-permute-done.18 = f32[136,128]{1,0:T(8,128)S(1)} collective-permute-done((f32[136,128]{1,0:T(8,128)S(1)}, f32[136,128]{1,0:T(8,128)S(1)}, u32[]{:S(2)}, u32[]{:S(2)}) %collective-permute-start.18) | collective-permute-done | bytes 69664 | tf_op jit(solution)/shard_map/ppermute | solution.py:138
  128.7 5.0 %while.26 = (s32[]{:T(128)}, f32[2,256,256]{1,2,0:T(8,128)S(1)}, f32[2]{0:T(128)S(1)}, f32[256,256]{1,0:T(8,128)S(1)}, f32[2]{0:T(128)S(1)}, /*index=5*/f32[256,256]{1,0:T(8,128)S(1)}, s32[]{:T(128)}) while((s32[]{:T(128)}, f32[2,256,256]{1,2,0:T(8,128)S(1)}, f32[2]{0:T(128)S(1)}, f32[256,256]{1,0:T(8,128)S(1)}, f32[2]{0:T(128)S(1)}, ...), condition=%wide.region_3.4_spmd.clone, body=%wide.region_2.3_spmd.clone.sunk | while | flops 403308544 | bytes 4194421 | solution.py:221
  133.7 6.2 %while.27 = (s32[]{:T(128)}, f32[2,256,256]{1,2,0:T(8,128)S(1)}, f32[2]{0:T(128)S(1)}, f32[256,256]{1,0:T(8,128)S(1)}, f32[2]{0:T(128)S(1)}, /*index=5*/f32[256,256]{1,0:T(8,128)S(1)}, s32[]{:T(128)}) while((s32[]{:T(128)}, f32[2,256,256]{1,2,0:T(8,128)S(1)}, f32[2]{0:T(128)S(1)}, f32[256,256]{1,0:T(8,128)S(1)}, f32[2]{0:T(128)S(1)}, ...), condition=%wide.region_5.6_spmd.clone, body=%wide.region_4.5_spmd.clone.sunk | while | flops 805961728 | bytes 4194421 | solution.py:222
  140.2 6.2 %multiply_reduce_fusion = (f32[8192]{0:T(1024)}, bf16[8192,256]{1,0:T(8,128)(2,1)}) fusion(bf16[8192,256]{1,0:T(8,128)(2,1)} %copy-done, f32[256,256]{1,0:T(8,128)S(1)} %fusion.22), kind=kOutput, calls=%fused_computation.29 | convolution fusion | flops 1082187776 | bytes 8683520 | tf_op jit(solution)/shard_map/dot_general | solution.py:237
  (97 shorter events, 20.7 us)
Async XLA Ops:
  0.6 8.4 %copy-start.1 = (bf16[8,8,128,256]{3,2,1,0:T(8,128)(2,1)S(1)}, bf16[8,8,128,256]{3,2,1,0:T(8,128)(2,1)}, u32[]{:S(2)}) copy-start(bf16[8,8,128,256]{3,2,1,0:T(8,128)(2,1)} %block_ref.1) | copy-start | bytes 12582916
  3.0 9.0 %copy-start.6 = (bf16[32]{0:T(256)(128)(2,1)S(1)}, bf16[32]{0:T(256)(128)(2,1)}, u32[]{:S(2)}) copy-start(bf16[32]{0:T(256)(128)(2,1)} %param.13) | copy-start | bytes 196
  3.0 38.0 %collective-permute-start.2 = (bf16[8,3,128,256]{3,2,1,0:T(8,128)(2,1)S(1)}, bf16[8,3,128,256]{3,2,1,0:T(8,128)(2,1)S(1)}, u32[]{:S(2)}, u32[]{:S(2)}) collective-permute-start(bf16[8,3,128,256]{3,2,1,0:T(8,128)(2,1)S(1)} %get-tuple-element.117), channel_id=1, source_target_pairs={{0,1},{1,2},{2,3},{3,4},{4,5},{5,6},{6,7},{7,8},{8,9},{9,10},{10,1... | collective-permute-start | bytes 4718600 | tf_op jit(solution)/shard_map/ppermute | solution.py:19
  6.5 39.3 %collective-permute-start.5 = (bf16[8,3,128,256]{3,2,1,0:T(8,128)(2,1)S(1)}, bf16[8,3,128,256]{3,2,1,0:T(8,128)(2,1)S(1)}, u32[]{:S(2)}, u32[]{:S(2)}) collective-permute-start(bf16[8,3,128,256]{3,2,1,0:T(8,128)(2,1)S(1)} %get-tuple-element.116), channel_id=1, source_target_pairs={{1,0},{2,1},{3,2},{4,3},{5,4},{6,5},{7,6},{8,7},{9,8},{10,9},{11,1... | collective-permute-start | bytes 4718600 | tf_op jit(solution)/shard_map/ppermute | solution.py:19
  9.4 42.8 %collective-permute-start = (bf16[3,8,128,256]{3,2,1,0:T(8,128)(2,1)S(1)}, bf16[3,8,128,256]{3,2,1,0:T(8,128)(2,1)S(1)}, u32[]{:S(2)}, u32[]{:S(2)}) collective-permute-start(bf16[3,8,128,256]{3,2,1,0:T(8,128)(2,1)S(1)} %get-tuple-element.119), channel_id=1, source_target_pairs={{0,16},{16,32},{32,48},{48,64},{64,80},{80,96},{96,112},{112,128},... | collective-permute-start | bytes 4718600 | tf_op jit(solution)/shard_map/ppermute | solution.py:19
  10.8 44.8 %collective-permute-start.1 = (bf16[3,8,128,256]{3,2,1,0:T(8,128)(2,1)S(1)}, bf16[3,8,128,256]{3,2,1,0:T(8,128)(2,1)}, u32[]{:S(2)}, u32[]{:S(2)}) collective-permute-start(bf16[3,8,128,256]{3,2,1,0:T(8,128)(2,1)S(1)} %get-tuple-element.118), channel_id=1, source_target_pairs={{16,0},{32,16},{48,32},{64,48},{80,64},{96,80},{112,96},{128,112},... | collective-permute-start | bytes 4718600 | tf_op jit(solution)/shard_map/ppermute | solution.py:19
  41.1 25.9 %copy-start.2 = (bf16[8,3,128,256]{3,2,1,0:T(8,128)(2,1)}, bf16[8,3,128,256]{3,2,1,0:T(8,128)(2,1)S(1)}, u32[]{:S(2)}) copy-start(bf16[8,3,128,256]{3,2,1,0:T(8,128)(2,1)S(1)} %collective-permute-done.2.refs_1_) | copy-start | bytes 4718596
  42.4 24.7 %collective-permute-start.3 = (bf16[3,3,128,256]{3,2,1,0:T(8,128)(2,1)}, bf16[3,3,128,256]{3,2,1,0:T(8,128)(2,1)}, u32[]{:S(2)}, u32[]{:S(2)}) collective-permute-start(bf16[3,3,128,256]{3,2,1,0:T(8,128)(2,1)} %get-tuple-element.123), channel_id=1, source_target_pairs={{0,16},{16,32},{32,48},{48,64},{64,80},{80,96},{96,112},{112,128},... | collective-permute-start | bytes 1769480 | tf_op jit(solution)/shard_map/ppermute | solution.py:19
  44.4 22.6 %collective-permute-start.4 = (bf16[3,3,128,256]{3,2,1,0:T(8,128)(2,1)}, bf16[3,3,128,256]{3,2,1,0:T(8,128)(2,1)}, u32[]{:S(2)}, u32[]{:S(2)}) collective-permute-start(bf16[3,3,128,256]{3,2,1,0:T(8,128)(2,1)} %get-tuple-element.122), channel_id=1, source_target_pairs={{16,0},{32,16},{48,32},{64,48},{80,64},{96,80},{112,96},{128,112},... | collective-permute-start | bytes 1769480 | tf_op jit(solution)/shard_map/ppermute | solution.py:19
  45.7 21.3 %copy-start.3 = (bf16[8,3,128,256]{3,2,1,0:T(8,128)(2,1)}, bf16[8,3,128,256]{3,2,1,0:T(8,128)(2,1)S(1)}, u32[]{:S(2)}) copy-start(bf16[8,3,128,256]{3,2,1,0:T(8,128)(2,1)S(1)} %collective-permute-done.5.refs_4_) | copy-start | bytes 4718596
  47.0 20.1 %collective-permute-start.6 = (bf16[3,3,128,256]{3,2,1,0:T(8,128)(2,1)}, bf16[3,3,128,256]{3,2,1,0:T(8,128)(2,1)}, u32[]{:S(2)}, u32[]{:S(2)}) collective-permute-start(bf16[3,3,128,256]{3,2,1,0:T(8,128)(2,1)} %get-tuple-element.121), channel_id=1, source_target_pairs={{0,16},{16,32},{32,48},{48,64},{64,80},{80,96},{96,112},{112,128},... | collective-permute-start | bytes 1769480 | tf_op jit(solution)/shard_map/ppermute | solution.py:19
  52.2 1.1 copy-start.4
  53.3 13.7 %collective-permute-start.7 = (bf16[3,3,128,256]{3,2,1,0:T(8,128)(2,1)}, bf16[3,3,128,256]{3,2,1,0:T(8,128)(2,1)}, u32[]{:S(2)}, u32[]{:S(2)}) collective-permute-start(bf16[3,3,128,256]{3,2,1,0:T(8,128)(2,1)} %get-tuple-element.120), channel_id=1, source_target_pairs={{16,0},{32,16},{48,32},{64,48},{80,64},{96,80},{112,96},{128,112},... | collective-permute-start | bytes 1769480 | tf_op jit(solution)/shard_map/ppermute | solution.py:19
  80.8 2.0 %copy-start = (bf16[8192,256]{1,0:T(8,128)(2,1)}, bf16[8192,256]{1,0:T(8,128)(2,1)S(1)}, u32[]{:S(2)}) copy-start(bf16[8192,256]{1,0:T(8,128)(2,1)S(1)} %convolution_convert_fusion.1) | copy-start | bytes 12582916
  84.1 2.7 %collective-permute-start.8 = (f32[272,128]{1,0:T(8,128)S(1)}, f32[272,128]{1,0:T(8,128)S(1)}, u32[]{:S(2)}, u32[]{:S(2)}) collective-permute-start(f32[272,128]{1,0:T(8,128)S(1)} %select_maximum_fusion), channel_id=1, source_target_pairs={{0,16},{16,0},{32,48},{48,32},{64,80},{80,64},{96,112},{112,96},{1... | collective-permute-start | bytes 417800 | tf_op jit(solution)/shard_map/ppermute | solution.py:165
  86.7 7.7 %collective-permute-start.10 = (f32[136,128]{1,0:T(8,128)S(1)}, f32[136,128]{1,0:T(8,128)S(1)}, u32[]{:S(2)}, u32[]{:S(2)}) collective-permute-start(f32[136,128]{1,0:T(8,128)S(1)} %dynamic-slice_add_fusion), channel_id=1, source_target_pairs={{0,64},{16,80},{32,96},{48,112},{64,0},{80,16},{96,32},{112,48},{1... | collective-permute-start | bytes 208904 | tf_op jit(solution)/shard_map/ppermute | solution.py:138
  90.2 8.2 %collective-permute-start.11 = (f32[136,128]{1,0:T(8,128)S(1)}, f32[136,128]{1,0:T(8,128)S(1)}, u32[]{:S(2)}, u32[]{:S(2)}) collective-permute-start(f32[136,128]{1,0:T(8,128)S(1)} %dynamic-slice_add_fusion), channel_id=1, source_target_pairs={{0,96},{16,112},{32,64},{48,80},{64,32},{80,48},{96,0},{112,16},{1... | collective-permute-start | bytes 208904 | tf_op jit(solution)/shard_map/ppermute | solution.py:138
  94.0 5.5 %collective-permute-start.9 = (f32[136,128]{1,0:T(8,128)S(1)}, f32[136,128]{1,0:T(8,128)S(1)}, u32[]{:S(2)}, u32[]{:S(2)}) collective-permute-start(f32[136,128]{1,0:T(8,128)S(1)} %dynamic-slice_add_fusion), channel_id=1, source_target_pairs={{0,32},{16,48},{32,0},{48,16},{64,96},{80,112},{96,64},{112,80},{1... | collective-permute-start | bytes 208904 | tf_op jit(solution)/shard_map/ppermute | solution.py:138
  99.5 8.3 %collective-permute-start.12 = (f32[136,128]{1,0:T(8,128)S(1)}, f32[136,128]{1,0:T(8,128)S(1)}, u32[]{:S(2)}, u32[]{:S(2)}) collective-permute-start(f32[136,128]{1,0:T(8,128)S(1)} %add_add_fusion.2), channel_id=1, source_target_pairs={{0,128},{16,144},{32,160},{48,176},{64,192},{80,208},{96,224},{112... | collective-permute-start | bytes 208904 | tf_op jit(solution)/shard_map/ppermute | solution.py:138
  107.8 6.2 %collective-permute-start.14 = (f32[136,128]{1,0:T(8,128)S(1)}, f32[136,128]{1,0:T(8,128)S(1)}, u32[]{:S(2)}, u32[]{:S(2)}) collective-permute-start(f32[136,128]{1,0:T(8,128)S(1)} %add.80), channel_id=1, source_target_pairs={{0,2},{1,3},{2,0},{3,1},{4,6},{5,7},{6,4},{7,5},{8,10},{9,11},{10,... | collective-permute-start | bytes 208904 | tf_op jit(solution)/shard_map/ppermute | solution.py:138
  110.0 4.7 %collective-permute-start.15 = (f32[136,128]{1,0:T(8,128)S(1)}, f32[136,128]{1,0:T(8,128)S(1)}, u32[]{:S(2)}, u32[]{:S(2)}) collective-permute-start(f32[136,128]{1,0:T(8,128)S(1)} %add.80), channel_id=1, source_target_pairs={{0,3},{1,2},{2,1},{3,0},{4,7},{5,6},{6,5},{7,4},{8,11},{9,10},{10,... | collective-permute-start | bytes 208904 | tf_op jit(solution)/shard_map/ppermute | solution.py:138
  110.0 4.9 %collective-permute-start.13 = (f32[136,128]{1,0:T(8,128)S(1)}, f32[136,128]{1,0:T(8,128)S(1)}, u32[]{:S(2)}, u32[]{:S(2)}) collective-permute-start(f32[136,128]{1,0:T(8,128)S(1)} %add.80), channel_id=1, source_target_pairs={{0,1},{1,0},{2,3},{3,2},{4,5},{5,4},{6,7},{7,6},{8,9},{9,8},{10,11... | collective-permute-start | bytes 208904 | tf_op jit(solution)/shard_map/ppermute | solution.py:138
  114.9 7.3 %collective-permute-start.17 = (f32[136,128]{1,0:T(8,128)S(1)}, f32[136,128]{1,0:T(8,128)S(1)}, u32[]{:S(2)}, u32[]{:S(2)}) collective-permute-start(f32[136,128]{1,0:T(8,128)S(1)} %add_add_fusion.1), channel_id=1, source_target_pairs={{0,8},{1,9},{2,10},{3,11},{4,12},{5,13},{6,14},{7,15},{8,0},{9,1},... | collective-permute-start | bytes 208904 | tf_op jit(solution)/shard_map/ppermute | solution.py:138
  119.8 5.5 %collective-permute-start.18 = (f32[136,128]{1,0:T(8,128)S(1)}, f32[136,128]{1,0:T(8,128)S(1)}, u32[]{:S(2)}, u32[]{:S(2)}) collective-permute-start(f32[136,128]{1,0:T(8,128)S(1)} %add_add_fusion.1), channel_id=1, source_target_pairs={{0,12},{1,13},{2,14},{3,15},{4,8},{5,9},{6,10},{7,11},{8,4},{9,5},... | collective-permute-start | bytes 208904 | tf_op jit(solution)/shard_map/ppermute | solution.py:138
  120.8 4.5 %collective-permute-start.16 = (f32[136,128]{1,0:T(8,128)S(1)}, f32[136,128]{1,0:T(8,128)S(1)}, u32[]{:S(2)}, u32[]{:S(2)}) collective-permute-start(f32[136,128]{1,0:T(8,128)S(1)} %add_add_fusion.1), channel_id=1, source_target_pairs={{0,4},{1,5},{2,6},{3,7},{4,0},{5,1},{6,2},{7,3},{8,12},{9,13},{10,... | collective-permute-start | bytes 208904 | tf_op jit(solution)/shard_map/ppermute | solution.py:138
  125.3 1.6 %collective-permute-start.19 = (f32[136,128]{1,0:T(8,128)S(1)}, f32[136,128]{1,0:T(8,128)S(1)}, u32[]{:S(2)}, u32[]{:S(2)}) collective-permute-start(f32[136,128]{1,0:T(8,128)S(1)} %add_add_fusion), channel_id=1, source_target_pairs={{0,16},{16,0},{32,48},{48,32},{64,80},{80,64},{96,112},{112,96},{1... | collective-permute-start | bytes 208904 | tf_op jit(solution)/shard_map/ppermute | solution.py:170
  140.2 6.2 %copy-start.5 = (f32[256,256]{1,0:T(8,128)}, f32[256,256]{1,0:T(8,128)S(1)}, u32[]{:S(2)}) copy-start(f32[256,256]{1,0:T(8,128)S(1)} %fusion.22) | copy-start | bytes 786436

commit v10 on v9

--- a/solution.py
+++ b/solution.py
@@ -96,7 +96,7 @@
             out_ref[l, e] = total.astype(out_ref.dtype)
 
 
-def tiled_call(kernel, pieces, out_dtype, lat_taps, elev_taps, tile=16):
+def tiled_call(kernel, pieces, out_dtype, lat_taps, elev_taps, tile=32):
     _, _, depth, columns = pieces[0].shape
     tile = tile if depth % tile == 0 else depth
     smem = pl.BlockSpec(memory_space=pltpu.SMEM)
@@ -120,7 +120,7 @@
 def smooth(pieces, lat_taps, elev_taps):
     left, center, right = pieces
     middle = tiled_call(center_smooth_kernel, center, jnp.float32, lat_taps, elev_taps)
-    return tiled_call(edge_smooth_kernel, (middle, *left, *right), jnp.bfloat16, lat_taps, elev_taps)
+    return tiled_call(edge_smooth_kernel, (middle, *left, *right), jnp.bfloat16, lat_taps, elev_taps, tile=64)
 
 
 def filtered_rows(pieces, lat_taps, elev_taps, matrix):
@@ -195,7 +195,7 @@
     )
 
 
-def band_filter(gram_sum, clutter_rank, noise_rank, steps=9, coarse_steps=5):
+def band_filter(gram_sum, clutter_rank, noise_rank, steps=8, coarse_steps=5):
     width = gram_sum.shape[0]
     identity = jnp.eye(width, dtype=jnp.float32)
     total_trace = jnp.sum(gram_sum * identity)

time: 149 us -> 144 us (0.966)
  Pallas kernels: 21.8 us -> 18.8 us
  matrix products: 21.3 us -> 19.8 us
    pallas_call x2, Pallas kernels: 21.8 us -> 18.8 us  [tiled_call(): pl.pallas_call(kernel, out_shape=jax.ShapeDtypeStruct(pieces[0].shape, ou...]
    dot_general x9 -> x8, matrix products: 5.5 us -> 4.74 us  [step(): product = jnp.einsum('bij,bjk->bik', shifted, inverse, precision=precision)]
    dot_general x9 -> x8, matrix products: 4.88 us -> 4.19 us  [step(): jnp.einsum('bij,bjk->bik', inverse, product, precision=precision)]
  transfers between devices with their start and end apart: 20 -> 20, of which waited for: 10 -> 10; matrix products, arithmetic and copies ran while one was open for 3% -> 3% of each run, Pallas kernels for 8% -> 7%
where the time goes in v10:
time: 144 us; the launch traced here: 142 us
  waiting for transfers between devices  44.8 us (31%)
  starting transfers between devices  43.7 us (30%)
  matrix products  19.8 us (14%)
  Pallas kernels  18.8 us (13%)
  local copies, waits for them, and re-layouts  9.11 us (6%)
  other arithmetic  2.81 us (2%)
  between operations  2.32 us (2%)
    ppermute x8, waiting for transfers between devices, shift(): return lax.ppermute(piece, axis, pairs)  29 us
    ppermute x10, starting transfers between devices, butterfly_sum(): lax.ppermute(block, axis, [(i, i ^ mask) for i in range(count)])  23.5 us
    pallas_call x2, Pallas kernels, tiled_call(): pl.pallas_call(kernel, out_shape=jax.ShapeDtypeStruct(pieces[0].shape, ou...  18.8 us
    ppermute x8, starting transfers between devices, shift(): return lax.ppermute(piece, axis, pairs)  18.5 us
    ppermute x10, waiting for transfers between devices, butterfly_sum(): lax.ppermute(block, axis, [(i, i ^ mask) for i in range(count)])  14.8 us
    dot_general x1, matrix products, body(): jnp.dot(row_block, weights.astype(jnp.bfloat16), preferred_element_type=j...  6.16 us
    dot_general x8, matrix products, step(): product = jnp.einsum('bij,bjk->bik', shifted, inverse, precision=precision)  4.74 us
    dot_general x8, matrix products, step(): jnp.einsum('bij,bjk->bik', inverse, product, precision=precision)  4.19 us
  transfers between devices with their start and end apart: 20, of which 10 were waited for; matrix products, arithmetic and copies ran while one was open for 3% of the time, Pallas kernels for 7%

profile of v10, /device:TPU:2, one launch (start us, length us, event | category | flops | bytes accessed | tf_op | source)
XLA Modules:
  0.0 141.7 jit_solution(1556760468114448796)
XLA Ops:
  0.6 2.4 %fusion.31 = (bf16[8,3,128,256]{3,2,1,0:T(8,128)(2,1)S(1)}, bf16[8,3,128,256]{3,2,1,0:T(8,128)(2,1)S(1)}) fusion(bf16[8,8,128,256]{3,2,1,0:T(8,128)(2,1)} %block_ref.1), kind=kLoop, calls=%fused_computation.70 | loop fusion | bytes 6291456 | tf_op jit(solution)/shard_map/slice | solution.py:24
  3.0 3.4 %collective-permute-start.2 = (bf16[8,3,128,256]{3,2,1,0:T(8,128)(2,1)S(1)}, bf16[8,3,128,256]{3,2,1,0:T(8,128)(2,1)S(1)}, u32[]{:S(2)}, u32[]{:S(2)}) collective-permute-start(bf16[8,3,128,256]{3,2,1,0:T(8,128)(2,1)S(1)} %get-tuple-element.117), channel_id=1, source_target_pairs={{0,1},{1,2},{2,3},{3,4},{4,5},{5,6},{6,7},{7,8},{8,9},{9,10},{10,1... | collective-permute-start | bytes 4718600 | tf_op jit(solution)/shard_map/ppermute | solution.py:19
  6.5 2.5 %collective-permute-start.5 = (bf16[8,3,128,256]{3,2,1,0:T(8,128)(2,1)S(1)}, bf16[8,3,128,256]{3,2,1,0:T(8,128)(2,1)S(1)}, u32[]{:S(2)}, u32[]{:S(2)}) collective-permute-start(bf16[8,3,128,256]{3,2,1,0:T(8,128)(2,1)S(1)} %get-tuple-element.116), channel_id=1, source_target_pairs={{1,0},{2,1},{3,2},{4,3},{5,4},{6,5},{7,6},{8,7},{9,8},{10,9},{11,1... | collective-permute-start | bytes 4718600 | tf_op jit(solution)/shard_map/ppermute | solution.py:19
  9.4 1.4 collective-permute-start
  10.8 1.3 collective-permute-start.1
  12.1 29.0 %collective-permute-done.2.refs_1_ = bf16[8,3,128,256]{3,2,1,0:T(8,128)(2,1)S(1)} collective-permute-done((bf16[8,3,128,256]{3,2,1,0:T(8,128)(2,1)S(1)}, bf16[8,3,128,256]{3,2,1,0:T(8,128)(2,1)S(1)}, u32[]{:S(2)}, u32[]{:S(2)}) %collective-permute-start.2) | collective-permute-done | bytes 1572896 | tf_op jit(solution)/shard_map/ppermute | solution.py:19
  41.1 1.3 fusion.34
  42.4 2.1 %collective-permute-start.3 = (bf16[3,3,128,256]{3,2,1,0:T(8,128)(2,1)}, bf16[3,3,128,256]{3,2,1,0:T(8,128)(2,1)}, u32[]{:S(2)}, u32[]{:S(2)}) collective-permute-start(bf16[3,3,128,256]{3,2,1,0:T(8,128)(2,1)} %get-tuple-element.123), channel_id=1, source_target_pairs={{0,16},{16,32},{32,48},{48,64},{64,80},{80,96},{96,112},{112,128},... | collective-permute-start | bytes 1769480 | tf_op jit(solution)/shard_map/ppermute | solution.py:19
  44.4 1.3 collective-permute-start.4
  45.8 1.2 fusion.33
  47.0 5.2 %collective-permute-start.6 = (bf16[3,3,128,256]{3,2,1,0:T(8,128)(2,1)}, bf16[3,3,128,256]{3,2,1,0:T(8,128)(2,1)}, u32[]{:S(2)}, u32[]{:S(2)}) collective-permute-start(bf16[3,3,128,256]{3,2,1,0:T(8,128)(2,1)} %get-tuple-element.121), channel_id=1, source_target_pairs={{0,16},{16,32},{32,48},{48,64},{64,80},{80,96},{96,112},{112,128},... | collective-permute-start | bytes 1769480 | tf_op jit(solution)/shard_map/ppermute | solution.py:19
  53.3 1.3 collective-permute-start.7
  55.5 10.3 %shard_map.85.middle_ref = f32[8,8,128,256]{3,2,1,0:T(8,128)} custom-call(f32[7]{0:T(128)} %lat_ref.3, f32[7]{0:T(128)} %elev_ref.3, bf16[8,8,128,256]{3,2,1,0:T(8,128)(2,1)} %block_ref.1, bf16[3,8,128,256]{3,2,1,0:T(8,128)(2,1)} %copy-done.4, bf16[3,8,128,256]{3,2,1,0:T(8,128)(2,1)} %collective-permute-done.1.south_ref), custom_call_target="tpu_custom_call" | custom-call | tf_op jit(solution)/shard_map/pallas_call | solution.py:107
  65.9 8.4 %shard_map.86 = bf16[8,8,128,256]{3,2,1,0:T(8,128)(2,1)} custom-call(f32[7]{0:T(128)} %lat_ref.3, f32[7]{0:T(128)} %elev_ref.3, f32[8,8,128,256]{3,2,1,0:T(8,128)} %shard_map.85.middle_ref, bf16[3,3,128,256]{3,2,1,0:T(8,128)(2,1)} %collective-permute-done.3.refs_0_, bf16[8,3,128,256]{3,2,1,0:T(8,128)(2,1)} %copy-done.2, ...), custom_call_target="tpu_custom_call" | custom-call | tf_op jit(solution)/shard_map/pallas_call | solution.py:107
  74.4 3.4 %convolution_convert_fusion.1 = bf16[8192,256]{1,0:T(8,128)(2,1)S(1)} fusion(bf16[8192,256]{1,0:T(8,128)(2,1)} %bitcast.64, bf16[32,8,2,128]{3,2,1,0:T(2,128)(2,1)S(1)} %bitcast.65), kind=kOutput, calls=%fused_computation.28 | convolution fusion | flops 1075838976 | bytes 8519680 | tf_op jit(solution)/shard_map/dot_general | solution.py:129
  77.8 1.3 fusion.37
  79.8 1.2 gather_fusion
  81.0 1.7 %collective-permute-start.8 = (f32[272,128]{1,0:T(8,128)S(1)}, f32[272,128]{1,0:T(8,128)S(1)}, u32[]{:S(2)}, u32[]{:S(2)}) collective-permute-start(f32[272,128]{1,0:T(8,128)S(1)} %select_maximum_fusion), channel_id=1, source_target_pairs={{0,16},{16,0},{32,48},{48,32},{64,80},{80,64},{96,112},{112,96},{1... | collective-permute-start | bytes 417800 | tf_op jit(solution)/shard_map/ppermute | solution.py:165
  83.7 3.4 %collective-permute-start.10 = (f32[136,128]{1,0:T(8,128)S(1)}, f32[136,128]{1,0:T(8,128)S(1)}, u32[]{:S(2)}, u32[]{:S(2)}) collective-permute-start(f32[136,128]{1,0:T(8,128)S(1)} %dynamic-slice_add_fusion), channel_id=1, source_target_pairs={{0,64},{16,80},{32,96},{48,112},{64,0},{80,16},{96,32},{112,48},{1... | collective-permute-start | bytes 208904 | tf_op jit(solution)/shard_map/ppermute | solution.py:138
  87.1 3.8 %collective-permute-start.11 = (f32[136,128]{1,0:T(8,128)S(1)}, f32[136,128]{1,0:T(8,128)S(1)}, u32[]{:S(2)}, u32[]{:S(2)}) collective-permute-start(f32[136,128]{1,0:T(8,128)S(1)} %dynamic-slice_add_fusion), channel_id=1, source_target_pairs={{0,96},{16,112},{32,64},{48,80},{64,32},{80,48},{96,0},{112,16},{1... | collective-permute-start | bytes 208904 | tf_op jit(solution)/shard_map/ppermute | solution.py:138
  91.4 4.0 %collective-permute-done.11 = f32[136,128]{1,0:T(8,128)S(1)} collective-permute-done((f32[136,128]{1,0:T(8,128)S(1)}, f32[136,128]{1,0:T(8,128)S(1)}, u32[]{:S(2)}, u32[]{:S(2)}) %collective-permute-start.11) | collective-permute-done | bytes 69664 | tf_op jit(solution)/shard_map/ppermute | solution.py:138
  96.4 5.3 %collective-permute-start.12 = (f32[136,128]{1,0:T(8,128)S(1)}, f32[136,128]{1,0:T(8,128)S(1)}, u32[]{:S(2)}, u32[]{:S(2)}) collective-permute-start(f32[136,128]{1,0:T(8,128)S(1)} %add_add_fusion.2), channel_id=1, source_target_pairs={{0,128},{16,144},{32,160},{48,176},{64,192},{80,208},{96,224},{112... | collective-permute-start | bytes 208904 | tf_op jit(solution)/shard_map/ppermute | solution.py:138
  101.7 3.0 %collective-permute-done.12 = f32[136,128]{1,0:T(8,128)S(1)} collective-permute-done((f32[136,128]{1,0:T(8,128)S(1)}, f32[136,128]{1,0:T(8,128)S(1)}, u32[]{:S(2)}, u32[]{:S(2)}) %collective-permute-start.12) | collective-permute-done | bytes 69664 | tf_op jit(solution)/shard_map/ppermute | solution.py:138
  104.7 2.2 %collective-permute-start.14 = (f32[136,128]{1,0:T(8,128)S(1)}, f32[136,128]{1,0:T(8,128)S(1)}, u32[]{:S(2)}, u32[]{:S(2)}) collective-permute-start(f32[136,128]{1,0:T(8,128)S(1)} %add.80), channel_id=1, source_target_pairs={{0,2},{1,3},{2,0},{3,1},{4,6},{5,7},{6,4},{7,5},{8,10},{9,11},{10,... | collective-permute-start | bytes 208904 | tf_op jit(solution)/shard_map/ppermute | solution.py:138
  107.0 2.6 %collective-permute-start.13 = (f32[136,128]{1,0:T(8,128)S(1)}, f32[136,128]{1,0:T(8,128)S(1)}, u32[]{:S(2)}, u32[]{:S(2)}) collective-permute-start(f32[136,128]{1,0:T(8,128)S(1)} %add.80), channel_id=1, source_target_pairs={{0,1},{1,0},{2,3},{3,2},{4,5},{5,4},{6,7},{7,6},{8,9},{9,8},{10,11... | collective-permute-start | bytes 208904 | tf_op jit(solution)/shard_map/ppermute | solution.py:138
  109.5 1.5 %collective-permute-done.14 = f32[136,128]{1,0:T(8,128)S(1)} collective-permute-done((f32[136,128]{1,0:T(8,128)S(1)}, f32[136,128]{1,0:T(8,128)S(1)}, u32[]{:S(2)}, u32[]{:S(2)}) %collective-permute-start.14) | collective-permute-done | bytes 69664 | tf_op jit(solution)/shard_map/ppermute | solution.py:138
  111.8 4.7 %collective-permute-start.17 = (f32[136,128]{1,0:T(8,128)S(1)}, f32[136,128]{1,0:T(8,128)S(1)}, u32[]{:S(2)}, u32[]{:S(2)}) collective-permute-start(f32[136,128]{1,0:T(8,128)S(1)} %add_add_fusion.1), channel_id=1, source_target_pairs={{0,8},{1,9},{2,10},{3,11},{4,12},{5,13},{6,14},{7,15},{8,0},{9,1},... | collective-permute-start | bytes 208904 | tf_op jit(solution)/shard_map/ppermute | solution.py:138
  117.6 1.3 collective-permute-done.17
  118.9 3.1 %collective-permute-done.18 = f32[136,128]{1,0:T(8,128)S(1)} collective-permute-done((f32[136,128]{1,0:T(8,128)S(1)}, f32[136,128]{1,0:T(8,128)S(1)}, u32[]{:S(2)}, u32[]{:S(2)}) %collective-permute-start.18) | collective-permute-done | bytes 69664 | tf_op jit(solution)/shard_map/ppermute | solution.py:138
  125.4 5.0 %while.26 = (s32[]{:T(128)}, f32[2,256,256]{1,2,0:T(8,128)S(1)}, f32[2]{0:T(128)S(1)}, f32[256,256]{1,0:T(8,128)S(1)}, f32[2]{0:T(128)S(1)}, /*index=5*/f32[256,256]{1,0:T(8,128)S(1)}, s32[]{:T(128)}) while((s32[]{:T(128)}, f32[2,256,256]{1,2,0:T(8,128)S(1)}, f32[2]{0:T(128)S(1)}, f32[256,256]{1,0:T(8,128)S(1)}, f32[2]{0:T(128)S(1)}, ...), condition=%wide.region_3.4_spmd.clone, body=%wide.region_2.3_spmd.clone.sunk | while | flops 403308544 | bytes 4194421 | solution.py:221
  130.5 4.6 %while.27 = (s32[]{:T(128)}, f32[2,256,256]{1,2,0:T(8,128)S(1)}, f32[2]{0:T(128)S(1)}, f32[256,256]{1,0:T(8,128)S(1)}, f32[2]{0:T(128)S(1)}, /*index=5*/f32[256,256]{1,0:T(8,128)S(1)}, s32[]{:T(128)}) while((s32[]{:T(128)}, f32[2,256,256]{1,2,0:T(8,128)S(1)}, f32[2]{0:T(128)S(1)}, f32[256,256]{1,0:T(8,128)S(1)}, f32[2]{0:T(128)S(1)}, ...), condition=%wide.region_5.6_spmd.clone, body=%wide.region_4.5_spmd.clone.sunk | while | flops 805961728 | bytes 4194421 | solution.py:222
  135.5 6.2 %multiply_reduce_fusion = (f32[8192]{0:T(1024)}, bf16[8192,256]{1,0:T(8,128)(2,1)}) fusion(bf16[8192,256]{1,0:T(8,128)(2,1)} %copy-done, f32[256,256]{1,0:T(8,128)S(1)} %fusion.22), kind=kOutput, calls=%fused_computation.29 | convolution fusion | flops 1082187776 | bytes 8683520 | tf_op jit(solution)/shard_map/dot_general | solution.py:237
  (93 shorter events, 19.2 us)
Async XLA Ops:
  0.6 8.4 %copy-start.1 = (bf16[8,8,128,256]{3,2,1,0:T(8,128)(2,1)S(1)}, bf16[8,8,128,256]{3,2,1,0:T(8,128)(2,1)}, u32[]{:S(2)}) copy-start(bf16[8,8,128,256]{3,2,1,0:T(8,128)(2,1)} %block_ref.1) | copy-start | bytes 12582916
  3.0 9.0 %copy-start.6 = (bf16[32]{0:T(256)(128)(2,1)S(1)}, bf16[32]{0:T(256)(128)(2,1)}, u32[]{:S(2)}) copy-start(bf16[32]{0:T(256)(128)(2,1)} %param.13) | copy-start | bytes 196
  3.0 38.0 %collective-permute-start.2 = (bf16[8,3,128,256]{3,2,1,0:T(8,128)(2,1)S(1)}, bf16[8,3,128,256]{3,2,1,0:T(8,128)(2,1)S(1)}, u32[]{:S(2)}, u32[]{:S(2)}) collective-permute-start(bf16[8,3,128,256]{3,2,1,0:T(8,128)(2,1)S(1)} %get-tuple-element.117), channel_id=1, source_target_pairs={{0,1},{1,2},{2,3},{3,4},{4,5},{5,6},{6,7},{7,8},{8,9},{9,10},{10,1... | collective-permute-start | bytes 4718600 | tf_op jit(solution)/shard_map/ppermute | solution.py:19
  6.5 39.3 %collective-permute-start.5 = (bf16[8,3,128,256]{3,2,1,0:T(8,128)(2,1)S(1)}, bf16[8,3,128,256]{3,2,1,0:T(8,128)(2,1)S(1)}, u32[]{:S(2)}, u32[]{:S(2)}) collective-permute-start(bf16[8,3,128,256]{3,2,1,0:T(8,128)(2,1)S(1)} %get-tuple-element.116), channel_id=1, source_target_pairs={{1,0},{2,1},{3,2},{4,3},{5,4},{6,5},{7,6},{8,7},{9,8},{10,9},{11,1... | collective-permute-start | bytes 4718600 | tf_op jit(solution)/shard_map/ppermute | solution.py:19
  9.4 42.8 %collective-permute-start = (bf16[3,8,128,256]{3,2,1,0:T(8,128)(2,1)S(1)}, bf16[3,8,128,256]{3,2,1,0:T(8,128)(2,1)S(1)}, u32[]{:S(2)}, u32[]{:S(2)}) collective-permute-start(bf16[3,8,128,256]{3,2,1,0:T(8,128)(2,1)S(1)} %get-tuple-element.119), channel_id=1, source_target_pairs={{0,16},{16,32},{32,48},{48,64},{64,80},{80,96},{96,112},{112,128},... | collective-permute-start | bytes 4718600 | tf_op jit(solution)/shard_map/ppermute | solution.py:19
  10.8 44.8 %collective-permute-start.1 = (bf16[3,8,128,256]{3,2,1,0:T(8,128)(2,1)S(1)}, bf16[3,8,128,256]{3,2,1,0:T(8,128)(2,1)}, u32[]{:S(2)}, u32[]{:S(2)}) collective-permute-start(bf16[3,8,128,256]{3,2,1,0:T(8,128)(2,1)S(1)} %get-tuple-element.118), channel_id=1, source_target_pairs={{16,0},{32,16},{48,32},{64,48},{80,64},{96,80},{112,96},{128,112},... | collective-permute-start | bytes 4718600 | tf_op jit(solution)/shard_map/ppermute | solution.py:19
  41.1 24.8 %copy-start.2 = (bf16[8,3,128,256]{3,2,1,0:T(8,128)(2,1)}, bf16[8,3,128,256]{3,2,1,0:T(8,128)(2,1)S(1)}, u32[]{:S(2)}) copy-start(bf16[8,3,128,256]{3,2,1,0:T(8,128)(2,1)S(1)} %collective-permute-done.2.refs_1_) | copy-start | bytes 4718596
  42.4 23.5 %collective-permute-start.3 = (bf16[3,3,128,256]{3,2,1,0:T(8,128)(2,1)}, bf16[3,3,128,256]{3,2,1,0:T(8,128)(2,1)}, u32[]{:S(2)}, u32[]{:S(2)}) collective-permute-start(bf16[3,3,128,256]{3,2,1,0:T(8,128)(2,1)} %get-tuple-element.123), channel_id=1, source_target_pairs={{0,16},{16,32},{32,48},{48,64},{64,80},{80,96},{96,112},{112,128},... | collective-permute-start | bytes 1769480 | tf_op jit(solution)/shard_map/ppermute | solution.py:19
  44.4 21.5 %collective-permute-start.4 = (bf16[3,3,128,256]{3,2,1,0:T(8,128)(2,1)}, bf16[3,3,128,256]{3,2,1,0:T(8,128)(2,1)}, u32[]{:S(2)}, u32[]{:S(2)}) collective-permute-start(bf16[3,3,128,256]{3,2,1,0:T(8,128)(2,1)} %get-tuple-element.122), channel_id=1, source_target_pairs={{16,0},{32,16},{48,32},{64,48},{80,64},{96,80},{112,96},{128,112},... | collective-permute-start | bytes 1769480 | tf_op jit(solution)/shard_map/ppermute | solution.py:19
  45.7 20.1 %copy-start.3 = (bf16[8,3,128,256]{3,2,1,0:T(8,128)(2,1)}, bf16[8,3,128,256]{3,2,1,0:T(8,128)(2,1)S(1)}, u32[]{:S(2)}) copy-start(bf16[8,3,128,256]{3,2,1,0:T(8,128)(2,1)S(1)} %collective-permute-done.5.refs_4_) | copy-start | bytes 4718596
  47.0 18.9 %collective-permute-start.6 = (bf16[3,3,128,256]{3,2,1,0:T(8,128)(2,1)}, bf16[3,3,128,256]{3,2,1,0:T(8,128)(2,1)}, u32[]{:S(2)}, u32[]{:S(2)}) collective-permute-start(bf16[3,3,128,256]{3,2,1,0:T(8,128)(2,1)} %get-tuple-element.121), channel_id=1, source_target_pairs={{0,16},{16,32},{32,48},{48,64},{64,80},{80,96},{96,112},{112,128},... | collective-permute-start | bytes 1769480 | tf_op jit(solution)/shard_map/ppermute | solution.py:19
  52.2 1.1 copy-start.4
  53.3 12.6 %collective-permute-start.7 = (bf16[3,3,128,256]{3,2,1,0:T(8,128)(2,1)}, bf16[3,3,128,256]{3,2,1,0:T(8,128)(2,1)}, u32[]{:S(2)}, u32[]{:S(2)}) collective-permute-start(bf16[3,3,128,256]{3,2,1,0:T(8,128)(2,1)} %get-tuple-element.120), channel_id=1, source_target_pairs={{16,0},{32,16},{48,32},{64,48},{80,64},{96,80},{112,96},{128,112},... | collective-permute-start | bytes 1769480 | tf_op jit(solution)/shard_map/ppermute | solution.py:19
  77.8 2.0 %copy-start = (bf16[8192,256]{1,0:T(8,128)(2,1)}, bf16[8192,256]{1,0:T(8,128)(2,1)S(1)}, u32[]{:S(2)}) copy-start(bf16[8192,256]{1,0:T(8,128)(2,1)S(1)} %convolution_convert_fusion.1) | copy-start | bytes 12582916
  81.0 2.6 %collective-permute-start.8 = (f32[272,128]{1,0:T(8,128)S(1)}, f32[272,128]{1,0:T(8,128)S(1)}, u32[]{:S(2)}, u32[]{:S(2)}) collective-permute-start(f32[272,128]{1,0:T(8,128)S(1)} %select_maximum_fusion), channel_id=1, source_target_pairs={{0,16},{16,0},{32,48},{48,32},{64,80},{80,64},{96,112},{112,96},{1... | collective-permute-start | bytes 417800 | tf_op jit(solution)/shard_map/ppermute | solution.py:165
  83.7 7.7 %collective-permute-start.10 = (f32[136,128]{1,0:T(8,128)S(1)}, f32[136,128]{1,0:T(8,128)S(1)}, u32[]{:S(2)}, u32[]{:S(2)}) collective-permute-start(f32[136,128]{1,0:T(8,128)S(1)} %dynamic-slice_add_fusion), channel_id=1, source_target_pairs={{0,64},{16,80},{32,96},{48,112},{64,0},{80,16},{96,32},{112,48},{1... | collective-permute-start | bytes 208904 | tf_op jit(solution)/shard_map/ppermute | solution.py:138
  87.1 8.2 %collective-permute-start.11 = (f32[136,128]{1,0:T(8,128)S(1)}, f32[136,128]{1,0:T(8,128)S(1)}, u32[]{:S(2)}, u32[]{:S(2)}) collective-permute-start(f32[136,128]{1,0:T(8,128)S(1)} %dynamic-slice_add_fusion), channel_id=1, source_target_pairs={{0,96},{16,112},{32,64},{48,80},{64,32},{80,48},{96,0},{112,16},{1... | collective-permute-start | bytes 208904 | tf_op jit(solution)/shard_map/ppermute | solution.py:138
  90.9 5.5 %collective-permute-start.9 = (f32[136,128]{1,0:T(8,128)S(1)}, f32[136,128]{1,0:T(8,128)S(1)}, u32[]{:S(2)}, u32[]{:S(2)}) collective-permute-start(f32[136,128]{1,0:T(8,128)S(1)} %dynamic-slice_add_fusion), channel_id=1, source_target_pairs={{0,32},{16,48},{32,0},{48,16},{64,96},{80,112},{96,64},{112,80},{1... | collective-permute-start | bytes 208904 | tf_op jit(solution)/shard_map/ppermute | solution.py:138
  96.4 8.3 %collective-permute-start.12 = (f32[136,128]{1,0:T(8,128)S(1)}, f32[136,128]{1,0:T(8,128)S(1)}, u32[]{:S(2)}, u32[]{:S(2)}) collective-permute-start(f32[136,128]{1,0:T(8,128)S(1)} %add_add_fusion.2), channel_id=1, source_target_pairs={{0,128},{16,144},{32,160},{48,176},{64,192},{80,208},{96,224},{112... | collective-permute-start | bytes 208904 | tf_op jit(solution)/shard_map/ppermute | solution.py:138
  104.7 6.2 %collective-permute-start.14 = (f32[136,128]{1,0:T(8,128)S(1)}, f32[136,128]{1,0:T(8,128)S(1)}, u32[]{:S(2)}, u32[]{:S(2)}) collective-permute-start(f32[136,128]{1,0:T(8,128)S(1)} %add.80), channel_id=1, source_target_pairs={{0,2},{1,3},{2,0},{3,1},{4,6},{5,7},{6,4},{7,5},{8,10},{9,11},{10,... | collective-permute-start | bytes 208904 | tf_op jit(solution)/shard_map/ppermute | solution.py:138
  107.0 4.7 %collective-permute-start.15 = (f32[136,128]{1,0:T(8,128)S(1)}, f32[136,128]{1,0:T(8,128)S(1)}, u32[]{:S(2)}, u32[]{:S(2)}) collective-permute-start(f32[136,128]{1,0:T(8,128)S(1)} %add.80), channel_id=1, source_target_pairs={{0,3},{1,2},{2,1},{3,0},{4,7},{5,6},{6,5},{7,4},{8,11},{9,10},{10,... | collective-permute-start | bytes 208904 | tf_op jit(solution)/shard_map/ppermute | solution.py:138
  107.0 4.9 %collective-permute-start.13 = (f32[136,128]{1,0:T(8,128)S(1)}, f32[136,128]{1,0:T(8,128)S(1)}, u32[]{:S(2)}, u32[]{:S(2)}) collective-permute-start(f32[136,128]{1,0:T(8,128)S(1)} %add.80), channel_id=1, source_target_pairs={{0,1},{1,0},{2,3},{3,2},{4,5},{5,4},{6,7},{7,6},{8,9},{9,8},{10,11... | collective-permute-start | bytes 208904 | tf_op jit(solution)/shard_map/ppermute | solution.py:138
  111.8 7.1 %collective-permute-start.17 = (f32[136,128]{1,0:T(8,128)S(1)}, f32[136,128]{1,0:T(8,128)S(1)}, u32[]{:S(2)}, u32[]{:S(2)}) collective-permute-start(f32[136,128]{1,0:T(8,128)S(1)} %add_add_fusion.1), channel_id=1, source_target_pairs={{0,8},{1,9},{2,10},{3,11},{4,12},{5,13},{6,14},{7,15},{8,0},{9,1},... | collective-permute-start | bytes 208904 | tf_op jit(solution)/shard_map/ppermute | solution.py:138
  116.6 5.5 %collective-permute-start.18 = (f32[136,128]{1,0:T(8,128)S(1)}, f32[136,128]{1,0:T(8,128)S(1)}, u32[]{:S(2)}, u32[]{:S(2)}) collective-permute-start(f32[136,128]{1,0:T(8,128)S(1)} %add_add_fusion.1), channel_id=1, source_target_pairs={{0,12},{1,13},{2,14},{3,15},{4,8},{5,9},{6,10},{7,11},{8,4},{9,5},... | collective-permute-start | bytes 208904 | tf_op jit(solution)/shard_map/ppermute | solution.py:138
  117.6 4.5 %collective-permute-start.16 = (f32[136,128]{1,0:T(8,128)S(1)}, f32[136,128]{1,0:T(8,128)S(1)}, u32[]{:S(2)}, u32[]{:S(2)}) collective-permute-start(f32[136,128]{1,0:T(8,128)S(1)} %add_add_fusion.1), channel_id=1, source_target_pairs={{0,4},{1,5},{2,6},{3,7},{4,0},{5,1},{6,2},{7,3},{8,12},{9,13},{10,... | collective-permute-start | bytes 208904 | tf_op jit(solution)/shard_map/ppermute | solution.py:138
  122.1 1.6 %collective-permute-start.19 = (f32[136,128]{1,0:T(8,128)S(1)}, f32[136,128]{1,0:T(8,128)S(1)}, u32[]{:S(2)}, u32[]{:S(2)}) collective-permute-start(f32[136,128]{1,0:T(8,128)S(1)} %add_add_fusion), channel_id=1, source_target_pairs={{0,16},{16,0},{32,48},{48,32},{64,80},{80,64},{96,112},{112,96},{1... | collective-permute-start | bytes 208904 | tf_op jit(solution)/shard_map/ppermute | solution.py:170
  135.5 6.2 %copy-start.5 = (f32[256,256]{1,0:T(8,128)}, f32[256,256]{1,0:T(8,128)S(1)}, u32[]{:S(2)}) copy-start(f32[256,256]{1,0:T(8,128)S(1)} %fusion.22) | copy-start | bytes 786436
